TPU v7x, 32 devices: a whole 2x2x4 slice. The times are simulated.
32 devices in a mesh: dp: 4 (over z), seq: 8 (over y, x, core).
Axes of the slice: x: 2, y: 2, z: 4, core: 2. Of those that a mesh axis runs over, the one named last changes fastest.
Arguments:
- queries: bfloat16 [8, 2048, 2048], P('dp', 'seq'), may hold values from -6 to 6
- d_context: bfloat16 [8, 2048, 2048], P('dp', 'seq'), may hold values from -12 to 12
- database: bfloat16 [1024, 128, 896], P(('dp', 'seq')), may hold values from -6 to 6
- key_weight: bfloat16 [896, 2048], replicated, may hold values from -0.1875 to 0.1875
- value_weight: bfloat16 [896, 2048], replicated, may hold values from -0.1875 to 0.1875
- neighbour_shard: int32 [4, 8, 8, 2], P('dp', 'seq'), may hold values from 0 to 3, all different within a row; in each aligned block of 8 rows (0 to 7, 8 to 15, ..., all dimensions but the last counted through in order) at most 8 rows name the same one
- neighbour_row: int32 [4, 8, 8, 2], P('dp', 'seq'), may hold values from 0 to 31
Outputs:
- context: bfloat16 [8, 2048, 2048], P('dp', 'seq')
- query_grad: bfloat16 [8, 2048, 2048], P('dp', 'seq')
- database_grad: float32 [1024, 128, 896], P(('dp', 'seq'))
- key_weight_grad: float32 [896, 2048], P(('dp', 'seq'))
- value_weight_grad: float32 [896, 2048], P(('dp', 'seq'))
Inputs may be any that keep to these rules, and one draw needn't show every extreme that they name: `neighbour_shard`: among the 8 rows of one device (aligned blocks of the first three dimensions taken together), no shard is named more than 8 times, a bound that some block reaches; the 2 neighbours of one block name different shards.
All inputs are finite; a program needn't handle non-finite values.
Results may differ from a plain program's by a relative error of at most 0.015.
Values may be sent and summed in bfloat16 or wider, within the bound.
No kernel may reach another device: no remote copies, remote signals or barrier semaphores. Data moves between devices by JAX's collectives and lax.ppermute only.
A program may use at most 192 MiB of HBM per device.

v0:
```python
import jax
import jax.numpy as jnp
from jax import lax
from jax.sharding import PartitionSpec as P

HD = 128
ENC = 896
SPAN = 64
NB_LEN = 128


def shifted(array, axis, by):
    count = lax.axis_size(axis)
    pairs = [(i, i + by) for i in range(count) if 0 <= i + by < count]
    return lax.ppermute(array, axis, pairs)


def local(queries, d_context, database, key_weight, value_weight, neighbour_shard, neighbour_row):
    seq_count, seq_span, feat_width = queries.shape
    head_count = feat_width // HD
    lag_rows = SPAN - 1
    block_count = seq_count * seq_span // SPAN
    pick_count = neighbour_shard.shape[-1]
    ref_count = block_count * pick_count
    shard_count = lax.axis_size("dp")
    capacity = 2 * ref_count // shard_count
    slot_count = shard_count * capacity
    near_len = pick_count * NB_LEN
    target = neighbour_shard.reshape(ref_count)
    wanted = neighbour_row.reshape(ref_count)
    owners = (target[:, None] == jnp.arange(shard_count, dtype=jnp.int32)[None, :]).astype(
        jnp.int32
    )
    before = jnp.cumsum(owners, axis=0) - owners
    slot_rank = jnp.sum(before * owners, axis=1)
    slot_index = target * capacity + slot_rank
    placed = (slot_index[:, None] == jnp.arange(slot_count, dtype=jnp.int32)[None, :]).astype(
        jnp.int32
    )
    request = jnp.sum(placed * wanted[:, None], axis=0)
    arrived = lax.all_to_all(request, "dp", split_axis=0, concat_axis=0, tiled=True)
    outgoing = jnp.take(database, arrived, axis=0)
    incoming = lax.all_to_all(outgoing, "dp", split_axis=0, concat_axis=0, tiled=True)
    neighbours = jnp.take(incoming, slot_index, axis=0).reshape(ref_count * NB_LEN, ENC)
    key_rows = jnp.dot(neighbours, key_weight, preferred_element_type=jnp.float32).astype(
        jnp.bfloat16
    )
    value_rows = jnp.dot(neighbours, value_weight, preferred_element_type=jnp.float32).astype(
        jnp.bfloat16
    )
    key_heads = key_rows.reshape(block_count, near_len, head_count, HD)
    value_heads = value_rows.reshape(block_count, near_len, head_count, HD)
    head_rows, head_grads = shifted((queries[:, :lag_rows], d_context[:, :lag_rows]), "seq", -1)
    query_blocks = jnp.concatenate([queries[:, lag_rows:], head_rows], axis=1).reshape(
        block_count, SPAN, head_count, HD
    )
    grad_blocks = jnp.concatenate([d_context[:, lag_rows:], head_grads], axis=1).reshape(
        block_count, SPAN, head_count, HD
    )
    score_scale = HD ** (-0.5)
    scores = (
        jnp.einsum("cqhd,ckhd->chqk", query_blocks, key_heads, preferred_element_type=jnp.float32)
        * score_scale
    )
    weights = jnp.exp(scores)
    weights = weights / jnp.sum(weights, axis=-1, keepdims=True)
    weight_half = weights.astype(jnp.bfloat16)
    context_shift = jnp.einsum(
        "chqk,ckhd->cqhd", weight_half, value_heads, preferred_element_type=jnp.float32
    )
    context_shift = context_shift.astype(jnp.bfloat16).reshape(seq_count, seq_span, feat_width)
    prob_grads = jnp.einsum(
        "cqhd,ckhd->chqk", grad_blocks, value_heads, preferred_element_type=jnp.float32
    )
    row_delta = jnp.sum(weights * prob_grads, axis=-1, keepdims=True)
    score_grads = (score_scale * weights * (prob_grads - row_delta)).astype(jnp.bfloat16)
    query_shift = jnp.einsum(
        "chqk,ckhd->cqhd", score_grads, key_heads, preferred_element_type=jnp.float32
    )
    query_shift = query_shift.astype(jnp.bfloat16).reshape(seq_count, seq_span, feat_width)
    key_grads = jnp.einsum(
        "chqk,cqhd->ckhd", score_grads, query_blocks, preferred_element_type=jnp.float32
    )
    key_grads = key_grads.astype(jnp.bfloat16).reshape(ref_count * NB_LEN, feat_width)
    value_grads = jnp.einsum(
        "chqk,cqhd->ckhd", weight_half, grad_blocks, preferred_element_type=jnp.float32
    )
    value_grads = value_grads.astype(jnp.bfloat16).reshape(ref_count * NB_LEN, feat_width)
    proj_grads = jnp.concatenate([key_grads, value_grads], axis=1)
    both_weights = jnp.concatenate([key_weight, value_weight], axis=1)
    near_grads = jnp.einsum(
        "pz,xz->px", proj_grads, both_weights, preferred_element_type=jnp.float32
    )
    near_grads = near_grads.reshape(ref_count, NB_LEN * ENC)
    slot_grads = jnp.einsum(
        "rs,rx->sx", placed.astype(jnp.float32), near_grads, precision=lax.Precision.HIGHEST
    )
    returned = lax.all_to_all(
        slot_grads.reshape(slot_count, NB_LEN, ENC).astype(jnp.bfloat16),
        "dp",
        split_axis=0,
        concat_axis=0,
        tiled=True,
    ).astype(jnp.float32)
    row_hits = (jnp.arange(database.shape[0], dtype=jnp.int32)[:, None] == arrived[None, :]).astype(
        jnp.float32
    )
    database_grad = jnp.einsum(
        "rs,sx->rx",
        row_hits,
        returned.reshape(slot_count, NB_LEN * ENC),
        precision=lax.Precision.HIGHEST,
    )
    database_grad = database_grad.reshape(database.shape)
    keep_rows = seq_span - lag_rows
    prior_context, prior_grads = shifted(
        (context_shift[:, keep_rows:], query_shift[:, keep_rows:]), "seq", 1
    )
    context = jnp.concatenate([prior_context, context_shift[:, :keep_rows]], axis=1)
    query_grad = jnp.concatenate([prior_grads, query_shift[:, :keep_rows]], axis=1)
    owned_grads = lax.psum_scatter(
        jnp.einsum("px,pz->xz", neighbours, proj_grads, preferred_element_type=jnp.float32),
        ("dp", "seq"),
        scatter_dimension=0,
        tiled=True,
    )
    return (
        context,
        query_grad,
        database_grad,
        owned_grads[:, :feat_width],
        owned_grads[:, feat_width:],
    )


def solution(mesh):
    return jax.shard_map(
        local,
        mesh=mesh,
        in_specs=(
            P("dp", "seq", None),
            P("dp", "seq", None),
            P(("dp", "seq"), None, None),
            P(),
            P(),
            P("dp", "seq", None, None),
            P("dp", "seq", None, None),
        ),
        out_specs=(
            P("dp", "seq", None),
            P("dp", "seq", None),
            P(("dp", "seq"), None, None),
            P(("dp", "seq"), None),
            P(("dp", "seq"), None),
        ),
        check_vma=False,
    )
```

profile of v0, /device:TPU:0, one launch (start us, length us, event | category | flops | bytes accessed | tf_op | source)
XLA Modules:
  0.0 846.5 jit_solution(10082519209467631817)
XLA Ops:
  9.8 11.7 %all_to_all.25 = s32[4,8,1]{1,2,0:T(1,128)S(1)} all-to-all(s32[4,8,1]{1,2,0:T(1,128)S(1)} %bitcast.104), channel_id=1, replica_groups=mesh['dp'=4,'seq'=8] {'dp'}, dimensions={0} | all-to-all | bytes 256 | tf_op jit(solution)/shard_map/all_to_all | solution.py:41
  23.4 7.5 gather_fusion
  31.0 6.9 broadcast_select_fusion
  55.8 147.1 %all-to-all-done.1 = bf16[32,128,896]{2,1,0:T(8,128)(2,1)} async-done(((bf16[32,128,896]{2,1,0:T(8,128)(2,1)}), bf16[32,128,896]{2,1,0:T(8,128)(2,1)}, u32[]{:S(2)}, u32[]{:S(2)}) %all-to-all-start.1) | async-done | bytes 7340064 | tf_op jit(solution)/shard_map/all_to_all | solution.py:43
  213.7 10.9 %convert_bitcast_fusion.2 = bf16[256,8,16,128]{3,1,2,0:T(8,128)(2,1)} fusion(bf16[2048,896]{1,0:T(8,128)(2,1)S(1)} %bitcast_select_fusion, bf16[896,2048]{1,0:T(8,128)(2,1)S(1)} %copy-done.11), kind=kOutput, calls=%fused_computation.9 | convolution fusion | flops 7520387072 | bytes 15728640 | tf_op jit(solution)/shard_map/dot_general | solution.py:45
  224.6 9.8 %copy.62 = bf16[256,8,16,128]{3,2,1,0:T(8,128)(2,1)} copy(bf16[256,8,16,128]{3,1,2,0:T(8,128)(2,1)} %convert_bitcast_fusion.2) | data formatting | bytes 16777216
  234.3 13.7 %convert_bitcast_fusion.3 = bf16[256,8,16,128]{3,1,2,0:T(8,128)(2,1)} fusion(bf16[2048,896]{1,0:T(8,128)(2,1)} %copy-done.2, bf16[896,2048]{1,0:T(8,128)(2,1)} %param.11), kind=kOutput, calls=%fused_computation.10 | convolution fusion | flops 7520387072 | bytes 15728640 | tf_op jit(solution)/shard_map/dot_general | solution.py:48
  248.0 9.8 %copy.63 = bf16[256,8,16,128]{3,2,1,0:T(8,128)(2,1)} copy(bf16[256,8,16,128]{3,1,2,0:T(8,128)(2,1)} %convert_bitcast_fusion.3) | data formatting | bytes 16777216
  257.8 6.9 fusion.1
  264.8 7.3 convert_bitcast_fusion
  272.1 9.4 %multiply_reduce_fusion = (f32[8,16,64]{2,1,0:T(8,128)S(1)}, f32[8,16,64,256]{3,2,1,0:T(8,128)}) fusion(f32[8,16,64]{2,1,0:T(8,128)S(1)} %get-tuple-element.24, f32[8,16,64,256]{3,2,1,0:T(8,128)S(1)} %get-tuple-element.25, bf16[8,256,16,128]{3,2,1,0:T(8,128)(2,1)} %bitcast.97, bf16[8,64,16,128]{3,2,1,0:T(8,128)(2,1)S(1)} %bitcast.102), kind=kOutput, calls=%fused_computation.7 | convolution fusion | flops 545251328 | bytes 27328512 | tf_op jit(solution)/shard_map/cqhd,ckhd->chqk/dot_general | solution.py:72
  281.5 12.7 %copy.54 = bf16[8,256,16,128]{3,2,1,0:T(8,128)(2,1)} copy(bf16[8,256,16,128]{1,3,2,0:T(8,128)(2,1)} %convert_bitcast_fusion) | data formatting | bytes 16777216 | tf_op jit(solution)/shard_map/convert_element_type | solution.py:88
  294.2 7.2 multiply_convert_fusion
  309.2 12.9 %copy.52 = bf16[8,256,16,128]{3,2,1,0:T(8,128)(2,1)} copy(bf16[8,256,16,128]{1,3,2,0:T(8,128)(2,1)} %convert_bitcast_fusion.1) | data formatting | bytes 16777216 | tf_op jit(solution)/shard_map/convert_element_type | solution.py:84
  322.0 11.1 %bitcast_dynamic-update-slice_fusion.1 = bf16[2048,4096]{1,0:T(8,128)(2,1)} fusion(bf16[256,8,16,128]{3,2,1,0:T(8,128)(2,1)} %bitcast.93), kind=kLoop, calls=%fused_computation.3 | loop fusion | bytes 16777216
  333.2 11.3 %bitcast_dynamic-update-slice_fusion = bf16[2048,4096]{1,0:T(8,128)(2,1)} fusion(bf16[2048,4096]{1,0:T(8,128)(2,1)} %bitcast_dynamic-update-slice_fusion.1, bf16[256,8,16,128]{3,2,1,0:T(8,128)(2,1)} %bitcast.92), kind=kLoop, calls=%fused_computation.2 | loop fusion | bytes 16777216 | tf_op jit(solution)/shard_map/concatenate | solution.py:89
  344.5 23.1 %fusion.16 = f32[2048,896]{1,0:T(8,128)} fusion(bf16[2048,4096]{1,0:T(8,128)(2,1)} %bitcast_dynamic-update-slice_fusion, bf16[896,2048]{1,0:T(8,128)(2,1)S(1)} %copy-done.10, bf16[896,2048]{1,0:T(8,128)(2,1)} %param.10), kind=kOutput, calls=%fused_computation.27 | convolution fusion | flops 15047065600 | bytes 31457280 | tf_op jit(solution)/shard_map/pz,xz->px/dot_general | solution.py:91
  373.2 14.1 %fusion.20 = bf16[32,128,896]{2,0,1:T(8,128)(2,1)S(1)} fusion(f32[2,128,8,896]{3,2,1,0:T(8,128)} %bitcast.94, s32[16]{0:T(128)S(1)} %copy-done.9), kind=kOutput, calls=%fused_computation.32 | convolution fusion | flops 708314624 | bytes 14680128 | tf_op jit(solution)/shard_map/rs,rx->sx/dot_general | solution.py:95
  398.2 21.4 %fusion.49 = f32[896,4096]{1,0:T(8,128)} fusion(bf16[2048,896]{1,0:T(8,128)(2,1)} %copy-done.2, bf16[2048,4096]{1,0:T(8,128)(2,1)} %bitcast_dynamic-update-slice_fusion), kind=kOutput, calls=%fused_computation.76 | convolution fusion | flops 15032385536 | bytes 35127296 | tf_op jit(solution)/shard_map/px,pz->xz/dot_general | solution.py:122
  419.7 8.0 convert_bitcast_fusion.5
  435.6 7.4 convert_bitcast_fusion.4
  461.3 340.1 %all-reduce.3.cloned.1.call-done = f32[896,4096]{1,0:T(8,128)} async-done(((f32[896,4096]{1,0:T(8,128)}), f32[896,4096]{1,0:T(8,128)}) %all-reduce.3.cloned.1.call-update) | async-done | bytes 14680080
  803.4 16.6 %fusion.10 = f32[32,128,896]{2,0,1:T(8,128)} fusion(s32[32]{0:T(128)S(1)} %copy-done.7, bf16[4,8,128,896]{3,2,1,0:T(8,128)(2,1)} %bitcast.44), kind=kOutput, calls=%fused_computation.21 | convolution fusion | flops 234882048 | bytes 22020224 | tf_op jit(solution)/shard_map/rs,sx->rx/dot_general | solution.py:108
  820.0 19.4 %copy.58 = f32[32,128,896]{2,1,0:T(8,128)} copy(f32[32,128,896]{2,0,1:T(8,128)} %fusion.10) | data formatting | bytes 29360128
  (85 shorter events, 85.7 us)
Async XLA Ops:
  9.1 0.5 copy-start.8
  22.8 0.6 copy-start.6
  37.9 8.0 copy-start.3
  37.9 9.3 %copy-start.5 = (s32[1,1,8,2]{2,3,1,0:T(2,128)S(1)}, s32[1,1,8,2]{2,3,1,0:T(2,128)}, u32[]{:S(2)}) copy-start(s32[1,1,8,2]{2,3,1,0:T(2,128)} %param.12) | copy-start | bytes 196
  37.9 165.0 %all-to-all-start.1 = ((bf16[32,128,896]{2,1,0:T(8,128)(2,1)}), bf16[32,128,896]{2,1,0:T(8,128)(2,1)}, u32[]{:S(2)}, u32[]{:S(2)}) async-start(bf16[32,128,896]{2,1,0:T(8,128)(2,1)} %broadcast_select_fusion), calls=%async_computation.1 | async-start | bytes 14680064 | tf_op jit(solution)/shard_map/all_to_all | solution.py:43
  44.5 8.0 collective-permute-start.2
  45.9 4.6 collective-permute-start
  208.8 4.9 copy-start.11
  211.9 1.8 copy-start.2
  264.7 7.4 copy-start.1
  264.7 7.3 copy-start.4
  301.4 1.9 copy-start
  333.2 11.3 %copy-start.10 = (bf16[896,2048]{1,0:T(8,128)(2,1)S(1)}, bf16[896,2048]{1,0:T(8,128)(2,1)}, u32[]{:S(2)}) copy-start(bf16[896,2048]{1,0:T(8,128)(2,1)} %param.11) | copy-start | bytes 11010052
  367.5 5.7 copy-start.9
  392.8 410.6 %all-to-all-start.2 = ((bf16[32,128,896]{2,1,0:T(8,128)(2,1)}), bf16[32,128,896]{2,1,0:T(8,128)(2,1)}, u32[]{:S(2)}, u32[]{:S(2)}) async-start(bf16[32,128,896]{2,1,0:T(8,128)(2,1)} %copy.56), calls=%async_computation.2 | async-start | bytes 14680064 | tf_op jit(solution)/shard_map/all_to_all | solution.py:98
  398.2 403.3 %all-reduce.3.cloned.1.call-start = ((), (), s32[]{:S(2)}) async-start(), calls=%async_computation.3 | async-start | bytes 29360128
  433.4 22.1 %collective-permute-start.1 = (bf16[2,63,2048]{2,1,0:T(8,128)(2,1)S(1)}, bf16[2,63,2048]{2,1,0:T(8,128)(2,1)}, u32[]{:S(2)}, u32[]{:S(2)}) collective-permute-start(bf16[2,63,2048]{2,1,0:T(8,128)(2,1)S(1)} %slice.44), channel_id=1, source_target_pairs={{0,1},{1,2},{2,3},{3,4},{4,5},{5,6},{6,7},{8,9},{9,10},{10,11},{11... | collective-permute-start | bytes 1548296 | tf_op jit(solution)/shard_map/ppermute | solution.py:15
  451.1 7.5 collective-permute-start.3
  455.4 3.2 slice-start
  455.4 348.0 %copy-start.7 = (s32[32]{0:T(128)S(1)}, s32[32]{0:T(128)}, u32[]{:S(2)}) copy-start(s32[32]{0:T(128)} %copy-done.6) | copy-start | bytes 388
Sparse Core Ops, SparseCore 0:
  419.8 381.5 all-reduce.2
where the time goes:
time: 852 us; the launch traced here: 846 us
  waiting for transfers between devices  488 us (57%)
  matrix products  145 us (17%)
  local copies, waits for them, and re-layouts  141 us (17%)
  other arithmetic  26.9 us (3%)
  starting transfers between devices  20 us (2%)
  between operations  14.6 us (2%)
  blocking collectives  11.7 us (1%)
    unnamed x2, waiting for transfers between devices  340 us
    all_to_all x1, waiting for transfers between devices, local(): lax.all_to_all(outgoing, 'dp', split_axis=0, concat_axis=0, tiled=True)  147 us
    unnamed x32, local copies, waits for them, and re-layouts  58.9 us
    dot_general x1, matrix products, local(): jnp.einsum('pz,xz->px', proj_grads, both_weights, preferred_element_type=...  23.1 us
    dot_general x1, matrix products, local(): jnp.einsum('px,pz->xz', neighbours, proj_grads, preferred_element_type=jn...  21.4 us
  transfers between devices with their start and end apart: 7, of which 3 were waited for; matrix products, arithmetic and copies ran while one was open for 8% of the time, Pallas kernels for 0%

commit v1 on v0

--- a/solution.py
+++ b/solution.py
@@ -118,12 +118,23 @@
     )
     context = jnp.concatenate([prior_context, context_shift[:, :keep_rows]], axis=1)
     query_grad = jnp.concatenate([prior_grads, query_shift[:, :keep_rows]], axis=1)
+    seq_total = lax.axis_size("seq")
+    enc_share = ENC // (shard_count * seq_total)
+    seq_major = (
+        neighbours.reshape(ref_count * NB_LEN, shard_count, seq_total, enc_share)
+        .transpose(0, 2, 1, 3)
+        .reshape(ref_count * NB_LEN, ENC)
+    )
+    weight_terms = jnp.einsum(
+        "px,pz->xz", seq_major, proj_grads, preferred_element_type=jnp.float32
+    ).reshape(seq_total, shard_count * enc_share, 2 * feat_width)
+    plane_sums = lax.psum_scatter(weight_terms, "seq", scatter_dimension=0, tiled=True)
     owned_grads = lax.psum_scatter(
-        jnp.einsum("px,pz->xz", neighbours, proj_grads, preferred_element_type=jnp.float32),
-        ("dp", "seq"),
+        plane_sums.reshape(shard_count, enc_share, 2 * feat_width),
+        "dp",
         scatter_dimension=0,
         tiled=True,
-    )
+    ).reshape(enc_share, 2 * feat_width)
     return (
         context,
         query_grad,

time: 852 us -> 689 us (0.81)
  waiting for transfers between devices: 488 us -> 299 us
  local copies, waits for them, and re-layouts: 141 us -> 164 us
    unnamed x2, waiting for transfers between devices: 340 us -> 0.03 us
    all_to_all x1, waiting for transfers between devices: 0.01 us -> 104 us  [local(): lax.all_to_all(slot_grads.reshape(slot_count, NB_LEN, ENC).astype(jnp.bfl...]
    reduce_scatter x0 -> x2, waiting for transfers between devices: none -> 47.4 us  [the longest x1 47.4 us: local(): lax.psum_scatter(weight_terms, 'seq', scatter_dimension=0, tiled=True)]
    gather x1 -> x3, local copies, waits for them, and re-layouts: 5.88 us -> 19.4 us  [local(): jnp.take(incoming, slot_index, axis=0).reshape(ref_count * NB_LEN, ENC)]
    reshape x0 -> x2, local copies, waits for them, and re-layouts: none -> 8.84 us  [the longest x1 5.84 us: local(): seq_major = neighbours.reshape(ref_count * NB_LEN, shard_count, seq_total...]
    unnamed x32 -> x28, local copies, waits for them, and re-layouts: 58.9 us -> 57.1 us
  transfers between devices with their start and end apart: 7 -> 8, of which waited for: 3 -> 4; matrix products, arithmetic and copies ran while one was open for 8% -> 19% of each run, Pallas kernels for 0% -> 0%
where the time goes in v1:
time: 689 us; the launch traced here: 684 us
  waiting for transfers between devices  299 us (43%)
  local copies, waits for them, and re-layouts  164 us (24%)
  matrix products  148 us (21%)
  other arithmetic  27.7 us (4%)
  starting transfers between devices  19.3 us (3%)
  between operations  14.6 us (2%)
  blocking collectives  11.7 us (2%)
    all_to_all x1, waiting for transfers between devices, local(): lax.all_to_all(outgoing, 'dp', split_axis=0, concat_axis=0, tiled=True)  147 us
    all_to_all x1, waiting for transfers between devices, local(): lax.all_to_all(slot_grads.reshape(slot_count, NB_LEN, ENC).astype(jnp.bfl...  104 us
    unnamed x28, local copies, waits for them, and re-layouts  57.1 us
    reduce_scatter x1, waiting for transfers between devices, local(): lax.psum_scatter(weight_terms, 'seq', scatter_dimension=0, tiled=True)  47.4 us
    dot_general x1, matrix products, local(): jnp.einsum('pz,xz->px', proj_grads, both_weights, preferred_element_type=...  23.8 us
    dot_general x1, matrix products, local(): jnp.einsum('px,pz->xz', seq_major, proj_grads, preferred_element_type=jnp...  20.2 us
    gather x3, local copies, waits for them, and re-layouts, local(): jnp.take(incoming, slot_index, axis=0).reshape(ref_count * NB_LEN, ENC)  19.4 us
    dot_general x1, matrix products, local(): jnp.einsum('rs,sx->rx', row_hits, returned.reshape(slot_count, NB_LEN * E...  16.6 us
  transfers between devices with their start and end apart: 8, of which 4 were waited for; matrix products, arithmetic and copies ran while one was open for 19% of the time, Pallas kernels for 0%

profile of v1, /device:TPU:0, one launch (start us, length us, event | category | flops | bytes accessed | tf_op | source)
XLA Modules:
  0.0 684.3 jit_solution(4496259338128169139)
XLA Ops:
  9.8 11.7 %all_to_all.25 = s32[4,8,1]{1,2,0:T(1,128)S(1)} all-to-all(s32[4,8,1]{1,2,0:T(1,128)S(1)} %bitcast.118), channel_id=1, replica_groups=mesh['dp'=4,'seq'=8] {'dp'}, dimensions={0} | all-to-all | bytes 256 | tf_op jit(solution)/shard_map/all_to_all | solution.py:41
  23.4 7.5 %gather_fusion = bf16[32,128,896]{2,1,0:T(8,128)(2,1)} fusion(bf16[32,128,896]{2,1,0:T(8,128)(2,1)} %param.9, s32[1024]{0:T(1024)S(1)} %pad_clamp_fusion.1), kind=kCustom, calls=%fused_computation | custom fusion | bytes 14680192 | tf_op jit(solution)/shard_map/jit(_take)/gather | solution.py:42
  30.9 6.9 %broadcast_select_fusion = bf16[32,128,896]{2,1,0:T(8,128)(2,1)} fusion(bf16[32,128,896]{2,1,0:T(8,128)(2,1)} %gather_fusion, pred[32]{0:T(512)(128)(4,1)S(1)} %compare_and_fusion), kind=kLoop, calls=%fused_computation.33 | loop fusion | flops 3670016 | bytes 14680096 | tf_op jit(solution)/shard_map/jit(_take)/select_n | solution.py:42
  55.8 147.0 %all-to-all-done.1 = bf16[32,128,896]{2,1,0:T(8,128)(2,1)} async-done(((bf16[32,128,896]{2,1,0:T(8,128)(2,1)}), bf16[32,128,896]{2,1,0:T(8,128)(2,1)}, u32[]{:S(2)}, u32[]{:S(2)}) %all-to-all-start.1) | async-done | bytes 7340064 | tf_op jit(solution)/shard_map/all_to_all | solution.py:43
  236.6 13.7 %convert_bitcast_fusion.2 = bf16[256,8,16,128]{3,1,2,0:T(8,128)(2,1)} fusion(bf16[2048,896]{1,0:T(8,128)(2,1)} %bitcast_select_fusion, bf16[896,2048]{1,0:T(8,128)(2,1)} %param.10), kind=kOutput, calls=%fused_computation.11 | convolution fusion | flops 7520387072 | bytes 15728640 | tf_op jit(solution)/shard_map/dot_general | solution.py:45
  250.3 9.8 %copy.66 = bf16[256,8,16,128]{3,2,1,0:T(8,128)(2,1)} copy(bf16[256,8,16,128]{3,1,2,0:T(8,128)(2,1)} %convert_bitcast_fusion.2) | data formatting | bytes 16777216
  260.1 13.9 %convert_bitcast_fusion.3 = bf16[256,8,16,128]{3,1,2,0:T(8,128)(2,1)} fusion(bf16[2048,896]{1,0:T(8,128)(2,1)} %bitcast_select_fusion, bf16[896,2048]{1,0:T(8,128)(2,1)} %param.11), kind=kOutput, calls=%fused_computation.12 | convolution fusion | flops 7520387072 | bytes 15728640 | tf_op jit(solution)/shard_map/dot_general | solution.py:48
  273.9 9.8 %copy.67 = bf16[256,8,16,128]{3,2,1,0:T(8,128)(2,1)} copy(bf16[256,8,16,128]{3,1,2,0:T(8,128)(2,1)} %convert_bitcast_fusion.3) | data formatting | bytes 16777216
  290.5 7.3 %convert_bitcast_fusion = bf16[8,256,16,128]{1,3,2,0:T(8,128)(2,1)} fusion(bf16[8,64,16,128]{3,2,1,0:T(8,128)(2,1)} %bitcast.114, f32[8,16,64,256]{3,2,1,0:T(8,128)S(1)} %get-tuple-element.25, f32[8,16,64]{2,1,0:T(8,128)S(1)} %get-tuple-element.24), kind=kOutput, calls=%fused_computation.6 | convolution fusion | flops 547356672 | bytes 18907136 | tf_op jit(solution)/shard_map/chqk,cqhd->ckhd/dot_general | solution.py:85
  297.8 9.8 %multiply_reduce_fusion = (f32[8,16,64]{2,1,0:T(8,128)S(1)}, f32[8,16,64,256]{3,2,1,0:T(8,128)}) fusion(f32[8,16,64]{2,1,0:T(8,128)S(1)} %get-tuple-element.24, f32[8,16,64,256]{3,2,1,0:T(8,128)S(1)} %get-tuple-element.25, bf16[8,256,16,128]{3,2,1,0:T(8,128)(2,1)} %bitcast.109, bf16[8,64,16,128]{3,2,1,0:T(8,128)(2,1)S(1)} %bitcast.115), kind=kOutput, calls=%fused_computation.9 | convolution fusion | flops 545251328 | bytes 27328512 | tf_op jit(solution)/shard_map/cqhd,ckhd->chqk/dot_general | solution.py:72
  307.7 12.6 %copy.56 = bf16[8,256,16,128]{3,2,1,0:T(8,128)(2,1)} copy(bf16[8,256,16,128]{1,3,2,0:T(8,128)(2,1)} %convert_bitcast_fusion) | data formatting | bytes 16777216 | tf_op jit(solution)/shard_map/convert_element_type | solution.py:88
  320.3 7.2 %multiply_convert_fusion = bf16[8,16,64,256]{3,2,1,0:T(8,128)(2,1)S(1)} fusion(f32[8,16,64,256]{3,2,1,0:T(8,128)} %get-tuple-element.27, f32[8,16,64]{2,1,0:T(8,128)S(1)} %get-tuple-element.26, f32[8,16,64]{2,1,0:T(8,128)S(1)} %get-tuple-element.24, f32[8,16,64,256]{3,2,1,0:T(8,128)} %copy-done.1), kind=kLoop, calls=%fused_computation.8 | loop fusion | flops 12582912 | bytes 21037056 | tf_op jit(solution)/shard_map/convert_element_type | solution.py:76
  335.3 12.8 %copy.54 = bf16[8,256,16,128]{3,2,1,0:T(8,128)(2,1)} copy(bf16[8,256,16,128]{1,3,2,0:T(8,128)(2,1)} %convert_bitcast_fusion.1) | data formatting | bytes 16777216 | tf_op jit(solution)/shard_map/convert_element_type | solution.py:84
  348.1 11.1 %bitcast_dynamic-update-slice_fusion.1 = bf16[2048,4096]{1,0:T(8,128)(2,1)} fusion(bf16[256,8,16,128]{3,2,1,0:T(8,128)(2,1)} %bitcast.105), kind=kLoop, calls=%fused_computation.5 | loop fusion | bytes 16777216
  359.2 11.3 %bitcast_dynamic-update-slice_fusion = bf16[2048,4096]{1,0:T(8,128)(2,1)} fusion(bf16[2048,4096]{1,0:T(8,128)(2,1)} %bitcast_dynamic-update-slice_fusion.1, bf16[256,8,16,128]{3,2,1,0:T(8,128)(2,1)} %bitcast.104), kind=kLoop, calls=%fused_computation.4 | loop fusion | bytes 16777216 | tf_op jit(solution)/shard_map/concatenate | solution.py:89
  370.5 20.2 %fusion = f32[8,112,4096]{2,1,0:T(8,128)} fusion(bf16[8,112,2048]{2,1,0:T(8,128)(2,1)S(1)} %bitcast.113, bf16[2048,4096]{1,0:T(8,128)(2,1)} %bitcast_dynamic-update-slice_fusion), kind=kOutput, calls=%fused_computation.2 | convolution fusion | flops 15032385536 | bytes 35127296 | tf_op jit(solution)/shard_map/px,pz->xz/dot_general | solution.py:128
  390.7 23.8 %fusion.18 = f32[2048,896]{1,0:T(8,128)} fusion(bf16[2048,4096]{1,0:T(8,128)(2,1)} %bitcast_dynamic-update-slice_fusion, bf16[896,2048]{1,0:T(8,128)(2,1)} %param.11, bf16[896,2048]{1,0:T(8,128)(2,1)} %param.10), kind=kOutput, calls=%fused_computation.29 | convolution fusion | flops 15047065600 | bytes 31457280 | tf_op jit(solution)/shard_map/pz,xz->px/dot_general | solution.py:91
  420.1 15.0 %fusion.22 = bf16[32,128,896]{2,0,1:T(8,128)(2,1)S(1)} fusion(f32[2,128,8,896]{3,2,1,0:T(8,128)} %bitcast.106, s32[16]{0:T(128)S(1)} %copy-done.9), kind=kOutput, calls=%fused_computation.34 | convolution fusion | flops 708314624 | bytes 14680128 | tf_op jit(solution)/shard_map/rs,rx->sx/dot_general | solution.py:95
  446.2 47.4 %reduce-scatter.3.cloned.1.call-done = f32[1,112,4096]{2,1,0:T(8,128)} async-done(((f32[8,112,4096]{2,1,0:T(8,128)}), f32[1,112,4096]{2,1,0:T(8,128)}) %reduce-scatter.3.cloned.1.call-update) | async-done | bytes 1835024 | tf_op jit(solution)/shard_map/reduce_scatter | solution.py:131
  496.6 8.0 %convert_bitcast_fusion.5 = bf16[8,64,16,128]{3,1,2,0:T(8,128)(2,1)S(1)} fusion(bf16[8,256,16,128]{3,2,1,0:T(8,128)(2,1)} %bitcast.110, f32[8,16,64,256]{3,2,1,0:T(8,128)} %copy-done.1, f32[8,16,64]{2,1,0:T(8,128)S(1)} %get-tuple-element.24), kind=kOutput, calls=%fused_computation.42 | convolution fusion | flops 544210944 | bytes 18907136 | tf_op jit(solution)/shard_map/chqk,ckhd->cqhd/dot_general | solution.py:68
  512.1 7.3 %convert_bitcast_fusion.4 = bf16[8,64,16,128]{3,1,2,0:T(8,128)(2,1)S(1)} fusion(bf16[8,16,64,256]{3,2,1,0:T(8,128)(2,1)} %copy-done, bf16[8,256,16,128]{3,2,1,0:T(8,128)(2,1)} %bitcast.103), kind=kOutput, calls=%fused_computation.41 | convolution fusion | flops 537919488 | bytes 14680064 | tf_op jit(solution)/shard_map/chqk,ckhd->cqhd/dot_general | solution.py:77
  535.0 104.4 %all-to-all-done.2 = bf16[32,128,896]{2,1,0:T(8,128)(2,1)} async-done(((bf16[32,128,896]{2,1,0:T(8,128)(2,1)}), bf16[32,128,896]{2,1,0:T(8,128)(2,1)}, u32[]{:S(2)}, u32[]{:S(2)}) %all-to-all-start.2) | async-done | bytes 7340064 | tf_op jit(solution)/shard_map/all_to_all | solution.py:98
  639.4 16.6 %fusion.12 = f32[32,128,896]{2,0,1:T(8,128)} fusion(s32[32]{0:T(128)S(1)} %copy-done.7, bf16[4,8,128,896]{3,2,1,0:T(8,128)(2,1)} %bitcast.50), kind=kOutput, calls=%fused_computation.23 | convolution fusion | flops 234882048 | bytes 22020224 | tf_op jit(solution)/shard_map/rs,sx->rx/dot_general | solution.py:108
  656.0 19.3 %copy.62 = f32[32,128,896]{2,1,0:T(8,128)} copy(f32[32,128,896]{2,0,1:T(8,128)} %fusion.12) | data formatting | bytes 29360128
  (90 shorter events, 115.3 us)
Async XLA Ops:
  9.1 0.5 copy-start.8
  22.8 0.5 copy-start.6
  37.8 8.0 %copy-start.3 = (bf16[2,256,2048]{2,1,0:T(8,128)(2,1)S(1)}, bf16[2,256,2048]{2,1,0:T(8,128)(2,1)}, u32[]{:S(2)}) copy-start(bf16[2,256,2048]{2,1,0:T(8,128)(2,1)} %param.7) | copy-start | bytes 6291460
  37.8 9.5 %copy-start.5 = (s32[1,1,8,2]{2,3,1,0:T(2,128)S(1)}, s32[1,1,8,2]{2,3,1,0:T(2,128)}, u32[]{:S(2)}) copy-start(s32[1,1,8,2]{2,3,1,0:T(2,128)} %param.12) | copy-start | bytes 196
  37.8 165.0 %all-to-all-start.1 = ((bf16[32,128,896]{2,1,0:T(8,128)(2,1)}), bf16[32,128,896]{2,1,0:T(8,128)(2,1)}, u32[]{:S(2)}, u32[]{:S(2)}) async-start(bf16[32,128,896]{2,1,0:T(8,128)(2,1)} %broadcast_select_fusion), calls=%async_computation.1 | async-start | bytes 14680064 | tf_op jit(solution)/shard_map/all_to_all | solution.py:43
  43.4 450.1 %reduce-scatter.3.cloned.1.call-start = ((), (), s32[]{:S(2)}) async-start(), calls=%async_computation.5 | async-start | bytes 16515072 | tf_op jit(solution)/shard_map/reduce_scatter | solution.py:131
  44.5 8.0 %collective-permute-start.2 = (bf16[2,63,2048]{2,1,0:T(8,128)(2,1)S(1)}, bf16[2,63,2048]{2,1,0:T(8,128)(2,1)}, u32[]{:S(2)}, u32[]{:S(2)}) collective-permute-start(bf16[2,63,2048]{2,1,0:T(8,128)(2,1)S(1)} %slice.35), channel_id=1, source_target_pairs={{1,0},{2,1},{3,2},{4,3},{5,4},{6,5},{7,6},{9,8},{10,9},{11,10},{12... | collective-permute-start | bytes 1548296 | tf_op jit(solution)/shard_map/ppermute | solution.py:15
  45.9 4.6 collective-permute-start
  290.5 7.3 %copy-start.1 = (f32[8,16,64,256]{3,2,1,0:T(8,128)}, f32[8,16,64,256]{3,2,1,0:T(8,128)S(1)}, u32[]{:S(2)}) copy-start(f32[8,16,64,256]{3,2,1,0:T(8,128)S(1)} %get-tuple-element.25) | copy-start | bytes 25165828
  290.5 7.3 %copy-start.4 = (bf16[64,8,16,128]{3,2,1,0:T(8,128)(2,1)S(1)}, bf16[64,8,16,128]{3,2,1,0:T(8,128)(2,1)}, u32[]{:S(2)}) copy-start(bf16[64,8,16,128]{3,2,1,0:T(8,128)(2,1)} %copy.68) | copy-start | bytes 6291460
  327.5 1.9 copy-start
  359.2 11.3 %copy-start.2 = (bf16[2048,896]{0,1:T(8,128)(2,1)S(1)}, bf16[2048,896]{0,1:T(8,128)(2,1)}, u32[]{:S(2)}) copy-start(bf16[2048,896]{0,1:T(8,128)(2,1)} %reshape.156) | copy-start | bytes 11010052
  414.5 5.7 copy-start.9
  440.7 198.7 %all-to-all-start.2 = ((bf16[32,128,896]{2,1,0:T(8,128)(2,1)}), bf16[32,128,896]{2,1,0:T(8,128)(2,1)}, u32[]{:S(2)}, u32[]{:S(2)}) async-start(bf16[32,128,896]{2,1,0:T(8,128)(2,1)} %copy.58), calls=%async_computation.2 | async-start | bytes 14680064 | tf_op jit(solution)/shard_map/all_to_all | solution.py:98
  446.1 229.2 %reduce-scatter.5.cloned.1.call-start = ((), (), s32[]{:S(2)}) async-start(), calls=%async_computation.6 | async-start | bytes 2621440 | tf_op jit(solution)/shard_map/reduce_scatter | solution.py:132
  510.3 21.2 %collective-permute-start.1 = (bf16[2,63,2048]{2,1,0:T(8,128)(2,1)S(1)}, bf16[2,63,2048]{2,1,0:T(8,128)(2,1)S(1)}, u32[]{:S(2)}, u32[]{:S(2)}) collective-permute-start(bf16[2,63,2048]{2,1,0:T(8,128)(2,1)S(1)} %slice.44), channel_id=1, source_target_pairs={{0,1},{1,2},{2,3},{3,4},{4,5},{5,6},{6,7},{8,9},{9,10},{10,11},{11... | collective-permute-start | bytes 1548296 | tf_op jit(solution)/shard_map/ppermute | solution.py:15
  526.3 7.0 %slice-start = ((bf16[2,256,2048]{2,1,0:T(8,128)(2,1)}), bf16[2,193,2048]{2,1,0:T(8,128)(2,1)S(1)}, s32[]{:S(2)}) async-start(bf16[2,256,2048]{2,1,0:T(8,128)(2,1)} %reshape.151), calls=%async_computation.7 | async-start | bytes 3276800 | tf_op jit(solution)/shard_map/slice | solution.py:120
  527.6 111.9 %copy-start.7 = (s32[32]{0:T(128)S(1)}, s32[32]{0:T(128)}, u32[]{:S(2)}) copy-start(s32[32]{0:T(128)} %copy-done.6) | copy-start | bytes 388
  527.6 5.7 collective-permute-start.3
Sparse Core Ops, SparseCore 0:
  390.8 102.6 reduce-scatter.2
  496.7 112.8 reduce-scatter.4

commit v2 on v0

v2 whole, which is shorter than its diff:
```python
import jax
import jax.numpy as jnp
from jax import lax
from jax.sharding import PartitionSpec as P

HD = 128
ENC = 896
SPAN = 64
NB_LEN = 128
CHUNKS = 4


def shifted(array, axis, by):
    count = lax.axis_size(axis)
    pairs = [(i, i + by) for i in range(count) if 0 <= i + by < count]
    return lax.ppermute(array, axis, pairs)


def one_hot(index, count):
    return (index[:, None] == jnp.arange(count, dtype=jnp.int32)[None, :]).astype(jnp.int32)


def attend_chunk(query_blocks, grad_blocks, neighbours, key_weight, value_weight, head_count):
    block_count = query_blocks.shape[0]
    near_len = neighbours.shape[0] // block_count
    key_rows = jnp.dot(neighbours, key_weight, preferred_element_type=jnp.float32).astype(
        jnp.bfloat16
    )
    value_rows = jnp.dot(neighbours, value_weight, preferred_element_type=jnp.float32).astype(
        jnp.bfloat16
    )
    key_heads = key_rows.reshape(block_count, near_len, head_count, HD)
    value_heads = value_rows.reshape(block_count, near_len, head_count, HD)
    score_scale = HD ** (-0.5)
    scores = (
        jnp.einsum("cqhd,ckhd->chqk", query_blocks, key_heads, preferred_element_type=jnp.float32)
        * score_scale
    )
    weights = jnp.exp(scores)
    weights = weights / jnp.sum(weights, axis=-1, keepdims=True)
    weight_half = weights.astype(jnp.bfloat16)
    context_shift = jnp.einsum(
        "chqk,ckhd->cqhd", weight_half, value_heads, preferred_element_type=jnp.float32
    ).astype(jnp.bfloat16)
    prob_grads = jnp.einsum(
        "cqhd,ckhd->chqk", grad_blocks, value_heads, preferred_element_type=jnp.float32
    )
    row_delta = jnp.sum(weights * prob_grads, axis=-1, keepdims=True)
    score_grads = (score_scale * weights * (prob_grads - row_delta)).astype(jnp.bfloat16)
    query_shift = jnp.einsum(
        "chqk,ckhd->cqhd", score_grads, key_heads, preferred_element_type=jnp.float32
    ).astype(jnp.bfloat16)
    key_grads = jnp.einsum(
        "chqk,cqhd->ckhd", score_grads, query_blocks, preferred_element_type=jnp.float32
    ).astype(jnp.bfloat16)
    value_grads = jnp.einsum(
        "chqk,cqhd->ckhd", weight_half, grad_blocks, preferred_element_type=jnp.float32
    ).astype(jnp.bfloat16)
    feat_width = head_count * HD
    proj_grads = jnp.concatenate(
        [
            key_grads.reshape(block_count * near_len, feat_width),
            value_grads.reshape(block_count * near_len, feat_width),
        ],
        axis=1,
    )
    both_weights = jnp.concatenate([key_weight, value_weight], axis=1)
    near_grads = jnp.einsum(
        "pz,xz->px", proj_grads, both_weights, preferred_element_type=jnp.float32
    )
    return context_shift, query_shift, proj_grads, near_grads


def local(queries, d_context, database, key_weight, value_weight, neighbour_shard, neighbour_row):
    seq_count, seq_span, feat_width = queries.shape
    head_count = feat_width // HD
    lag_rows = SPAN - 1
    block_count = seq_count * seq_span // SPAN
    pick_count = neighbour_shard.shape[-1]
    ref_count = block_count * pick_count
    shard_count = lax.axis_size("dp")
    seq_total = lax.axis_size("seq")
    capacity = 2 * ref_count // shard_count
    chunk_count = CHUNKS if block_count % CHUNKS == 0 else 1
    chunk_blocks = block_count // chunk_count
    chunk_refs = chunk_blocks * pick_count
    chunk_cap = min(chunk_blocks, capacity)
    chunk_slots = shard_count * chunk_cap

    own = lax.axis_index("dp")
    target = neighbour_shard.reshape(chunk_count, chunk_refs)
    wanted = neighbour_row.reshape(chunk_count, chunk_refs)
    slot_indices = []
    requests = []
    slot_refs = []
    for g in range(chunk_count):
        owners = one_hot(target[g], shard_count)
        before = jnp.cumsum(owners, axis=0) - owners
        slot_rank = jnp.sum(before * owners, axis=1)
        asked = one_hot(target[g] * chunk_cap + slot_rank, chunk_slots)
        requests.append(
            jnp.sum(asked * wanted[g][:, None], axis=0).reshape(shard_count, 1, chunk_cap)
        )
        slot_index = ((own - target[g]) % shard_count) * chunk_cap + slot_rank
        placed = one_hot(slot_index, chunk_slots)
        ref_ids = jnp.arange(1, chunk_refs + 1, dtype=jnp.int32)
        slot_refs.append(jnp.sum(placed * ref_ids[:, None], axis=0))
        slot_indices.append(slot_index)
    request = jnp.concatenate(requests, axis=1)
    arrived = lax.all_to_all(request, "dp", split_axis=0, concat_axis=0, tiled=True)
    offsets = jnp.arange(shard_count, dtype=jnp.int32)
    sent_rows = jnp.take(arrived, (own + offsets) % shard_count, axis=0)

    def exchange(parts, direction):
        received = [parts[0]]
        for k in range(1, shard_count):
            pairs = [(i, (i + direction * k) % shard_count) for i in range(shard_count)]
            received.append(lax.ppermute(parts[k], "dp", pairs))
        return jnp.stack(received, axis=0)

    head_rows, head_grads = shifted((queries[:, :lag_rows], d_context[:, :lag_rows]), "seq", -1)
    query_blocks = jnp.concatenate([queries[:, lag_rows:], head_rows], axis=1).reshape(
        block_count, SPAN, head_count, HD
    )
    grad_blocks = jnp.concatenate([d_context[:, lag_rows:], head_grads], axis=1).reshape(
        block_count, SPAN, head_count, HD
    )

    enc_share = ENC // (shard_count * seq_total)
    context_parts = []
    query_parts = []
    returned_parts = []
    weight_terms = None
    for g in range(chunk_count):
        outgoing = jnp.take(database, sent_rows[:, g, :].reshape(chunk_slots), axis=0)
        incoming = exchange(outgoing.reshape(shard_count, chunk_cap, NB_LEN, ENC), 1)
        neighbours = jnp.take(
            incoming.reshape(chunk_slots, NB_LEN, ENC), slot_indices[g], axis=0
        ).reshape(chunk_refs * NB_LEN, ENC)
        blocks = slice(g * chunk_blocks, (g + 1) * chunk_blocks)
        context_shift, query_shift, proj_grads, near_grads = attend_chunk(
            query_blocks[blocks], grad_blocks[blocks], neighbours, key_weight, value_weight,
            head_count,
        )
        context_parts.append(context_shift)
        query_parts.append(query_shift)
        padded = jnp.concatenate(
            [
                jnp.zeros((1, NB_LEN, ENC), jnp.bfloat16),
                near_grads.astype(jnp.bfloat16).reshape(chunk_refs, NB_LEN, ENC),
            ],
            axis=0,
        )
        slot_grads = jnp.take(padded, slot_refs[g], axis=0)
        returned_parts.append(
            exchange(slot_grads.reshape(shard_count, chunk_cap, NB_LEN, ENC), -1)
        )
        seq_major = (
            neighbours.reshape(chunk_refs * NB_LEN, shard_count, seq_total, enc_share)
            .transpose(0, 2, 1, 3)
            .reshape(chunk_refs * NB_LEN, ENC)
        )
        term = jnp.einsum("px,pz->xz", seq_major, proj_grads, preferred_element_type=jnp.float32)
        weight_terms = term if weight_terms is None else weight_terms + term

    returned = jnp.stack(
        [part.reshape(shard_count, chunk_cap, NB_LEN * ENC) for part in returned_parts], axis=1
    ).reshape(shard_count * chunk_count * chunk_cap, NB_LEN * ENC)
    row_hits = one_hot(sent_rows.reshape(-1), database.shape[0]).astype(jnp.bfloat16)
    database_grad = jnp.einsum(
        "sr,sx->rx", row_hits, returned, preferred_element_type=jnp.float32
    ).reshape(database.shape)

    context_shift = jnp.concatenate(context_parts, axis=0).reshape(seq_count, seq_span, feat_width)
    query_shift = jnp.concatenate(query_parts, axis=0).reshape(seq_count, seq_span, feat_width)
    keep_rows = seq_span - lag_rows
    prior_context, prior_grads = shifted(
        (context_shift[:, keep_rows:], query_shift[:, keep_rows:]), "seq", 1
    )
    context = jnp.concatenate([prior_context, context_shift[:, :keep_rows]], axis=1)
    query_grad = jnp.concatenate([prior_grads, query_shift[:, :keep_rows]], axis=1)

    plane_sums = lax.psum_scatter(
        weight_terms.reshape(seq_total, shard_count * enc_share, 2 * feat_width),
        "seq",
        scatter_dimension=0,
        tiled=True,
    )
    owned_grads = lax.psum_scatter(
        plane_sums.reshape(shard_count, enc_share, 2 * feat_width),
        "dp",
        scatter_dimension=0,
        tiled=True,
    ).reshape(enc_share, 2 * feat_width)
    return (
        context,
        query_grad,
        database_grad,
        owned_grads[:, :feat_width],
        owned_grads[:, feat_width:],
    )


def solution(mesh):
    return jax.shard_map(
        local,
        mesh=mesh,
        in_specs=(
            P("dp", "seq", None),
            P("dp", "seq", None),
            P(("dp", "seq"), None, None),
            P(),
            P(),
            P("dp", "seq", None, None),
            P("dp", "seq", None, None),
        ),
        out_specs=(
            P("dp", "seq", None),
            P("dp", "seq", None),
            P(("dp", "seq"), None, None),
            P(("dp", "seq"), None),
            P(("dp", "seq"), None),
        ),
        check_vma=False,
    )
```

time: 852 us -> 697 us (0.82)
  the two profiles are of different devices: /device:TPU:0 before, /device:TPU:24 now
where the time goes in v2:
time: 697 us; the launch traced here: 688 us
  local copies, waits for them, and re-layouts  237 us (34%)
  matrix products  155 us (22%)
  starting transfers between devices  136 us (20%)
  waiting for transfers between devices  84.4 us (12%)
  other arithmetic  60.7 us (9%)
  between operations  15.7 us (2%)
    ppermute x24, starting transfers between devices, exchange(): received.append(lax.ppermute(parts[k], 'dp', pairs))  122 us
    ppermute x24, waiting for transfers between devices, exchange(): received.append(lax.ppermute(parts[k], 'dp', pairs))  84.4 us
    unnamed x206, local copies, waits for them, and re-layouts  77.1 us
    dot_general x4, matrix products, local(): jnp.einsum('px,pz->xz', seq_major, proj_grads, preferred_element_type=jnp...  44.4 us
    dot_general x4, matrix products, attend_chunk(): jnp.einsum('pz,xz->px', proj_grads, both_weights, preferred_element_type=...  28.9 us
    another operation x16, local copies, waits for them, and re-layouts, exchange(): return jnp.stack(received, axis=0)  22.2 us
    another operation x1, other arithmetic, local(): jnp.stack([part.reshape(shard_count, chunk_cap, NB_LEN * ENC) for part in...  21.1 us
    gather x4, local copies, waits for them, and re-layouts, local(): jnp.take(database, sent_rows[:, g, :].reshape(chunk_slots), axis=0)  19.1 us
  transfers between devices with their start and end apart: 31, of which 5 were waited for; matrix products, arithmetic and copies ran while one was open for 37% of the time, Pallas kernels for 0%

profile of v2, /device:TPU:24, one launch (start us, length us, event | category | flops | bytes accessed | tf_op | source)
XLA Modules:
  0.0 688.4 jit_solution(11192574015258072280)
XLA Ops:
  64.8 32.0 %collective-permute-done.8 = bf16[2,128,896]{2,1,0:T(8,128)(2,1)} collective-permute-done((bf16[2,128,896]{2,1,0:T(8,128)(2,1)}, bf16[2,128,896]{2,1,0:T(8,128)(2,1)}, u32[]{:S(2)}, u32[]{:S(2)}) %collective-permute-start.8) | collective-permute-done | bytes 458784 | tf_op jit(solution)/shard_map/ppermute | solution.py:118
  102.9 13.6 %collective-permute-start.6 = (bf16[2,128,896]{2,1,0:T(8,128)(2,1)}, bf16[2,128,896]{2,1,0:T(8,128)(2,1)}, u32[]{:S(2)}, u32[]{:S(2)}) collective-permute-start(bf16[2,128,896]{2,1,0:T(8,128)(2,1)} %get-tuple-element.73), channel_id=1, source_target_pairs={{0,24},{8,0},{16,8},{24,16},{1,25},{9,1},{17,9},{25,17},{2,26},{10... | collective-permute-start | bytes 1376264 | tf_op jit(solution)/shard_map/ppermute | solution.py:118
  116.5 16.3 %collective-permute-done.1 = bf16[2,128,896]{2,1,0:T(8,128)(2,1)} collective-permute-done((bf16[2,128,896]{2,1,0:T(8,128)(2,1)}, bf16[2,128,896]{2,1,0:T(8,128)(2,1)}, u32[]{:S(2)}, u32[]{:S(2)}) %collective-permute-start.1) | collective-permute-done | bytes 458784 | tf_op jit(solution)/shard_map/ppermute | solution.py:118
  139.2 5.9 fusion.44
  156.2 15.3 %collective-permute-start.12 = (bf16[2,128,896]{2,1,0:T(8,128)(2,1)}, bf16[2,128,896]{2,1,0:T(8,128)(2,1)}, u32[]{:S(2)}, u32[]{:S(2)}) collective-permute-start(bf16[2,128,896]{2,1,0:T(8,128)(2,1)} %get-tuple-element.81), channel_id=1, source_target_pairs={{0,24},{8,0},{16,8},{24,16},{1,25},{9,1},{17,9},{25,17},{2,26},{10... | collective-permute-start | bytes 1376264 | tf_op jit(solution)/shard_map/ppermute | solution.py:118
  182.3 5.8 fusion.46
  191.9 9.1 %collective-permute-done.11 = bf16[2,128,896]{2,1,0:T(8,128)(2,1)} collective-permute-done((bf16[2,128,896]{2,1,0:T(8,128)(2,1)}, bf16[2,128,896]{2,1,0:T(8,128)(2,1)}, u32[]{:S(2)}, u32[]{:S(2)}) %collective-permute-start.11) | collective-permute-done | bytes 458784 | tf_op jit(solution)/shard_map/ppermute | solution.py:118
  351.7 7.9 %fusion.166 = f32[896,4096]{1,0:T(8,128)} fusion(bf16[512,896]{0,1:T(8,128)(2,1)S(1)} %copy-done.76, bf16[512,4096]{1,0:T(8,128)(2,1)S(1)} %bitcast_dynamic-update-slice_fusion.6), kind=kOutput, calls=%fused_computation.299 | convolution fusion | flops 3758096384 | bytes 19791872 | tf_op jit(solution)/shard_map/px,pz->xz/dot_general | solution.py:163
  359.5 7.5 %fusion.167 = f32[896,4096]{1,0:T(8,128)} fusion(bf16[512,896]{0,1:T(8,128)(2,1)S(1)} %copy-done.74, bf16[512,4096]{1,0:T(8,128)(2,1)S(1)} %copy-done.67), kind=kOutput, calls=%fused_computation.300 | convolution fusion | flops 3758096384 | bytes 19791872 | tf_op jit(solution)/shard_map/px,pz->xz/dot_general | solution.py:163
  367.0 7.6 %fusion.168 = f32[896,4096]{1,0:T(8,128)} fusion(bf16[512,896]{0,1:T(8,128)(2,1)S(1)} %copy-done.75, bf16[512,4096]{1,0:T(8,128)(2,1)S(1)} %bitcast_dynamic-update-slice_fusion.2), kind=kOutput, calls=%fused_computation.301 | convolution fusion | flops 3758096384 | bytes 19791872 | tf_op jit(solution)/shard_map/px,pz->xz/dot_general | solution.py:163
  374.6 21.5 %add_add_fusion = f32[896,4096]{1,0:T(8,128)} fusion(f32[896,4096]{1,0:T(8,128)} %fusion.168, f32[896,4096]{1,0:T(8,128)} %fusion.166, f32[896,4096]{1,0:T(8,128)} %fusion.167, bf16[512,896]{0,1:T(8,128)(2,1)S(1)} %copy-done.30, bf16[512,4096]{1,0:T(8,128)(2,1)S(1)} %bitcast_dynamic-update-slice_fusion), kind=kOutput, calls=%fused_computation.13 | convolution fusion | flops 3769106432 | bytes 63832064 | tf_op jit(solution)/shard_map/px,pz->xz/dot_general | solution.py:163
  421.1 7.8 %convolution_convert_fusion.8 = bf16[512,896]{1,0:T(8,128)(2,1)S(1)} fusion(bf16[512,4096]{1,0:T(8,128)(2,1)S(1)} %copy-done.13, bf16[896,4096]{1,0:T(8,128)(2,1)} %constant_dynamic-update-slice_fusion), kind=kOutput, calls=%fused_computation.120 | convolution fusion | flops 3758555136 | bytes 12451840 | tf_op jit(solution)/shard_map/pz,xz->px/dot_general | solution.py:68
  431.3 13.6 %collective-permute-start.27 = (bf16[2,128,896]{2,1,0:T(8,128)(2,1)}, bf16[2,128,896]{2,1,0:T(8,128)(2,1)}, u32[]{:S(2)}, u32[]{:S(2)}) collective-permute-start(bf16[2,128,896]{2,1,0:T(8,128)(2,1)} %get-tuple-element.65), channel_id=1, source_target_pairs={{0,8},{8,16},{16,24},{24,0},{1,9},{9,17},{17,25},{25,1},{2,10},{10... | collective-permute-start | bytes 1376264 | tf_op jit(solution)/shard_map/ppermute | solution.py:118
  445.4 6.9 %convolution_convert_fusion.9 = bf16[512,896]{1,0:T(8,128)(2,1)S(1)} fusion(bf16[512,4096]{1,0:T(8,128)(2,1)S(1)} %copy-done.71, bf16[896,4096]{1,0:T(8,128)(2,1)} %constant_dynamic-update-slice_fusion), kind=kOutput, calls=%fused_computation.121 | convolution fusion | flops 3758555136 | bytes 12451840 | tf_op jit(solution)/shard_map/pz,xz->px/dot_general | solution.py:68
  459.2 7.3 %convolution_convert_fusion.10 = bf16[512,896]{1,0:T(8,128)(2,1)S(1)} fusion(bf16[512,4096]{1,0:T(8,128)(2,1)S(1)} %copy-done.68, bf16[896,4096]{1,0:T(8,128)(2,1)} %constant_dynamic-update-slice_fusion), kind=kOutput, calls=%fused_computation.122 | convolution fusion | flops 3758555136 | bytes 12451840 | tf_op jit(solution)/shard_map/pz,xz->px/dot_general | solution.py:68
  466.6 7.0 %convolution_convert_fusion.11 = bf16[512,896]{1,0:T(8,128)(2,1)S(1)} fusion(bf16[512,4096]{1,0:T(8,128)(2,1)S(1)} %copy-done.73, bf16[896,4096]{1,0:T(8,128)(2,1)} %constant_dynamic-update-slice_fusion), kind=kOutput, calls=%fused_computation.123 | convolution fusion | flops 3758555136 | bytes 12451840 | tf_op jit(solution)/shard_map/pz,xz->px/dot_general | solution.py:68
  486.0 17.6 %collective-permute-done.26 = bf16[2,128,896]{2,1,0:T(8,128)(2,1)} collective-permute-done((bf16[2,128,896]{2,1,0:T(8,128)(2,1)}, bf16[2,128,896]{2,1,0:T(8,128)(2,1)}, u32[]{:S(2)}, u32[]{:S(2)}) %collective-permute-start.26) | collective-permute-done | bytes 458784 | tf_op jit(solution)/shard_map/ppermute | solution.py:118
  508.8 26.0 %collective-permute-start.16 = (bf16[2,128,896]{2,1,0:T(8,128)(2,1)}, bf16[2,128,896]{2,1,0:T(8,128)(2,1)}, u32[]{:S(2)}, u32[]{:S(2)}) collective-permute-start(bf16[2,128,896]{2,1,0:T(8,128)(2,1)} %get-tuple-element.55), channel_id=1, source_target_pairs={{0,24},{8,0},{16,8},{24,16},{1,25},{9,1},{17,9},{25,17},{2,26},{10... | collective-permute-start | bytes 1376264 | tf_op jit(solution)/shard_map/ppermute | solution.py:118
  534.8 9.3 %collective-permute-done.23 = bf16[2,128,896]{2,1,0:T(8,128)(2,1)} collective-permute-done((bf16[2,128,896]{2,1,0:T(8,128)(2,1)}, bf16[2,128,896]{2,1,0:T(8,128)(2,1)}, u32[]{:S(2)}, u32[]{:S(2)}) %collective-permute-start.23) | collective-permute-done | bytes 458784 | tf_op jit(solution)/shard_map/ppermute | solution.py:118
  545.5 29.4 %collective-permute-start.19 = (bf16[2,128,896]{2,1,0:T(8,128)(2,1)}, bf16[2,128,896]{2,1,0:T(8,128)(2,1)}, u32[]{:S(2)}, u32[]{:S(2)}) collective-permute-start(bf16[2,128,896]{2,1,0:T(8,128)(2,1)} %get-tuple-element.59), channel_id=1, source_target_pairs={{0,24},{8,0},{16,8},{24,16},{1,25},{9,1},{17,9},{25,17},{2,26},{10... | collective-permute-start | bytes 1376264 | tf_op jit(solution)/shard_map/ppermute | solution.py:118
  615.1 21.1 %maximum_maximum_fusion = bf16[4,4,2,114688]{3,2,1,0:T(2,128)(2,1)} fusion(bf16[1,1,2,114688]{3,2,1,0:T(2,128)(2,1)S(1)} %stack.141, bf16[1,1,2,114688]{3,2,1,0:T(2,128)(2,1)S(1)} %stack.140, bf16[1,1,2,114688]{3,2,1,0:T(2,128)(2,1)S(1)} %stack.139, bf16[1,1,2,114688]{3,2,1,0:T(2,128)(2,1)S(1)} %stack.138, bf16[1,1,2,114688]{3,2,1,0:T(2,128)(2,1)} %stack.136, ...), kind=kLoop, calls=%fused_computation.17 | loop fusion | flops 55050240 | bytes 14680064 | tf_op jit(solution)/shard_map/stack | solution.py:166
  636.2 7.8 %reshape.512 = bf16[32,114688]{1,0:T(8,128)(2,1)} reshape(bf16[4,4,2,114688]{3,2,1,0:T(2,128)(2,1)} %maximum_maximum_fusion) | data formatting | bytes 14680064 | tf_op jit(solution)/shard_map/reshape | solution.py:168
  644.1 10.3 %fusion = f32[32,128,896]{2,0,1:T(8,128)} fusion(bf16[4,128,8,896]{3,2,1,0:T(8,128)(2,1)} %bitcast.213, s32[32]{0:T(128)S(1)} %select_n.105), kind=kOutput, calls=%fused_computation.14 | convolution fusion | flops 234884096 | bytes 22020224 | tf_op jit(solution)/shard_map/sr,sx->rx/dot_general | solution.py:170
  654.4 19.3 %copy.204 = f32[32,128,896]{2,1,0:T(8,128)} copy(f32[32,128,896]{2,0,1:T(8,128)} %fusion) | data formatting | bytes 29360128
  (491 shorter events, 346.9 us)
Async XLA Ops:
  18.1 594.0 %reduce-scatter.3.cloned.1.call-start = ((), (), s32[]{:S(2)}) async-start(), calls=%async_computation.3 | async-start | bytes 16515072 | tf_op jit(solution)/shard_map/reduce_scatter | solution.py:183
  45.6 51.2 %collective-permute-start.8 = (bf16[2,128,896]{2,1,0:T(8,128)(2,1)}, bf16[2,128,896]{2,1,0:T(8,128)(2,1)}, u32[]{:S(2)}, u32[]{:S(2)}) collective-permute-start(bf16[2,128,896]{2,1,0:T(8,128)(2,1)} %get-tuple-element.78), channel_id=1, source_target_pairs={{0,16},{8,24},{16,0},{24,8},{1,17},{9,25},{17,1},{25,9},{2,18},{10... | collective-permute-start | bytes 1376264 | tf_op jit(solution)/shard_map/ppermute | solution.py:118
  45.6 52.5 %collective-permute-start.7 = (bf16[2,128,896]{2,1,0:T(8,128)(2,1)}, bf16[2,128,896]{2,1,0:T(8,128)(2,1)}, u32[]{:S(2)}, u32[]{:S(2)}) collective-permute-start(bf16[2,128,896]{2,1,0:T(8,128)(2,1)} %get-tuple-element.79), channel_id=1, source_target_pairs={{0,8},{8,16},{16,24},{24,0},{1,9},{9,17},{17,25},{25,1},{2,10},{10... | collective-permute-start | bytes 1376264 | tf_op jit(solution)/shard_map/ppermute | solution.py:118
  57.0 45.9 %collective-permute-start.2 = (bf16[2,128,896]{2,1,0:T(8,128)(2,1)}, bf16[2,128,896]{2,1,0:T(8,128)(2,1)}, u32[]{:S(2)}, u32[]{:S(2)}) collective-permute-start(bf16[2,128,896]{2,1,0:T(8,128)(2,1)} %get-tuple-element.69), channel_id=1, source_target_pairs={{0,24},{8,0},{16,8},{24,16},{1,25},{9,1},{17,9},{25,17},{2,26},{10... | collective-permute-start | bytes 1376264 | tf_op jit(solution)/shard_map/ppermute | solution.py:118
  57.5 75.3 %collective-permute-start.1 = (bf16[2,128,896]{2,1,0:T(8,128)(2,1)}, bf16[2,128,896]{2,1,0:T(8,128)(2,1)}, u32[]{:S(2)}, u32[]{:S(2)}) collective-permute-start(bf16[2,128,896]{2,1,0:T(8,128)(2,1)} %get-tuple-element.70), channel_id=1, source_target_pairs={{0,16},{8,24},{16,0},{24,8},{1,17},{9,25},{17,1},{25,9},{2,18},{10... | collective-permute-start | bytes 1376264 | tf_op jit(solution)/shard_map/ppermute | solution.py:118
  60.6 72.2 %collective-permute-start = (bf16[2,128,896]{2,1,0:T(8,128)(2,1)}, bf16[2,128,896]{2,1,0:T(8,128)(2,1)}, u32[]{:S(2)}, u32[]{:S(2)}) collective-permute-start(bf16[2,128,896]{2,1,0:T(8,128)(2,1)} %get-tuple-element.71), channel_id=1, source_target_pairs={{0,8},{8,16},{16,24},{24,0},{1,9},{9,17},{17,25},{25,1},{2,10},{10... | collective-permute-start | bytes 1376264 | tf_op jit(solution)/shard_map/ppermute | solution.py:118
  96.8 143.3 %collective-permute-start.14 = (bf16[2,63,2048]{2,1,0:T(8,128)(2,1)}, bf16[2,63,2048]{2,1,0:T(8,128)(2,1)}, u32[]{:S(2)}, u32[]{:S(2)}) collective-permute-start(bf16[2,63,2048]{2,1,0:T(8,128)(2,1)} %slice.283), channel_id=1, source_target_pairs={{1,0},{2,1},{3,2},{4,3},{5,4},{6,5},{7,6},{9,8},{10,9},{11,10},{12... | collective-permute-start | bytes 1548296 | tf_op jit(solution)/shard_map/ppermute | solution.py:16
  98.1 137.9 %collective-permute-start.3 = (bf16[2,63,2048]{2,1,0:T(8,128)(2,1)}, bf16[2,63,2048]{2,1,0:T(8,128)(2,1)}, u32[]{:S(2)}, u32[]{:S(2)}) collective-permute-start(bf16[2,63,2048]{2,1,0:T(8,128)(2,1)} %slice.257), channel_id=1, source_target_pairs={{1,0},{2,1},{3,2},{4,3},{5,4},{6,5},{7,6},{9,8},{10,9},{11,10},{12... | collective-permute-start | bytes 1548296 | tf_op jit(solution)/shard_map/ppermute | solution.py:16
  102.9 53.3 %collective-permute-start.6 = (bf16[2,128,896]{2,1,0:T(8,128)(2,1)}, bf16[2,128,896]{2,1,0:T(8,128)(2,1)}, u32[]{:S(2)}, u32[]{:S(2)}) collective-permute-start(bf16[2,128,896]{2,1,0:T(8,128)(2,1)} %get-tuple-element.73), channel_id=1, source_target_pairs={{0,24},{8,0},{16,8},{24,16},{1,25},{9,1},{17,9},{25,17},{2,26},{10... | collective-permute-start | bytes 1376264 | tf_op jit(solution)/shard_map/ppermute | solution.py:118
  396.1 283.4 %reduce-scatter.5.cloned.1.call-start = ((), (), s32[]{:S(2)}) async-start(), calls=%async_computation.4 | async-start | bytes 2621440 | tf_op jit(solution)/shard_map/reduce_scatter | solution.py:189
  431.3 54.4 %collective-permute-start.27 = (bf16[2,128,896]{2,1,0:T(8,128)(2,1)}, bf16[2,128,896]{2,1,0:T(8,128)(2,1)}, u32[]{:S(2)}, u32[]{:S(2)}) collective-permute-start(bf16[2,128,896]{2,1,0:T(8,128)(2,1)} %get-tuple-element.65), channel_id=1, source_target_pairs={{0,8},{8,16},{16,24},{24,0},{1,9},{9,17},{17,25},{25,1},{2,10},{10... | collective-permute-start | bytes 1376264 | tf_op jit(solution)/shard_map/ppermute | solution.py:118
  444.8 58.8 %collective-permute-start.26 = (bf16[2,128,896]{2,1,0:T(8,128)(2,1)}, bf16[2,128,896]{2,1,0:T(8,128)(2,1)}, u32[]{:S(2)}, u32[]{:S(2)}) collective-permute-start(bf16[2,128,896]{2,1,0:T(8,128)(2,1)} %get-tuple-element.66), channel_id=1, source_target_pairs={{0,16},{8,24},{16,0},{24,8},{1,17},{9,25},{17,1},{25,9},{2,18},{10... | collective-permute-start | bytes 1376264 | tf_op jit(solution)/shard_map/ppermute | solution.py:118
  444.8 59.8 %collective-permute-start.25 = (bf16[2,128,896]{2,1,0:T(8,128)(2,1)}, bf16[2,128,896]{2,1,0:T(8,128)(2,1)}, u32[]{:S(2)}, u32[]{:S(2)}) collective-permute-start(bf16[2,128,896]{2,1,0:T(8,128)(2,1)} %get-tuple-element.67), channel_id=1, source_target_pairs={{0,24},{8,0},{16,8},{24,16},{1,25},{9,1},{17,9},{25,17},{2,26},{10... | collective-permute-start | bytes 1376264 | tf_op jit(solution)/shard_map/ppermute | solution.py:118
  454.8 54.0 %collective-permute-start.24 = (bf16[2,128,896]{2,1,0:T(8,128)(2,1)}, bf16[2,128,896]{2,1,0:T(8,128)(2,1)}, u32[]{:S(2)}, u32[]{:S(2)}) collective-permute-start(bf16[2,128,896]{2,1,0:T(8,128)(2,1)} %get-tuple-element.61), channel_id=1, source_target_pairs={{0,8},{8,16},{16,24},{24,0},{1,9},{9,17},{17,25},{25,1},{2,10},{10... | collective-permute-start | bytes 1376264 | tf_op jit(solution)/shard_map/ppermute | solution.py:118
  458.1 86.0 %collective-permute-start.23 = (bf16[2,128,896]{2,1,0:T(8,128)(2,1)}, bf16[2,128,896]{2,1,0:T(8,128)(2,1)}, u32[]{:S(2)}, u32[]{:S(2)}) collective-permute-start(bf16[2,128,896]{2,1,0:T(8,128)(2,1)} %get-tuple-element.62), channel_id=1, source_target_pairs={{0,16},{8,24},{16,0},{24,8},{1,17},{9,25},{17,1},{25,9},{2,18},{10... | collective-permute-start | bytes 1376264 | tf_op jit(solution)/shard_map/ppermute | solution.py:118
  485.8 58.3 %collective-permute-start.22 = (bf16[2,128,896]{2,1,0:T(8,128)(2,1)S(1)}, bf16[2,128,896]{2,1,0:T(8,128)(2,1)S(1)}, u32[]{:S(2)}, u32[]{:S(2)}) collective-permute-start(bf16[2,128,896]{2,1,0:T(8,128)(2,1)S(1)} %copy-done.80), channel_id=1, source_target_pairs={{0,24},{8,0},{16,8},{24,16},{1,25},{9,1},{17,9},{25,17},{2,26},{10... | collective-permute-start | bytes 1376264 | tf_op jit(solution)/shard_map/ppermute | solution.py:118
  503.7 41.0 %collective-permute-start.18 = (bf16[2,128,896]{2,1,0:T(8,128)(2,1)S(1)}, bf16[2,128,896]{2,1,0:T(8,128)(2,1)S(1)}, u32[]{:S(2)}, u32[]{:S(2)}) collective-permute-start(bf16[2,128,896]{2,1,0:T(8,128)(2,1)S(1)} %get-tuple-element.53), channel_id=1, source_target_pairs={{0,8},{8,16},{16,24},{24,0},{1,9},{9,17},{17,25},{25,1},{2,10},{10... | collective-permute-start | bytes 1376264 | tf_op jit(solution)/shard_map/ppermute | solution.py:118
  504.6 91.6 %collective-permute-start.17 = (bf16[2,128,896]{2,1,0:T(8,128)(2,1)}, bf16[2,128,896]{2,1,0:T(8,128)(2,1)}, u32[]{:S(2)}, u32[]{:S(2)}) collective-permute-start(bf16[2,128,896]{2,1,0:T(8,128)(2,1)} %get-tuple-element.54), channel_id=1, source_target_pairs={{0,16},{8,24},{16,0},{24,8},{1,17},{9,25},{17,1},{25,9},{2,18},{10... | collective-permute-start | bytes 1376264 | tf_op jit(solution)/shard_map/ppermute | solution.py:118
  508.8 91.5 %collective-permute-start.16 = (bf16[2,128,896]{2,1,0:T(8,128)(2,1)}, bf16[2,128,896]{2,1,0:T(8,128)(2,1)}, u32[]{:S(2)}, u32[]{:S(2)}) collective-permute-start(bf16[2,128,896]{2,1,0:T(8,128)(2,1)} %get-tuple-element.55), channel_id=1, source_target_pairs={{0,24},{8,0},{16,8},{24,16},{1,25},{9,1},{17,9},{25,17},{2,26},{10... | collective-permute-start | bytes 1376264 | tf_op jit(solution)/shard_map/ppermute | solution.py:118
  544.1 62.2 %collective-permute-start.21 = (bf16[2,128,896]{2,1,0:T(8,128)(2,1)}, bf16[2,128,896]{2,1,0:T(8,128)(2,1)}, u32[]{:S(2)}, u32[]{:S(2)}) collective-permute-start(bf16[2,128,896]{2,1,0:T(8,128)(2,1)} %get-tuple-element.57), channel_id=1, source_target_pairs={{0,8},{8,16},{16,24},{24,0},{1,9},{9,17},{17,25},{25,1},{2,10},{10... | collective-permute-start | bytes 1376264 | tf_op jit(solution)/shard_map/ppermute | solution.py:118
  544.1 64.1 %collective-permute-start.20 = (bf16[2,128,896]{2,1,0:T(8,128)(2,1)}, bf16[2,128,896]{2,1,0:T(8,128)(2,1)}, u32[]{:S(2)}, u32[]{:S(2)}) collective-permute-start(bf16[2,128,896]{2,1,0:T(8,128)(2,1)} %get-tuple-element.58), channel_id=1, source_target_pairs={{0,16},{8,24},{16,0},{24,8},{1,17},{9,25},{17,1},{25,9},{2,18},{10... | collective-permute-start | bytes 1376264 | tf_op jit(solution)/shard_map/ppermute | solution.py:118
  545.5 64.7 %collective-permute-start.19 = (bf16[2,128,896]{2,1,0:T(8,128)(2,1)}, bf16[2,128,896]{2,1,0:T(8,128)(2,1)}, u32[]{:S(2)}, u32[]{:S(2)}) collective-permute-start(bf16[2,128,896]{2,1,0:T(8,128)(2,1)} %get-tuple-element.59), channel_id=1, source_target_pairs={{0,24},{8,0},{16,8},{24,16},{1,25},{9,1},{17,9},{25,17},{2,26},{10... | collective-permute-start | bytes 1376264 | tf_op jit(solution)/shard_map/ppermute | solution.py:118
  596.2 77.5 %collective-permute-start.13 = (bf16[2,63,2048]{2,1,0:T(8,128)(2,1)}, bf16[2,63,2048]{2,1,0:T(8,128)(2,1)}, u32[]{:S(2)}, u32[]{:S(2)}) collective-permute-start(bf16[2,63,2048]{2,1,0:T(8,128)(2,1)} %slice.358), channel_id=1, source_target_pairs={{0,1},{1,2},{2,3},{3,4},{4,5},{5,6},{6,7},{8,9},{9,10},{10,11},{11... | collective-permute-start | bytes 1548296 | tf_op jit(solution)/shard_map/ppermute | solution.py:16
  600.3 76.4 %collective-permute-start.15 = (bf16[2,63,2048]{2,1,0:T(8,128)(2,1)}, bf16[2,63,2048]{2,1,0:T(8,128)(2,1)}, u32[]{:S(2)}, u32[]{:S(2)}) collective-permute-start(bf16[2,63,2048]{2,1,0:T(8,128)(2,1)} %slice.364), channel_id=1, source_target_pairs={{0,1},{1,2},{2,3},{3,4},{4,5},{5,6},{6,7},{8,9},{9,10},{10,11},{11... | collective-permute-start | bytes 1548296 | tf_op jit(solution)/shard_map/ppermute | solution.py:16
  (104 other events, 801.9 us)
Sparse Core Ops, SparseCore 0:
  396.2 114.6 reduce-scatter.2
  615.3 41.2 reduce-scatter.4

commit v3 on v2

--- a/solution.py
+++ b/solution.py
@@ -8,6 +8,7 @@
 SPAN = 64
 NB_LEN = 128
 CHUNKS = 4
+LEAD = 2
 
 
 def shifted(array, axis, by):
@@ -87,7 +88,6 @@
     chunk_cap = min(chunk_blocks, capacity)
     chunk_slots = shard_count * chunk_cap
 
-    own = lax.axis_index("dp")
     target = neighbour_shard.reshape(chunk_count, chunk_refs)
     wanted = neighbour_row.reshape(chunk_count, chunk_refs)
     slot_indices = []
@@ -97,26 +97,16 @@
         owners = one_hot(target[g], shard_count)
         before = jnp.cumsum(owners, axis=0) - owners
         slot_rank = jnp.sum(before * owners, axis=1)
-        asked = one_hot(target[g] * chunk_cap + slot_rank, chunk_slots)
+        slot_index = target[g] * chunk_cap + slot_rank
+        placed = one_hot(slot_index, chunk_slots)
         requests.append(
-            jnp.sum(asked * wanted[g][:, None], axis=0).reshape(shard_count, 1, chunk_cap)
-        )
-        slot_index = ((own - target[g]) % shard_count) * chunk_cap + slot_rank
-        placed = one_hot(slot_index, chunk_slots)
+            jnp.sum(placed * wanted[g][:, None], axis=0).reshape(shard_count, 1, chunk_cap)
+        )
         ref_ids = jnp.arange(1, chunk_refs + 1, dtype=jnp.int32)
         slot_refs.append(jnp.sum(placed * ref_ids[:, None], axis=0))
         slot_indices.append(slot_index)
     request = jnp.concatenate(requests, axis=1)
     arrived = lax.all_to_all(request, "dp", split_axis=0, concat_axis=0, tiled=True)
-    offsets = jnp.arange(shard_count, dtype=jnp.int32)
-    sent_rows = jnp.take(arrived, (own + offsets) % shard_count, axis=0)
-
-    def exchange(parts, direction):
-        received = [parts[0]]
-        for k in range(1, shard_count):
-            pairs = [(i, (i + direction * k) % shard_count) for i in range(shard_count)]
-            received.append(lax.ppermute(parts[k], "dp", pairs))
-        return jnp.stack(received, axis=0)
 
     head_rows, head_grads = shifted((queries[:, :lag_rows], d_context[:, :lag_rows]), "seq", -1)
     query_blocks = jnp.concatenate([queries[:, lag_rows:], head_rows], axis=1).reshape(
@@ -130,13 +120,17 @@
     context_parts = []
     query_parts = []
     returned_parts = []
-    weight_terms = None
+    markers = []
+    seq_major = []
+    proj_parts = []
     for g in range(chunk_count):
-        outgoing = jnp.take(database, sent_rows[:, g, :].reshape(chunk_slots), axis=0)
-        incoming = exchange(outgoing.reshape(shard_count, chunk_cap, NB_LEN, ENC), 1)
-        neighbours = jnp.take(
-            incoming.reshape(chunk_slots, NB_LEN, ENC), slot_indices[g], axis=0
-        ).reshape(chunk_refs * NB_LEN, ENC)
+        outgoing = jnp.take(database, arrived[:, g, :].reshape(chunk_slots), axis=0)
+        if g >= LEAD:
+            outgoing, _ = lax.optimization_barrier((outgoing, markers[g - LEAD]))
+        incoming = lax.all_to_all(outgoing, "dp", split_axis=0, concat_axis=0, tiled=True)
+        neighbours = jnp.take(incoming, slot_indices[g], axis=0).reshape(
+            chunk_refs * NB_LEN, ENC
+        )
         blocks = slice(g * chunk_blocks, (g + 1) * chunk_blocks)
         context_shift, query_shift, proj_grads, near_grads = attend_chunk(
             query_blocks[blocks], grad_blocks[blocks], neighbours, key_weight, value_weight,
@@ -152,21 +146,33 @@
             axis=0,
         )
         slot_grads = jnp.take(padded, slot_refs[g], axis=0)
+        markers.append(slot_grads)
         returned_parts.append(
-            exchange(slot_grads.reshape(shard_count, chunk_cap, NB_LEN, ENC), -1)
-        )
-        seq_major = (
+            lax.all_to_all(slot_grads, "dp", split_axis=0, concat_axis=0, tiled=True)
+        )
+        seq_major.append(
             neighbours.reshape(chunk_refs * NB_LEN, shard_count, seq_total, enc_share)
             .transpose(0, 2, 1, 3)
             .reshape(chunk_refs * NB_LEN, ENC)
         )
-        term = jnp.einsum("px,pz->xz", seq_major, proj_grads, preferred_element_type=jnp.float32)
-        weight_terms = term if weight_terms is None else weight_terms + term
+        proj_parts.append(proj_grads)
+
+    def weight_term(first, last):
+        return jnp.einsum(
+            "px,pz->xz",
+            jnp.concatenate(seq_major[first:last], axis=0),
+            jnp.concatenate(proj_parts[first:last], axis=0),
+            preferred_element_type=jnp.float32,
+        )
+
+    weight_terms = weight_term(chunk_count - 1, chunk_count)
+    if chunk_count > 1:
+        weight_terms = weight_term(0, chunk_count - 1) + weight_terms
 
     returned = jnp.stack(
         [part.reshape(shard_count, chunk_cap, NB_LEN * ENC) for part in returned_parts], axis=1
     ).reshape(shard_count * chunk_count * chunk_cap, NB_LEN * ENC)
-    row_hits = one_hot(sent_rows.reshape(-1), database.shape[0]).astype(jnp.bfloat16)
+    row_hits = one_hot(arrived.reshape(-1), database.shape[0]).astype(jnp.bfloat16)
     database_grad = jnp.einsum(
         "sr,sx->rx", row_hits, returned, preferred_element_type=jnp.float32
     ).reshape(database.shape)

time: 697 us -> 654 us (0.938)
  the two profiles are of different devices: /device:TPU:24 before, /device:TPU:0 now
where the time goes in v3:
time: 654 us; the launch traced here: 647 us
  local copies, waits for them, and re-layouts  208 us (32%)
  matrix products  146 us (22%)
  waiting for transfers between devices  132 us (20%)
  other arithmetic  53.6 us (8%)
  starting transfers between devices  47 us (7%)
  blocking collectives  45.3 us (7%)
  between operations  15.7 us (2%)
    all_to_all x4, waiting for transfers between devices, local(): lax.all_to_all(outgoing, 'dp', split_axis=0, concat_axis=0, tiled=True)  82.5 us
    unnamed x188, local copies, waits for them, and re-layouts  63.5 us
    all_to_all x3, waiting for transfers between devices, local(): lax.all_to_all(slot_grads, 'dp', split_axis=0, concat_axis=0, tiled=True)  49.8 us
    all_to_all x1, blocking collectives, local(): lax.all_to_all(slot_grads, 'dp', split_axis=0, concat_axis=0, tiled=True)  45.3 us
    dot_general x4, matrix products, attend_chunk(): jnp.einsum('pz,xz->px', proj_grads, both_weights, preferred_element_type=...  32.9 us
    dot_general x2, matrix products, weight_term(): jnp.einsum('px,pz->xz', jnp.concatenate(seq_major[first:last], axis=0), j...  27.7 us
    dot_general x4, matrix products, attend_chunk(): jnp.dot(neighbours, key_weight, preferred_element_type=jnp.float32)  22.6 us
    all_to_all x4, starting transfers between devices, local(): lax.all_to_all(outgoing, 'dp', split_axis=0, concat_axis=0, tiled=True)  18.7 us
  transfers between devices with their start and end apart: 14, of which 6 were waited for; matrix products, arithmetic and copies ran while one was open for 35% of the time, Pallas kernels for 0%

profile of v3, /device:TPU:0, one launch (start us, length us, event | category | flops | bytes accessed | tf_op | source)
XLA Modules:
  0.0 647.2 jit_solution(10307557262078429412)
XLA Ops:
  13.3 6.3 all-to-all-start
  36.4 5.2 all-to-all-start.1
  47.4 5.1 gather_fusion.2
  52.5 5.1 gather_fusion.4
  66.2 19.1 %all-to-all-done.1 = bf16[8,128,896]{2,1,0:T(8,128)(2,1)} async-done(((bf16[8,128,896]{2,1,0:T(8,128)(2,1)}), bf16[8,128,896]{2,1,0:T(8,128)(2,1)}, u32[]{:S(2)}, u32[]{:S(2)}) %all-to-all-start.1) | async-done | bytes 1835040 | tf_op jit(solution)/shard_map/all_to_all | solution.py:130
  101.2 6.1 fusion.58
  110.9 22.1 %all-to-all-done.2 = bf16[8,128,896]{2,1,0:T(8,128)(2,1)} async-done(((bf16[8,128,896]{2,1,0:T(8,128)(2,1)}), bf16[8,128,896]{2,1,0:T(8,128)(2,1)}, u32[]{:S(2)}, u32[]{:S(2)}) %all-to-all-start.2) | async-done | bytes 1835040 | tf_op jit(solution)/shard_map/all_to_all | solution.py:130
  180.1 8.4 %convolution_convert_fusion.11 = bf16[512,896]{1,0:T(8,128)(2,1)S(1)} fusion(bf16[512,4096]{1,0:T(8,128)(2,1)S(1)} %bitcast_dynamic-update-slice_fusion.6, bf16[896,4096]{1,0:T(8,128)(2,1)} %constant_dynamic-update-slice_fusion), kind=kOutput, calls=%fused_computation.129 | convolution fusion | flops 3758555136 | bytes 12451840 | tf_op jit(solution)/shard_map/pz,xz->px/dot_general | solution.py:69
  204.1 8.4 %convolution_convert_fusion.10 = bf16[512,896]{1,0:T(8,128)(2,1)S(1)} fusion(bf16[512,4096]{1,0:T(8,128)(2,1)S(1)} %bitcast_dynamic-update-slice_fusion.4, bf16[896,4096]{1,0:T(8,128)(2,1)} %constant_dynamic-update-slice_fusion), kind=kOutput, calls=%fused_computation.128 | convolution fusion | flops 3758555136 | bytes 12451840 | tf_op jit(solution)/shard_map/pz,xz->px/dot_general | solution.py:69
  217.6 20.4 %all-to-all-done.3 = bf16[8,128,896]{2,1,0:T(8,128)(2,1)} async-done(((bf16[8,128,896]{2,1,0:T(8,128)(2,1)}), bf16[8,128,896]{2,1,0:T(8,128)(2,1)}, u32[]{:S(2)}, u32[]{:S(2)}) %all-to-all-start.3) | async-done | bytes 1835040 | tf_op jit(solution)/shard_map/all_to_all | solution.py:130
  254.0 5.9 fusion.62
  263.6 21.0 %all-to-all-done.4 = bf16[8,128,896]{2,1,0:T(8,128)(2,1)} async-done(((bf16[8,128,896]{2,1,0:T(8,128)(2,1)}), bf16[8,128,896]{2,1,0:T(8,128)(2,1)}, u32[]{:S(2)}, u32[]{:S(2)}) %all-to-all-start.4) | async-done | bytes 1835040 | tf_op jit(solution)/shard_map/all_to_all | solution.py:130
  288.0 5.8 fusion.64
  362.1 7.6 %fusion.158 = f32[896,4096]{1,0:T(8,128)} fusion(bf16[512,896]{0,1:T(8,128)(2,1)S(1)} %copy-done.70, bf16[512,4096]{1,0:T(8,128)(2,1)S(1)} %copy-done.65), kind=kOutput, calls=%fused_computation.256 | convolution fusion | flops 3758096384 | bytes 19791872 | tf_op jit(solution)/shard_map/px,pz->xz/dot_general | solution.py:161
  369.7 20.1 %fusion.9 = f32[896,4096]{1,0:T(8,128)} fusion(f32[896,4096]{1,0:T(8,128)} %fusion.158, bf16[512,4096]{1,0:T(8,128)(2,1)} %bitcast_dynamic-update-slice_fusion.2, bf16[512,4096]{1,0:T(8,128)(2,1)} %copy-done.67, bf16[512,4096]{1,0:T(8,128)(2,1)} %copy-done.66, bf16[512,896]{0,1:T(8,128)(2,1)S(1)} %copy-done.71, bf16[512,896]{0,1:T(8,128)(2,1)S(1)} %copy-done.68, ...), kind=kOutput, calls=%fused_computation.22 | convolution fusion | flops 11323965440 | bytes 44695552 | tf_op jit(solution)/shard_map/px,pz->xz/dot_general | solution.py:161
  391.3 45.3 %all_to_all.45 = bf16[8,128,896]{2,1,0:T(8,128)(2,1)} all-to-all(bf16[8,128,896]{2,1,0:T(8,128)(2,1)S(1)} %copy-done.30), channel_id=1, replica_groups=mesh['dp'=4,'seq'=8] {'dp'}, dimensions={0} | all-to-all | bytes 3670016 | tf_op jit(solution)/shard_map/all_to_all | solution.py:151
  442.3 9.3 %convolution_convert_fusion.8 = bf16[512,896]{1,0:T(8,128)(2,1)S(1)} fusion(bf16[512,4096]{1,0:T(8,128)(2,1)} %bitcast_dynamic-update-slice_fusion, bf16[896,4096]{1,0:T(8,128)(2,1)} %constant_dynamic-update-slice_fusion), kind=kOutput, calls=%fused_computation.126 | convolution fusion | flops 3758555136 | bytes 12451840 | tf_op jit(solution)/shard_map/pz,xz->px/dot_general | solution.py:69
  457.1 25.8 %all-to-all-done.5 = bf16[8,128,896]{2,1,0:T(8,128)(2,1)} async-done(((bf16[8,128,896]{2,1,0:T(8,128)(2,1)}), bf16[8,128,896]{2,1,0:T(8,128)(2,1)}, u32[]{:S(2)}, u32[]{:S(2)}) %all-to-all-start.5) | async-done | bytes 1835040 | tf_op jit(solution)/shard_map/all_to_all | solution.py:151
  496.3 6.7 %convolution_convert_fusion.9 = bf16[512,896]{1,0:T(8,128)(2,1)S(1)} fusion(bf16[512,4096]{1,0:T(8,128)(2,1)} %bitcast_dynamic-update-slice_fusion.2, bf16[896,4096]{1,0:T(8,128)(2,1)S(1)} %bitcast.223), kind=kOutput, calls=%fused_computation.127 | convolution fusion | flops 3758555136 | bytes 12451840 | tf_op jit(solution)/shard_map/pz,xz->px/dot_general | solution.py:69
  505.6 24.0 %all-to-all-done.8 = bf16[8,128,896]{2,1,0:T(8,128)(2,1)} async-done(((bf16[8,128,896]{2,1,0:T(8,128)(2,1)}), bf16[8,128,896]{2,1,0:T(8,128)(2,1)}, u32[]{:S(2)}, u32[]{:S(2)}) %all-to-all-start.8) | async-done | bytes 1835040 | tf_op jit(solution)/shard_map/all_to_all | solution.py:151
  585.3 15.4 %pad_maximum_fusion = bf16[4,4,2,114688]{3,2,1,0:T(2,128)(2,1)} fusion(bf16[4,1,2,114688]{3,2,1,0:T(2,128)(2,1)} %stack_reshape.15, bf16[4,1,2,114688]{3,2,1,0:T(2,128)(2,1)} %stack_reshape.14, bf16[4,1,2,114688]{3,2,1,0:T(2,128)(2,1)S(1)} %stack_reshape.13, bf16[4,1,2,114688]{3,2,1,0:T(2,128)(2,1)} %stack_reshape.12), kind=kLoop, calls=%fused_computation.21 | loop fusion | flops 11010048 | bytes 14680064 | tf_op jit(solution)/shard_map/stack | solution.py:172
  600.7 7.9 %reshape.254 = bf16[32,114688]{1,0:T(8,128)(2,1)} reshape(bf16[4,4,2,114688]{3,2,1,0:T(2,128)(2,1)} %pad_maximum_fusion) | data formatting | bytes 14680064 | tf_op jit(solution)/shard_map/reshape | solution.py:174
  608.7 10.4 %fusion.6 = f32[32,128,896]{2,0,1:T(8,128)} fusion(bf16[4,128,8,896]{3,2,1,0:T(8,128)(2,1)} %bitcast.180, s32[32]{0:T(128)S(1)} %eq.143), kind=kOutput, calls=%fused_computation.18 | convolution fusion | flops 234884096 | bytes 22020224 | tf_op jit(solution)/shard_map/sr,sx->rx/dot_general | solution.py:176
  619.0 19.2 %copy.198 = f32[32,128,896]{2,1,0:T(8,128)} copy(f32[32,128,896]{2,0,1:T(8,128)} %fusion.6) | data formatting | bytes 29360128
  (405 shorter events, 300.9 us)
Async XLA Ops:
  13.3 17.1 %all-to-all-start = ((s32[4,4,2]{1,2,0:T(2,128)}), s32[4,4,2]{1,2,0:T(2,128)S(1)}, u32[]{:S(2)}, u32[]{:S(2)}) async-start(s32[4,4,2]{1,2,0:T(2,128)} %copy.153), calls=%async_computation | async-start | bytes 8192 | tf_op jit(solution)/shard_map/all_to_all | solution.py:109
  21.5 72.4 %collective-permute-start.1 = (bf16[2,63,2048]{2,1,0:T(8,128)(2,1)}, bf16[2,63,2048]{2,1,0:T(8,128)(2,1)}, u32[]{:S(2)}, u32[]{:S(2)}) collective-permute-start(bf16[2,63,2048]{2,1,0:T(8,128)(2,1)} %slice.118), channel_id=1, source_target_pairs={{1,0},{2,1},{3,2},{4,3},{5,4},{6,5},{7,6},{9,8},{10,9},{11,10},{12... | collective-permute-start | bytes 1548296 | tf_op jit(solution)/shard_map/ppermute | solution.py:17
  24.7 66.7 %collective-permute-start = (bf16[2,63,2048]{2,1,0:T(8,128)(2,1)}, bf16[2,63,2048]{2,1,0:T(8,128)(2,1)}, u32[]{:S(2)}, u32[]{:S(2)}) collective-permute-start(bf16[2,63,2048]{2,1,0:T(8,128)(2,1)} %slice.112), channel_id=1, source_target_pairs={{1,0},{2,1},{3,2},{4,3},{5,4},{6,5},{7,6},{9,8},{10,9},{11,10},{12... | collective-permute-start | bytes 1548296 | tf_op jit(solution)/shard_map/ppermute | solution.py:17
  36.4 48.9 %all-to-all-start.1 = ((bf16[8,128,896]{2,1,0:T(8,128)(2,1)}), bf16[8,128,896]{2,1,0:T(8,128)(2,1)}, u32[]{:S(2)}, u32[]{:S(2)}) async-start(bf16[8,128,896]{2,1,0:T(8,128)(2,1)} %broadcast_select_fusion.7), calls=%async_computation.1 | async-start | bytes 3670016 | tf_op jit(solution)/shard_map/all_to_all | solution.py:130
  85.3 47.7 %all-to-all-start.2 = ((bf16[8,128,896]{2,1,0:T(8,128)(2,1)}), bf16[8,128,896]{2,1,0:T(8,128)(2,1)}, u32[]{:S(2)}, u32[]{:S(2)}) async-start(bf16[8,128,896]{2,1,0:T(8,128)(2,1)} %broadcast_select_fusion.6), calls=%async_computation.2 | async-start | bytes 3670016 | tf_op jit(solution)/shard_map/all_to_all | solution.py:130
  97.2 50.3 %copy-start.37 = (bf16[2,64,16,128]{3,2,1,0:T(8,128)(2,1)}, bf16[2,64,16,128]{3,2,1,0:T(8,128)(2,1)S(1)}, u32[]{:S(2)}) copy-start(bf16[2,64,16,128]{3,2,1,0:T(8,128)(2,1)S(1)} %get-tuple-element.57) | copy-start | bytes 1572868
  144.2 14.8 %copy-start = (bf16[64,8,16,128]{3,2,1,0:T(8,128)(2,1)}, bf16[64,8,16,128]{3,2,1,0:T(8,128)(2,1)S(1)}, u32[]{:S(2)}) copy-start(bf16[64,8,16,128]{3,2,1,0:T(8,128)(2,1)S(1)} %copy.209) | copy-start | bytes 6291460
  160.1 10.3 %copy-start.79 = (f32[2,16,64]{2,1,0:T(8,128)}, f32[2,16,64]{2,1,0:T(8,128)S(1)}, u32[]{:S(2)}) copy-start(f32[2,16,64]{2,1,0:T(8,128)S(1)} %get-tuple-element.76) | copy-start | bytes 24580
  190.9 47.1 %all-to-all-start.3 = ((bf16[8,128,896]{2,1,0:T(8,128)(2,1)}), bf16[8,128,896]{2,1,0:T(8,128)(2,1)}, u32[]{:S(2)}, u32[]{:S(2)}) async-start(bf16[8,128,896]{2,1,0:T(8,128)(2,1)} %broadcast_select_fusion.5), calls=%async_computation.3 | async-start | bytes 3670016 | tf_op jit(solution)/shard_map/all_to_all | solution.py:130
  217.6 24.9 %copy-start.47 = (bf16[4,128,896]{2,1,0:T(8,128)(2,1)S(1)}, bf16[4,128,896]{2,1,0:T(8,128)(2,1)}, u32[]{:S(2)}) copy-start(bf16[4,128,896]{2,1,0:T(8,128)(2,1)} %copy-done.46) | copy-start | bytes 2752516
  217.6 26.5 %copy-start.45 = (bf16[4,128,896]{2,1,0:T(8,128)(2,1)S(1)}, bf16[4,128,896]{2,1,0:T(8,128)(2,1)}, u32[]{:S(2)}) copy-start(bf16[4,128,896]{2,1,0:T(8,128)(2,1)} %copy-done.44) | copy-start | bytes 2752516
  238.0 46.6 %all-to-all-start.4 = ((bf16[8,128,896]{2,1,0:T(8,128)(2,1)}), bf16[8,128,896]{2,1,0:T(8,128)(2,1)}, u32[]{:S(2)}, u32[]{:S(2)}) async-start(bf16[8,128,896]{2,1,0:T(8,128)(2,1)} %broadcast_select_fusion.3), calls=%async_computation.4 | async-start | bytes 3670016 | tf_op jit(solution)/shard_map/all_to_all | solution.py:130
  242.4 339.9 %reduce-scatter.3.cloned.1.call-start = ((), (), s32[]{:S(2)}) async-start(), calls=%async_computation.11 | async-start | bytes 16515072 | tf_op jit(solution)/shard_map/reduce_scatter | solution.py:189
  304.8 30.3 %copy-start.4 = (bf16[64,8,16,128]{3,2,1,0:T(8,128)(2,1)}, bf16[64,8,16,128]{3,2,1,0:T(8,128)(2,1)S(1)}, u32[]{:S(2)}) copy-start(bf16[64,8,16,128]{3,2,1,0:T(8,128)(2,1)S(1)} %copy.216) | copy-start | bytes 6291460
  436.6 46.2 %all-to-all-start.5 = ((bf16[8,128,896]{2,1,0:T(8,128)(2,1)}), bf16[8,128,896]{2,1,0:T(8,128)(2,1)}, u32[]{:S(2)}, u32[]{:S(2)}) async-start(bf16[8,128,896]{2,1,0:T(8,128)(2,1)} %broadcast_select_fusion.4), calls=%async_computation.5 | async-start | bytes 3670016 | tf_op jit(solution)/shard_map/all_to_all | solution.py:151
  457.1 30.4 %copy-start.3 = (bf16[64,8,16,128]{3,2,1,0:T(8,128)(2,1)S(1)}, bf16[64,8,16,128]{3,2,1,0:T(8,128)(2,1)}, u32[]{:S(2)}) copy-start(bf16[64,8,16,128]{3,2,1,0:T(8,128)(2,1)} %copy-done.2) | copy-start | bytes 6291460
  482.9 46.7 %all-to-all-start.8 = ((bf16[8,128,896]{2,1,0:T(8,128)(2,1)}), bf16[8,128,896]{2,1,0:T(8,128)(2,1)}, u32[]{:S(2)}, u32[]{:S(2)}) async-start(bf16[8,128,896]{2,1,0:T(8,128)(2,1)} %broadcast_select_fusion), calls=%async_computation.8 | async-start | bytes 3670016 | tf_op jit(solution)/shard_map/all_to_all | solution.py:151
  505.6 28.4 %copy-start.22 = (f32[2,16,64,256]{3,2,1,0:T(8,128)S(1)}, f32[2,16,64,256]{3,2,1,0:T(8,128)}, u32[]{:S(2)}) copy-start(f32[2,16,64,256]{3,2,1,0:T(8,128)} %copy-done.21) | copy-start | bytes 6291460
  529.6 48.8 %all-to-all-start.7 = ((bf16[8,128,896]{2,1,0:T(8,128)(2,1)}), bf16[8,128,896]{2,1,0:T(8,128)(2,1)}, u32[]{:S(2)}, u32[]{:S(2)}) async-start(bf16[8,128,896]{2,1,0:T(8,128)(2,1)} %broadcast_select_fusion.1), calls=%async_computation.7 | async-start | bytes 3670016 | tf_op jit(solution)/shard_map/all_to_all | solution.py:151
  534.0 104.3 %reduce-scatter.5.cloned.1.call-start = ((), (), s32[]{:S(2)}) async-start(), calls=%async_computation.12 | async-start | bytes 2621440 | tf_op jit(solution)/shard_map/reduce_scatter | solution.py:195
  540.9 8.7 %copy-start.7 = (bf16[64,8,16,128]{3,2,1,0:T(8,128)(2,1)S(1)}, bf16[64,8,16,128]{3,2,1,0:T(8,128)(2,1)}, u32[]{:S(2)}) copy-start(bf16[64,8,16,128]{3,2,1,0:T(8,128)(2,1)} %copy-done.6) | copy-start | bytes 6291460
  540.9 8.7 %copy-start.11 = (bf16[2,16,64,256]{3,2,1,0:T(8,128)(2,1)S(1)}, bf16[2,16,64,256]{3,2,1,0:T(8,128)(2,1)}, u32[]{:S(2)}) copy-start(bf16[2,16,64,256]{3,2,1,0:T(8,128)(2,1)} %copy-done.10) | copy-start | bytes 3145732
  547.4 21.4 %collective-permute-start.2 = (bf16[2,63,2048]{2,1,0:T(8,128)(2,1)}, bf16[2,63,2048]{2,1,0:T(8,128)(2,1)}, u32[]{:S(2)}, u32[]{:S(2)}) collective-permute-start(bf16[2,63,2048]{2,1,0:T(8,128)(2,1)} %slice.166), channel_id=1, source_target_pairs={{0,1},{1,2},{2,3},{3,4},{4,5},{5,6},{6,7},{8,9},{9,10},{10,11},{11... | collective-permute-start | bytes 1548296 | tf_op jit(solution)/shard_map/ppermute | solution.py:17
  558.6 13.1 %collective-permute-start.3 = (bf16[2,63,2048]{2,1,0:T(8,128)(2,1)}, bf16[2,63,2048]{2,1,0:T(8,128)(2,1)}, u32[]{:S(2)}, u32[]{:S(2)}) collective-permute-start(bf16[2,63,2048]{2,1,0:T(8,128)(2,1)} %slice.170), channel_id=1, source_target_pairs={{0,1},{1,2},{2,3},{3,4},{4,5},{5,6},{6,7},{8,9},{9,10},{10,11},{11... | collective-permute-start | bytes 1548296 | tf_op jit(solution)/shard_map/ppermute | solution.py:17
  (78 other events, 251.8 us)
Sparse Core Ops, SparseCore 0:
  390.0 103.7 reduce-scatter.2
  585.4 45.2 reduce-scatter.4

commit v4 on v3

--- a/solution.py
+++ b/solution.py
@@ -119,7 +119,7 @@
     enc_share = ENC // (shard_count * seq_total)
     context_parts = []
     query_parts = []
-    returned_parts = []
+    database_grad = None
     markers = []
     seq_major = []
     proj_parts = []
@@ -146,10 +146,16 @@
             axis=0,
         )
         slot_grads = jnp.take(padded, slot_refs[g], axis=0)
-        markers.append(slot_grads)
-        returned_parts.append(
-            lax.all_to_all(slot_grads, "dp", split_axis=0, concat_axis=0, tiled=True)
-        )
+        returned = lax.all_to_all(slot_grads, "dp", split_axis=0, concat_axis=0, tiled=True)
+        markers.append(returned)
+        row_hits = one_hot(arrived[:, g, :].reshape(chunk_slots), database.shape[0])
+        part = jnp.einsum(
+            "sr,sax->rax",
+            row_hits.astype(jnp.bfloat16),
+            returned,
+            preferred_element_type=jnp.float32,
+        )
+        database_grad = part if database_grad is None else database_grad + part
         seq_major.append(
             neighbours.reshape(chunk_refs * NB_LEN, shard_count, seq_total, enc_share)
             .transpose(0, 2, 1, 3)
@@ -169,13 +175,6 @@
     if chunk_count > 1:
         weight_terms = weight_term(0, chunk_count - 1) + weight_terms
 
-    returned = jnp.stack(
-        [part.reshape(shard_count, chunk_cap, NB_LEN * ENC) for part in returned_parts], axis=1
-    ).reshape(shard_count * chunk_count * chunk_cap, NB_LEN * ENC)
-    row_hits = one_hot(arrived.reshape(-1), database.shape[0]).astype(jnp.bfloat16)
-    database_grad = jnp.einsum(
-        "sr,sx->rx", row_hits, returned, preferred_element_type=jnp.float32
-    ).reshape(database.shape)
 
     context_shift = jnp.concatenate(context_parts, axis=0).reshape(seq_count, seq_span, feat_width)
     query_shift = jnp.concatenate(query_parts, axis=0).reshape(seq_count, seq_span, feat_width)

time: 654 us -> 662 us (1.012)
  waiting for transfers between devices: 132 us -> 181 us
  blocking collectives: 45.3 us -> 0 us
  matrix products: 146 us -> 180 us
  local copies, waits for them, and re-layouts: 208 us -> 189 us
  other arithmetic: 53.6 us -> 44.7 us
    all_to_all x1 -> x0, blocking collectives: 45.3 us -> none  [local(): lax.all_to_all(slot_grads, 'dp', split_axis=0, concat_axis=0, tiled=True)]
    dot_general x1 -> x4, matrix products: 10.4 us -> 47.1 us  [local(): jnp.einsum('sr,sax->rax', row_hits.astype(jnp.bfloat16), returned, prefer...]
    all_to_all x4, waiting for transfers between devices: 82.5 us -> 107 us  [local(): lax.all_to_all(outgoing, 'dp', split_axis=0, concat_axis=0, tiled=True)]
    all_to_all x3 -> x4, waiting for transfers between devices: 49.8 us -> 69.6 us  [local(): lax.all_to_all(slot_grads, 'dp', split_axis=0, concat_axis=0, tiled=True)]
    another operation x1 -> x0, other arithmetic: 15.4 us -> none  [local(): jnp.stack([part.reshape(shard_count, chunk_cap, NB_LEN * ENC) for part in...]
    another operation x4 -> x0, local copies, waits for them, and re-layouts: 14.2 us -> none  [local(): jnp.stack([part.reshape(shard_count, chunk_cap, NB_LEN * ENC) for part in...]
    reshape x1 -> x0, local copies, waits for them, and re-layouts: 7.93 us -> none  [local(): returned = jnp.stack([part.reshape(shard_count, chunk_cap, NB_LEN * ENC)...]
    unnamed x188 -> x206, local copies, waits for them, and re-layouts: 63.5 us -> 67.6 us
  transfers between devices with their start and end apart: 14 -> 15, of which waited for: 6 -> 9; matrix products, arithmetic and copies ran while one was open for 35% -> 34% of each run, Pallas kernels for 0% -> 0%
where the time goes in v4:
time: 662 us; the launch traced here: 656 us
  local copies, waits for them, and re-layouts  189 us (29%)
  waiting for transfers between devices  181 us (27%)
  matrix products  180 us (27%)
  starting transfers between devices  46.6 us (7%)
  other arithmetic  44.7 us (7%)
  between operations  15.9 us (2%)
    all_to_all x4, waiting for transfers between devices, local(): lax.all_to_all(outgoing, 'dp', split_axis=0, concat_axis=0, tiled=True)  107 us
    all_to_all x4, waiting for transfers between devices, local(): lax.all_to_all(slot_grads, 'dp', split_axis=0, concat_axis=0, tiled=True)  69.6 us
    unnamed x206, local copies, waits for them, and re-layouts  67.6 us
    dot_general x4, matrix products, local(): jnp.einsum('sr,sax->rax', row_hits.astype(jnp.bfloat16), returned, prefer...  47.1 us
    dot_general x4, matrix products, attend_chunk(): jnp.einsum('pz,xz->px', proj_grads, both_weights, preferred_element_type=...  28.2 us
    dot_general x2, matrix products, weight_term(): jnp.einsum('px,pz->xz', jnp.concatenate(seq_major[first:last], axis=0), j...  27.3 us
    dot_general x4, matrix products, attend_chunk(): jnp.dot(neighbours, key_weight, preferred_element_type=jnp.float32)  22.6 us
    convert_element_type x4, local copies, waits for them, and re-layouts, attend_chunk(): value_grads = jnp.einsum('chqk,cqhd->ckhd', weight_half, grad_blocks, pre...  18.4 us
  transfers between devices with their start and end apart: 15, of which 9 were waited for; matrix products, arithmetic and copies ran while one was open for 34% of the time, Pallas kernels for 0%

profile of v4, /device:TPU:0, one launch (start us, length us, event | category | flops | bytes accessed | tf_op | source)
XLA Modules:
  0.0 656.1 jit_solution(12695978259059909779)
XLA Ops:
  13.3 6.3 all-to-all-start
  48.2 31.5 %all-to-all-done.1 = bf16[8,128,896]{2,1,0:T(8,128)(2,1)} async-done(((bf16[8,128,896]{2,1,0:T(8,128)(2,1)}), bf16[8,128,896]{2,1,0:T(8,128)(2,1)}, u32[]{:S(2)}, u32[]{:S(2)}) %all-to-all-start.1) | async-done | bytes 1835040 | tf_op jit(solution)/shard_map/all_to_all | solution.py:130
  96.5 6.1 fusion.62
  106.3 20.1 %all-to-all-done.2 = bf16[8,128,896]{2,1,0:T(8,128)(2,1)S(1)} async-done(((bf16[8,128,896]{2,1,0:T(8,128)(2,1)}), bf16[8,128,896]{2,1,0:T(8,128)(2,1)S(1)}, u32[]{:S(2)}, u32[]{:S(2)}) %all-to-all-start.2) | async-done | bytes 1835040 | tf_op jit(solution)/shard_map/all_to_all | solution.py:130
  173.0 8.4 %convolution_convert_fusion.11 = bf16[512,896]{1,0:T(8,128)(2,1)S(1)} fusion(bf16[512,4096]{1,0:T(8,128)(2,1)S(1)} %bitcast_dynamic-update-slice_fusion.6, bf16[896,4096]{1,0:T(8,128)(2,1)} %copy-done.65), kind=kOutput, calls=%fused_computation.133 | convolution fusion | flops 3758555136 | bytes 12451840 | tf_op jit(solution)/shard_map/pz,xz->px/dot_general | solution.py:69
  200.7 8.4 %convolution_convert_fusion.10 = bf16[512,896]{1,0:T(8,128)(2,1)S(1)} fusion(bf16[512,4096]{1,0:T(8,128)(2,1)S(1)} %bitcast_dynamic-update-slice_fusion.4, bf16[896,4096]{1,0:T(8,128)(2,1)} %copy-done.65), kind=kOutput, calls=%fused_computation.132 | convolution fusion | flops 3758555136 | bytes 12451840 | tf_op jit(solution)/shard_map/pz,xz->px/dot_general | solution.py:69
  214.1 19.3 %all-to-all-done.3 = bf16[8,128,896]{2,1,0:T(8,128)(2,1)} async-done(((bf16[8,128,896]{2,1,0:T(8,128)(2,1)}), bf16[8,128,896]{2,1,0:T(8,128)(2,1)}, u32[]{:S(2)}, u32[]{:S(2)}) %all-to-all-start.3) | async-done | bytes 1835040 | tf_op jit(solution)/shard_map/all_to_all | solution.py:149
  237.1 5.1 gather_fusion.4
  245.2 33.9 %all-to-all-done.5 = bf16[8,128,896]{2,1,0:T(8,128)(2,1)S(1)} async-done(((bf16[8,128,896]{2,1,0:T(8,128)(2,1)}), bf16[8,128,896]{2,1,0:T(8,128)(2,1)S(1)}, u32[]{:S(2)}, u32[]{:S(2)}) %all-to-all-start.5) | async-done | bytes 1835040 | tf_op jit(solution)/shard_map/all_to_all | solution.py:149
  283.6 5.1 gather_fusion.7
  291.7 34.0 %all-to-all-done.4 = bf16[8,128,896]{2,1,0:T(8,128)(2,1)} async-done(((bf16[8,128,896]{2,1,0:T(8,128)(2,1)}), bf16[8,128,896]{2,1,0:T(8,128)(2,1)}, u32[]{:S(2)}, u32[]{:S(2)}) %all-to-all-start.4) | async-done | bytes 1835040 | tf_op jit(solution)/shard_map/all_to_all | solution.py:130
  341.6 5.9 fusion.66
  351.1 21.0 %all-to-all-done.6 = bf16[8,128,896]{2,1,0:T(8,128)(2,1)} async-done(((bf16[8,128,896]{2,1,0:T(8,128)(2,1)}), bf16[8,128,896]{2,1,0:T(8,128)(2,1)}, u32[]{:S(2)}, u32[]{:S(2)}) %all-to-all-start.6) | async-done | bytes 1835040 | tf_op jit(solution)/shard_map/all_to_all | solution.py:130
  375.6 5.8 fusion.68
  448.1 7.5 %fusion.171 = f32[896,4096]{1,0:T(8,128)} fusion(bf16[512,896]{0,1:T(8,128)(2,1)S(1)} %copy-done.73, bf16[512,4096]{1,0:T(8,128)(2,1)S(1)} %copy-done.66), kind=kOutput, calls=%fused_computation.272 | convolution fusion | flops 3758096384 | bytes 19791872 | tf_op jit(solution)/shard_map/px,pz->xz/dot_general | solution.py:167
  455.6 19.7 %fusion.6 = f32[896,4096]{1,0:T(8,128)} fusion(f32[896,4096]{1,0:T(8,128)} %fusion.171, bf16[512,4096]{1,0:T(8,128)(2,1)S(1)} %bitcast_dynamic-update-slice_fusion.2, bf16[512,4096]{1,0:T(8,128)(2,1)} %copy-done.71, bf16[512,4096]{1,0:T(8,128)(2,1)} %copy-done.70, bf16[512,896]{0,1:T(8,128)(2,1)} %reshape.254, bf16[512,896]{0,1:T(8,128)(2,1)S(1)} %copy-done.72, ...), kind=kOutput, calls=%fused_computation.19 | convolution fusion | flops 11323965440 | bytes 44695552 | tf_op jit(solution)/shard_map/px,pz->xz/dot_general | solution.py:167
  503.8 9.0 %fusion.59 = f32[32,128,896]{2,0,1:T(8,128)} fusion(bf16[8,128,896]{2,1,0:T(8,128)(2,1)} %all-to-all-done.3, s32[8]{0:T(128)S(1)} %copy-done.86), kind=kOutput, calls=%fused_computation.112 | convolution fusion | flops 58721024 | bytes 16515104 | tf_op jit(solution)/shard_map/sr,sax->rax/dot_general | solution.py:152
  512.8 6.9 %convolution_convert_fusion.8 = bf16[512,896]{1,0:T(8,128)(2,1)S(1)} fusion(bf16[512,4096]{1,0:T(8,128)(2,1)S(1)} %copy-done.67, bf16[896,4096]{1,0:T(8,128)(2,1)} %copy-done.65), kind=kOutput, calls=%fused_computation.130 | convolution fusion | flops 3758555136 | bytes 12451840 | tf_op jit(solution)/shard_map/pz,xz->px/dot_general | solution.py:69
  529.8 16.4 %all-to-all-done.7 = bf16[8,128,896]{2,1,0:T(8,128)(2,1)S(1)} async-done(((bf16[8,128,896]{2,1,0:T(8,128)(2,1)}), bf16[8,128,896]{2,1,0:T(8,128)(2,1)S(1)}, u32[]{:S(2)}, u32[]{:S(2)}) %all-to-all-start.7) | async-done | bytes 1835040 | tf_op jit(solution)/shard_map/all_to_all | solution.py:149
  554.8 5.0 reshape.244
  582.4 8.9 %fusion.57 = f32[32,128,896]{2,0,1:T(8,128)} fusion(bf16[8,128,896]{2,1,0:T(8,128)(2,1)} %copy-done.29, s32[8]{0:T(128)S(1)} %copy-done.84), kind=kOutput, calls=%fused_computation.110 | convolution fusion | flops 58721024 | bytes 16515104 | tf_op jit(solution)/shard_map/sr,sax->rax/dot_general | solution.py:152
  598.6 7.0 %fusion.55 = f32[32,128,896]{2,0,1:T(8,128)} fusion(bf16[8,128,896]{2,1,0:T(8,128)(2,1)S(1)} %copy-done.31, s32[8]{0:T(128)S(1)} %copy-done.88), kind=kOutput, calls=%fused_computation.108 | convolution fusion | flops 58721024 | bytes 16515104 | tf_op jit(solution)/shard_map/sr,sax->rax/dot_general | solution.py:152
  605.6 22.2 %add_add_fusion = f32[32,128,896]{2,0,1:T(8,128)} fusion(f32[32,128,896]{2,0,1:T(8,128)} %fusion.55, f32[32,128,896]{2,0,1:T(8,128)} %fusion.59, f32[32,128,896]{2,0,1:T(8,128)} %fusion.57, bf16[8,128,896]{2,1,0:T(8,128)(2,1)} %all-to-all-done.8, s32[8]{0:T(128)S(1)} %copy-done.82), kind=kOutput, calls=%fused_computation.12 | convolution fusion | flops 69731072 | bytes 60555296 | tf_op jit(solution)/shard_map/sr,sax->rax/dot_general | solution.py:152
  627.8 19.1 %copy.203 = f32[32,128,896]{2,1,0:T(8,128)} copy(f32[32,128,896]{2,0,1:T(8,128)} %add_add_fusion) | data formatting | bytes 29360128
  (419 shorter events, 307.6 us)
Async XLA Ops:
  13.3 11.9 %all-to-all-start = ((s32[4,4,2]{1,2,0:T(2,128)}), s32[4,4,2]{1,2,0:T(2,128)S(1)}, u32[]{:S(2)}, u32[]{:S(2)}) async-start(s32[4,4,2]{1,2,0:T(2,128)} %copy.156), calls=%async_computation | async-start | bytes 8192 | tf_op jit(solution)/shard_map/all_to_all | solution.py:109
  20.7 67.4 %collective-permute-start.1 = (bf16[2,63,2048]{2,1,0:T(8,128)(2,1)S(1)}, bf16[2,63,2048]{2,1,0:T(8,128)(2,1)S(1)}, u32[]{:S(2)}, u32[]{:S(2)}) collective-permute-start(bf16[2,63,2048]{2,1,0:T(8,128)(2,1)S(1)} %slice.122), channel_id=1, source_target_pairs={{1,0},{2,1},{3,2},{4,3},{5,4},{6,5},{7,6},{9,8},{10,9},{11,10},{12... | collective-permute-start | bytes 1548296 | tf_op jit(solution)/shard_map/ppermute | solution.py:17
  23.1 63.0 %collective-permute-start = (bf16[2,63,2048]{2,1,0:T(8,128)(2,1)S(1)}, bf16[2,63,2048]{2,1,0:T(8,128)(2,1)}, u32[]{:S(2)}, u32[]{:S(2)}) collective-permute-start(bf16[2,63,2048]{2,1,0:T(8,128)(2,1)S(1)} %slice.116), channel_id=1, source_target_pairs={{1,0},{2,1},{3,2},{4,3},{5,4},{6,5},{7,6},{9,8},{10,9},{11,10},{12... | collective-permute-start | bytes 1548296 | tf_op jit(solution)/shard_map/ppermute | solution.py:17
  31.6 48.1 %all-to-all-start.1 = ((bf16[8,128,896]{2,1,0:T(8,128)(2,1)}), bf16[8,128,896]{2,1,0:T(8,128)(2,1)}, u32[]{:S(2)}, u32[]{:S(2)}) async-start(bf16[8,128,896]{2,1,0:T(8,128)(2,1)} %broadcast_select_fusion.7), calls=%async_computation.1 | async-start | bytes 3670016 | tf_op jit(solution)/shard_map/all_to_all | solution.py:130
  79.7 46.8 %all-to-all-start.2 = ((bf16[8,128,896]{2,1,0:T(8,128)(2,1)}), bf16[8,128,896]{2,1,0:T(8,128)(2,1)S(1)}, u32[]{:S(2)}, u32[]{:S(2)}) async-start(bf16[8,128,896]{2,1,0:T(8,128)(2,1)} %broadcast_select_fusion.6), calls=%async_computation.2 | async-start | bytes 3670016 | tf_op jit(solution)/shard_map/all_to_all | solution.py:130
  90.4 50.9 %copy-start.36 = (bf16[2,64,16,128]{3,2,1,0:T(8,128)(2,1)}, bf16[2,64,16,128]{3,2,1,0:T(8,128)(2,1)S(1)}, u32[]{:S(2)}) copy-start(bf16[2,64,16,128]{3,2,1,0:T(8,128)(2,1)S(1)} %get-tuple-element.57) | copy-start | bytes 1572868
  90.4 62.5 %copy-start.38 = (bf16[2,64,16,128]{3,2,1,0:T(8,128)(2,1)}, bf16[2,64,16,128]{3,2,1,0:T(8,128)(2,1)S(1)}, u32[]{:S(2)}) copy-start(bf16[2,64,16,128]{3,2,1,0:T(8,128)(2,1)S(1)} %get-tuple-element.58) | copy-start | bytes 1572868
  138.2 14.8 %copy-start = (bf16[64,8,16,128]{3,2,1,0:T(8,128)(2,1)}, bf16[64,8,16,128]{3,2,1,0:T(8,128)(2,1)S(1)}, u32[]{:S(2)}) copy-start(bf16[64,8,16,128]{3,2,1,0:T(8,128)(2,1)S(1)} %copy.213) | copy-start | bytes 6291460
  186.5 47.0 %all-to-all-start.3 = ((bf16[8,128,896]{2,1,0:T(8,128)(2,1)}), bf16[8,128,896]{2,1,0:T(8,128)(2,1)}, u32[]{:S(2)}, u32[]{:S(2)}) async-start(bf16[8,128,896]{2,1,0:T(8,128)(2,1)} %broadcast_select_fusion.4), calls=%async_computation.3 | async-start | bytes 3670016 | tf_op jit(solution)/shard_map/all_to_all | solution.py:149
  233.4 45.6 %all-to-all-start.5 = ((bf16[8,128,896]{2,1,0:T(8,128)(2,1)}), bf16[8,128,896]{2,1,0:T(8,128)(2,1)S(1)}, u32[]{:S(2)}, u32[]{:S(2)}) async-start(bf16[8,128,896]{2,1,0:T(8,128)(2,1)} %broadcast_select_fusion.2), calls=%async_computation.5 | async-start | bytes 3670016 | tf_op jit(solution)/shard_map/all_to_all | solution.py:149
  279.1 46.5 %all-to-all-start.4 = ((bf16[8,128,896]{2,1,0:T(8,128)(2,1)}), bf16[8,128,896]{2,1,0:T(8,128)(2,1)}, u32[]{:S(2)}, u32[]{:S(2)}) async-start(bf16[8,128,896]{2,1,0:T(8,128)(2,1)} %broadcast_select_fusion.5), calls=%async_computation.4 | async-start | bytes 3670016 | tf_op jit(solution)/shard_map/all_to_all | solution.py:130
  291.6 38.5 %copy-start.48 = (bf16[4,128,896]{2,1,0:T(8,128)(2,1)S(1)}, bf16[4,128,896]{2,1,0:T(8,128)(2,1)}, u32[]{:S(2)}) copy-start(bf16[4,128,896]{2,1,0:T(8,128)(2,1)} %copy-done.47) | copy-start | bytes 2752516
  291.6 40.1 %copy-start.46 = (bf16[4,128,896]{2,1,0:T(8,128)(2,1)S(1)}, bf16[4,128,896]{2,1,0:T(8,128)(2,1)}, u32[]{:S(2)}) copy-start(bf16[4,128,896]{2,1,0:T(8,128)(2,1)} %copy-done.45) | copy-start | bytes 2752516
  325.6 46.5 %all-to-all-start.6 = ((bf16[8,128,896]{2,1,0:T(8,128)(2,1)}), bf16[8,128,896]{2,1,0:T(8,128)(2,1)}, u32[]{:S(2)}, u32[]{:S(2)}) async-start(bf16[8,128,896]{2,1,0:T(8,128)(2,1)} %broadcast_select_fusion.3), calls=%async_computation.6 | async-start | bytes 3670016 | tf_op jit(solution)/shard_map/all_to_all | solution.py:130
  330.0 249.4 %reduce-scatter.3.cloned.1.call-start = ((), (), s32[]{:S(2)}) async-start(), calls=%async_computation.11 | async-start | bytes 16515072 | tf_op jit(solution)/shard_map/reduce_scatter | solution.py:188
  392.4 30.5 %copy-start.4 = (bf16[64,8,16,128]{3,2,1,0:T(8,128)(2,1)}, bf16[64,8,16,128]{3,2,1,0:T(8,128)(2,1)S(1)}, u32[]{:S(2)}) copy-start(bf16[64,8,16,128]{3,2,1,0:T(8,128)(2,1)S(1)} %copy.220) | copy-start | bytes 6291460
  424.0 10.3 %copy-start.79 = (f32[2,16,64]{2,1,0:T(8,128)}, f32[2,16,64]{2,1,0:T(8,128)S(1)}, u32[]{:S(2)}) copy-start(f32[2,16,64]{2,1,0:T(8,128)S(1)} %get-tuple-element.80) | copy-start | bytes 24580
  499.8 46.4 %all-to-all-start.7 = ((bf16[8,128,896]{2,1,0:T(8,128)(2,1)}), bf16[8,128,896]{2,1,0:T(8,128)(2,1)S(1)}, u32[]{:S(2)}, u32[]{:S(2)}) async-start(bf16[8,128,896]{2,1,0:T(8,128)(2,1)} %broadcast_select_fusion.1), calls=%async_computation.7 | async-start | bytes 3670016 | tf_op jit(solution)/shard_map/all_to_all | solution.py:149
  529.8 20.9 %copy-start.76 = (bf16[2,64,16,128]{3,1,2,0:T(8,128)(2,1)S(1)}, bf16[2,64,16,128]{3,1,2,0:T(8,128)(2,1)}, u32[]{:S(2)}) copy-start(bf16[2,64,16,128]{3,1,2,0:T(8,128)(2,1)} %fusion.111) | copy-start | bytes 1572868
  546.2 59.3 %all-to-all-start.8 = ((bf16[8,128,896]{2,1,0:T(8,128)(2,1)}), bf16[8,128,896]{2,1,0:T(8,128)(2,1)}, u32[]{:S(2)}, u32[]{:S(2)}) async-start(bf16[8,128,896]{2,1,0:T(8,128)(2,1)} %broadcast_select_fusion), calls=%async_computation.8 | async-start | bytes 3670016 | tf_op jit(solution)/shard_map/all_to_all | solution.py:149
  550.7 96.3 %reduce-scatter.5.cloned.1.call-start = ((), (), s32[]{:S(2)}) async-start(), calls=%async_computation.12 | async-start | bytes 2621440 | tf_op jit(solution)/shard_map/reduce_scatter | solution.py:194
  571.5 10.9 %copy-start.84 = (s32[8]{0:T(128)S(1)}, s32[8]{0:T(128)}, u32[]{:S(2)}) copy-start(s32[8]{0:T(128)} %copy-done.83) | copy-start | bytes 100
  571.6 19.8 %collective-permute-start.2 = (bf16[2,63,2048]{2,1,0:T(8,128)(2,1)S(1)}, bf16[2,63,2048]{2,1,0:T(8,128)(2,1)}, u32[]{:S(2)}, u32[]{:S(2)}) collective-permute-start(bf16[2,63,2048]{2,1,0:T(8,128)(2,1)S(1)} %slice.170), channel_id=1, source_target_pairs={{0,1},{1,2},{2,3},{3,4},{4,5},{5,6},{6,7},{8,9},{9,10},{10,11},{11... | collective-permute-start | bytes 1548296 | tf_op jit(solution)/shard_map/ppermute | solution.py:17
  573.7 22.0 %collective-permute-start.3 = (bf16[2,63,2048]{2,1,0:T(8,128)(2,1)S(1)}, bf16[2,63,2048]{2,1,0:T(8,128)(2,1)}, u32[]{:S(2)}, u32[]{:S(2)}) collective-permute-start(bf16[2,63,2048]{2,1,0:T(8,128)(2,1)S(1)} %slice.174), channel_id=1, source_target_pairs={{0,1},{1,2},{2,3},{3,4},{4,5},{5,6},{6,7},{8,9},{9,10},{10,11},{11... | collective-permute-start | bytes 1548296 | tf_op jit(solution)/shard_map/ppermute | solution.py:17
  (88 other events, 309.6 us)
Sparse Core Ops, SparseCore 0:
  475.6 103.8 reduce-scatter.2
  582.5 44.9 reduce-scatter.4

commit v5 on v3

--- a/solution.py
+++ b/solution.py
@@ -120,42 +120,51 @@
     context_parts = []
     query_parts = []
     returned_parts = []
-    markers = []
+    neighbour_parts = []
+    grads_out = []
     seq_major = []
     proj_parts = []
-    for g in range(chunk_count):
-        outgoing = jnp.take(database, arrived[:, g, :].reshape(chunk_slots), axis=0)
-        if g >= LEAD:
-            outgoing, _ = lax.optimization_barrier((outgoing, markers[g - LEAD]))
-        incoming = lax.all_to_all(outgoing, "dp", split_axis=0, concat_axis=0, tiled=True)
-        neighbours = jnp.take(incoming, slot_indices[g], axis=0).reshape(
-            chunk_refs * NB_LEN, ENC
-        )
-        blocks = slice(g * chunk_blocks, (g + 1) * chunk_blocks)
-        context_shift, query_shift, proj_grads, near_grads = attend_chunk(
-            query_blocks[blocks], grad_blocks[blocks], neighbours, key_weight, value_weight,
-            head_count,
-        )
-        context_parts.append(context_shift)
-        query_parts.append(query_shift)
-        padded = jnp.concatenate(
-            [
-                jnp.zeros((1, NB_LEN, ENC), jnp.bfloat16),
-                near_grads.astype(jnp.bfloat16).reshape(chunk_refs, NB_LEN, ENC),
-            ],
-            axis=0,
-        )
-        slot_grads = jnp.take(padded, slot_refs[g], axis=0)
-        markers.append(slot_grads)
-        returned_parts.append(
-            lax.all_to_all(slot_grads, "dp", split_axis=0, concat_axis=0, tiled=True)
-        )
-        seq_major.append(
-            neighbours.reshape(chunk_refs * NB_LEN, shard_count, seq_total, enc_share)
-            .transpose(0, 2, 1, 3)
-            .reshape(chunk_refs * NB_LEN, ENC)
-        )
-        proj_parts.append(proj_grads)
+    for step in range(chunk_count + 2):
+        payload = []
+        if step < chunk_count:
+            rows = jnp.take(database, arrived[:, step, :].reshape(chunk_slots), axis=0)
+            payload.append(rows.reshape(shard_count, chunk_cap, NB_LEN, ENC))
+        if step >= 2:
+            payload.append(grads_out[step - 2].reshape(shard_count, chunk_cap, NB_LEN, ENC))
+        sent = payload[0] if len(payload) == 1 else jnp.concatenate(payload, axis=1)
+        got = lax.all_to_all(sent, "dp", split_axis=0, concat_axis=0, tiled=True)
+        width = 0
+        if step < chunk_count:
+            neighbour_parts.append(got[:, :chunk_cap].reshape(chunk_slots, NB_LEN, ENC))
+            width = chunk_cap
+        if step >= 2:
+            returned_parts.append(got[:, width:].reshape(chunk_slots, NB_LEN, ENC))
+        g = step - 1
+        if 0 <= g < chunk_count:
+            neighbours = jnp.take(neighbour_parts[g], slot_indices[g], axis=0).reshape(
+                chunk_refs * NB_LEN, ENC
+            )
+            blocks = slice(g * chunk_blocks, (g + 1) * chunk_blocks)
+            context_shift, query_shift, proj_grads, near_grads = attend_chunk(
+                query_blocks[blocks], grad_blocks[blocks], neighbours, key_weight, value_weight,
+                head_count,
+            )
+            context_parts.append(context_shift)
+            query_parts.append(query_shift)
+            padded = jnp.concatenate(
+                [
+                    jnp.zeros((1, NB_LEN, ENC), jnp.bfloat16),
+                    near_grads.astype(jnp.bfloat16).reshape(chunk_refs, NB_LEN, ENC),
+                ],
+                axis=0,
+            )
+            grads_out.append(jnp.take(padded, slot_refs[g], axis=0))
+            seq_major.append(
+                neighbours.reshape(chunk_refs * NB_LEN, shard_count, seq_total, enc_share)
+                .transpose(0, 2, 1, 3)
+                .reshape(chunk_refs * NB_LEN, ENC)
+            )
+            proj_parts.append(proj_grads)
 
     def weight_term(first, last):
         return jnp.einsum(
@@ -170,12 +179,12 @@
         weight_terms = weight_term(0, chunk_count - 1) + weight_terms
 
     returned = jnp.stack(
-        [part.reshape(shard_count, chunk_cap, NB_LEN * ENC) for part in returned_parts], axis=1
-    ).reshape(shard_count * chunk_count * chunk_cap, NB_LEN * ENC)
+        [part.reshape(shard_count, chunk_cap, NB_LEN, ENC) for part in returned_parts], axis=1
+    ).reshape(shard_count * chunk_count * chunk_cap, NB_LEN, ENC)
     row_hits = one_hot(arrived.reshape(-1), database.shape[0]).astype(jnp.bfloat16)
     database_grad = jnp.einsum(
-        "sr,sx->rx", row_hits, returned, preferred_element_type=jnp.float32
-    ).reshape(database.shape)
+        "sr,sax->rax", row_hits, returned, preferred_element_type=jnp.float32
+    )
 
     context_shift = jnp.concatenate(context_parts, axis=0).reshape(seq_count, seq_span, feat_width)
     query_shift = jnp.concatenate(query_parts, axis=0).reshape(seq_count, seq_span, feat_width)

time: 654 us -> 623 us (0.953)
  blocking collectives: 45.3 us -> 0 us
  local copies, waits for them, and re-layouts: 208 us -> 234 us
  other arithmetic: 53.6 us -> 40.9 us
  matrix products: 146 us -> 139 us
  waiting for transfers between devices: 132 us -> 139 us
    all_to_all x1 -> x0, blocking collectives: 45.3 us -> none  [local(): lax.all_to_all(slot_grads, 'dp', split_axis=0, concat_axis=0, tiled=True)]
    reshape x1 -> x3, local copies, waits for them, and re-layouts: 7.93 us -> 22.2 us  [the longest x1 16 us: local(): returned = jnp.stack([part.reshape(shard_count, chunk_cap, NB_LEN, ENC) f...]
    reduce_scatter x1, waiting for transfers between devices: 0.01 us -> 11.8 us  [local(): lax.psum_scatter(weight_terms.reshape(seq_total, shard_count * enc_share,...]
    select_n x24 -> x22, other arithmetic: 17.4 us -> 7.66 us  [the longest x8 5.99 us: local(): rows = jnp.take(database, arrived[:, step, :].reshape(chunk_slots), axis=0)]
    concatenate x0 -> x2, local copies, waits for them, and re-layouts: none -> 9.27 us  [local(): sent = payload[0] if len(payload) == 1 else jnp.concatenate(payload, axis=1)]
    another operation x8 -> x7, local copies, waits for them, and re-layouts: 14.5 us -> 21.9 us  [the longest x3 21.6 us: local(): jnp.stack([part.reshape(shard_count, chunk_cap, NB_LEN, ENC) for part in...]
    all_to_all x7 -> x6, waiting for transfers between devices: 132 us -> 128 us  [local(): got = lax.all_to_all(sent, 'dp', split_axis=0, concat_axis=0, tiled=True)]
    unnamed x188 -> x186, local copies, waits for them, and re-layouts: 63.5 us -> 66.7 us
  transfers between devices with their start and end apart: 14 -> 13, of which waited for: 6 -> 5; matrix products, arithmetic and copies ran while one was open for 35% -> 46% of each run, Pallas kernels for 0% -> 0%
where the time goes in v5:
time: 623 us; the launch traced here: 613 us
  local copies, waits for them, and re-layouts  234 us (38%)
  waiting for transfers between devices  139 us (22%)
  matrix products  139 us (22%)
  starting transfers between devices  44.3 us (7%)
  other arithmetic  40.9 us (7%)
  between operations  15.8 us (3%)
    all_to_all x6, waiting for transfers between devices, local(): got = lax.all_to_all(sent, 'dp', split_axis=0, concat_axis=0, tiled=True)  128 us
    unnamed x186, local copies, waits for them, and re-layouts  66.7 us
    dot_general x4, matrix products, attend_chunk(): jnp.einsum('pz,xz->px', proj_grads, both_weights, preferred_element_type=...  30.4 us
    all_to_all x6, starting transfers between devices, local(): got = lax.all_to_all(sent, 'dp', split_axis=0, concat_axis=0, tiled=True)  29.4 us
    dot_general x2, matrix products, weight_term(): jnp.einsum('px,pz->xz', jnp.concatenate(seq_major[first:last], axis=0), j...  26.9 us
    another operation x3, local copies, waits for them, and re-layouts, local(): jnp.stack([part.reshape(shard_count, chunk_cap, NB_LEN, ENC) for part in...  21.6 us
    dot_general x4, matrix products, attend_chunk(): jnp.dot(neighbours, key_weight, preferred_element_type=jnp.float32)  21.4 us
    convert_element_type x4, local copies, waits for them, and re-layouts, attend_chunk(): value_grads = jnp.einsum('chqk,cqhd->ckhd', weight_half, grad_blocks, pre...  18.2 us
  transfers between devices with their start and end apart: 13, of which 5 were waited for; matrix products, arithmetic and copies ran while one was open for 46% of the time, Pallas kernels for 0%

profile of v5, /device:TPU:0, one launch (start us, length us, event | category | flops | bytes accessed | tf_op | source)
XLA Modules:
  0.0 613.1 jit_solution(5590129732444612011)
XLA Ops:
  13.3 6.3 %all-to-all-start = ((s32[4,4,2]{1,2,0:T(2,128)}), s32[4,4,2]{1,2,0:T(2,128)S(1)}, u32[]{:S(2)}, u32[]{:S(2)}) async-start(s32[4,4,2]{1,2,0:T(2,128)} %copy.286), calls=%async_computation | async-start | bytes 8192 | tf_op jit(solution)/shard_map/all_to_all | solution.py:109
  40.8 5.1 all-to-all-start.2
  54.9 5.1 gather_fusion.4
  72.6 16.9 %all-to-all-done.2 = bf16[4,2,128,896]{3,2,1,0:T(8,128)(2,1)} async-done(((bf16[4,2,128,896]{3,2,1,0:T(8,128)(2,1)}), bf16[4,2,128,896]{3,2,1,0:T(8,128)(2,1)}, u32[]{:S(2)}, u32[]{:S(2)}) %all-to-all-start.2) | async-done | bytes 1835040 | tf_op jit(solution)/shard_map/all_to_all | solution.py:135
  123.2 8.4 %convolution_convert_fusion.10 = bf16[512,896]{1,0:T(8,128)(2,1)S(1)} fusion(bf16[512,4096]{1,0:T(8,128)(2,1)S(1)} %bitcast_dynamic-update-slice_fusion.4, bf16[896,4096]{1,0:T(8,128)(2,1)} %copy-done.60), kind=kOutput, calls=%fused_computation.129 | convolution fusion | flops 3758555136 | bytes 12451840 | tf_op jit(solution)/shard_map/pz,xz->px/dot_general | solution.py:69
  139.1 5.5 all-to-all-start.4
  177.4 8.6 %convolution_convert_fusion.11 = bf16[512,896]{1,0:T(8,128)(2,1)S(1)} fusion(bf16[512,4096]{1,0:T(8,128)(2,1)S(1)} %bitcast_dynamic-update-slice_fusion.6, bf16[896,4096]{1,0:T(8,128)(2,1)} %copy-done.60), kind=kOutput, calls=%fused_computation.130 | convolution fusion | flops 3758555136 | bytes 12451840 | tf_op jit(solution)/shard_map/pz,xz->px/dot_general | solution.py:69
  193.4 33.6 %all-to-all-done.4 = bf16[4,4,128,896]{3,1,2,0:T(4,128)(2,1)} async-done(((bf16[4,4,128,896]{3,1,2,0:T(4,128)(2,1)}), bf16[4,4,128,896]{3,1,2,0:T(4,128)(2,1)}, u32[]{:S(2)}, u32[]{:S(2)}) %all-to-all-start.4) | async-done | bytes 3670048 | tf_op jit(solution)/shard_map/all_to_all | solution.py:135
  238.9 7.7 %slice_bitcast_fusion = (bf16[4,1,2,128,896]{4,2,3,0,1:T(2,128)(2,1)}, bf16[4,2,128,896]{3,1,2,0:T(2,128)(2,1)S(1)}) fusion(bf16[4,4,128,896]{3,1,2,0:T(4,128)(2,1)} %all-to-all-done.4), kind=kLoop, calls=%fused_computation.109 | loop fusion | bytes 7340032 | tf_op jit(solution)/shard_map/stack;reshape;reshape | solution.py:181
  249.5 5.8 fusion.61
  259.0 54.2 %all-to-all-done.3 = bf16[4,4,128,896]{3,1,2,0:T(4,128)(2,1)} async-done(((bf16[4,4,128,896]{3,1,2,0:T(4,128)(2,1)}), bf16[4,4,128,896]{3,1,2,0:T(4,128)(2,1)}, u32[]{:S(2)}, u32[]{:S(2)}) %all-to-all-start.3) | async-done | bytes 3670048 | tf_op jit(solution)/shard_map/all_to_all | solution.py:135
  313.3 7.6 %slice_bitcast_fusion.1 = (bf16[4,1,2,128,896]{4,2,3,0,1:T(2,128)(2,1)}, bf16[4,2,128,896]{3,1,2,0:T(2,128)(2,1)S(1)}) fusion(bf16[4,4,128,896]{3,1,2,0:T(4,128)(2,1)} %all-to-all-done.3), kind=kLoop, calls=%fused_computation.110 | loop fusion | bytes 7340032 | tf_op jit(solution)/shard_map/stack;reshape;reshape | solution.py:181
  323.2 6.0 fusion.59
  395.6 7.6 %fusion.156 = f32[896,4096]{1,0:T(8,128)} fusion(bf16[512,896]{0,1:T(8,128)(2,1)S(1)} %copy-done.68, bf16[512,4096]{1,0:T(8,128)(2,1)S(1)} %bitcast_dynamic-update-slice_fusion), kind=kOutput, calls=%fused_computation.258 | convolution fusion | flops 3758096384 | bytes 19791872 | tf_op jit(solution)/shard_map/px,pz->xz/dot_general | solution.py:170
  403.2 19.3 %fusion.6 = f32[896,4096]{1,0:T(8,128)} fusion(f32[896,4096]{1,0:T(8,128)} %fusion.156, bf16[512,4096]{1,0:T(8,128)(2,1)S(1)} %copy-done.61, bf16[512,4096]{1,0:T(8,128)(2,1)} %copy-done.64, bf16[512,4096]{1,0:T(8,128)(2,1)} %copy-done.65, bf16[512,896]{0,1:T(8,128)(2,1)} %reshape.303, bf16[512,896]{0,1:T(8,128)(2,1)S(1)} %copy-done.66, ...), kind=kOutput, calls=%fused_computation.19 | convolution fusion | flops 11323965440 | bytes 44695552 | tf_op jit(solution)/shard_map/px,pz->xz/dot_general | solution.py:170
  424.3 8.9 %convolution_convert_fusion.9 = bf16[512,896]{1,0:T(8,128)(2,1)S(1)} fusion(bf16[512,4096]{1,0:T(8,128)(2,1)} %bitcast_dynamic-update-slice_fusion.2, bf16[896,4096]{1,0:T(8,128)(2,1)} %copy-done.60), kind=kOutput, calls=%fused_computation.128 | convolution fusion | flops 3758555136 | bytes 12451840 | tf_op jit(solution)/shard_map/pz,xz->px/dot_general | solution.py:69
  437.6 5.1 all-to-all-start.5
  461.9 22.8 %all-to-all-done.5 = bf16[4,2,128,896]{3,1,2,0:T(2,128)(2,1)} async-done(((bf16[4,2,128,896]{3,1,2,0:T(2,128)(2,1)}), bf16[4,2,128,896]{3,1,2,0:T(2,128)(2,1)}, u32[]{:S(2)}, u32[]{:S(2)}) %all-to-all-start.5) | async-done | bytes 1835040 | tf_op jit(solution)/shard_map/all_to_all | solution.py:135
  522.6 11.8 %reduce-scatter.3.cloned.1.call-done = f32[1,112,4096]{2,1,0:T(8,128)} async-done(((f32[8,112,4096]{2,1,0:T(8,128)}), f32[1,112,4096]{2,1,0:T(8,128)}) %reduce-scatter.3.cloned.1.call-update) | async-done | bytes 1835024 | tf_op jit(solution)/shard_map/reduce_scatter | solution.py:198
  537.5 15.0 %pad_maximum_fusion = bf16[4,4,2,128,896]{4,2,3,0,1:T(2,128)(2,1)S(1)} fusion(bf16[4,1,2,128,896]{4,2,3,0,1:T(2,128)(2,1)} %bitcast.40, bf16[4,1,2,128,896]{4,2,3,0,1:T(2,128)(2,1)} %bitcast.35, bf16[4,1,2,128,896]{4,2,3,0,1:T(2,128)(2,1)S(1)} %copy-done.30, bf16[4,1,2,128,896]{4,2,3,0,1:T(2,128)(2,1)} %get-tuple-element.58), kind=kLoop, calls=%fused_computation.18 | loop fusion | flops 11010048 | bytes 14680064 | tf_op jit(solution)/shard_map/stack | solution.py:181
  552.5 6.3 %copy.328 = bf16[4,4,2,128,896]{4,2,1,0,3:T(2,128)(2,1)} copy(bf16[4,4,2,128,896]{4,2,3,0,1:T(2,128)(2,1)S(1)} %pad_maximum_fusion) | data formatting | bytes 14680064 | tf_op jit(solution)/shard_map/stack | solution.py:181
  558.8 16.0 %reshape.300 = bf16[32,128,896]{2,0,1:T(8,128)(2,1)} reshape(bf16[4,4,2,128,896]{4,2,1,0,3:T(2,128)(2,1)} %copy.328) | data formatting | bytes 14680064 | tf_op jit(solution)/shard_map/reshape | solution.py:183
  574.7 10.4 %fusion.135 = f32[32,128,896]{2,0,1:T(8,128)} fusion(bf16[32,128,896]{2,0,1:T(8,128)(2,1)} %reshape.300, s32[32]{0:T(128)S(1)} %eq.143), kind=kOutput, calls=%fused_computation.180 | convolution fusion | flops 234884096 | bytes 22020224 | tf_op jit(solution)/shard_map/sr,sax->rax/dot_general | solution.py:185
  585.1 19.1 %copy.337 = f32[32,128,896]{2,1,0:T(8,128)} copy(f32[32,128,896]{2,0,1:T(8,128)} %fusion.135) | data formatting | bytes 29360128
  (402 shorter events, 284.2 us)
Async XLA Ops:
  13.3 20.7 %all-to-all-start = ((s32[4,4,2]{1,2,0:T(2,128)}), s32[4,4,2]{1,2,0:T(2,128)S(1)}, u32[]{:S(2)}, u32[]{:S(2)}) async-start(s32[4,4,2]{1,2,0:T(2,128)} %copy.286), calls=%async_computation | async-start | bytes 8192 | tf_op jit(solution)/shard_map/all_to_all | solution.py:109
  21.5 46.4 %collective-permute-start.1 = (bf16[2,63,2048]{2,1,0:T(8,128)(2,1)}, bf16[2,63,2048]{2,1,0:T(8,128)(2,1)}, u32[]{:S(2)}, u32[]{:S(2)}) collective-permute-start(bf16[2,63,2048]{2,1,0:T(8,128)(2,1)} %slice.130), channel_id=1, source_target_pairs={{1,0},{2,1},{3,2},{4,3},{5,4},{6,5},{7,6},{9,8},{10,9},{11,10},{12... | collective-permute-start | bytes 1548296 | tf_op jit(solution)/shard_map/ppermute | solution.py:17
  24.7 41.2 %collective-permute-start = (bf16[2,63,2048]{2,1,0:T(8,128)(2,1)}, bf16[2,63,2048]{2,1,0:T(8,128)(2,1)}, u32[]{:S(2)}, u32[]{:S(2)}) collective-permute-start(bf16[2,63,2048]{2,1,0:T(8,128)(2,1)} %slice.124), channel_id=1, source_target_pairs={{1,0},{2,1},{3,2},{4,3},{5,4},{6,5},{7,6},{9,8},{10,9},{11,10},{12... | collective-permute-start | bytes 1548296 | tf_op jit(solution)/shard_map/ppermute | solution.py:17
  40.8 48.8 %all-to-all-start.2 = ((bf16[4,2,128,896]{3,2,1,0:T(8,128)(2,1)}), bf16[4,2,128,896]{3,2,1,0:T(8,128)(2,1)}, u32[]{:S(2)}, u32[]{:S(2)}) async-start(bf16[4,2,128,896]{3,2,1,0:T(8,128)(2,1)} %bitcast.4), calls=%async_computation.2 | async-start | bytes 3670016 | tf_op jit(solution)/shard_map/all_to_all | solution.py:135
  89.5 49.6 %all-to-all-start.1 = ((bf16[4,2,128,896]{3,2,1,0:T(8,128)(2,1)}), bf16[4,2,128,896]{3,2,1,0:T(8,128)(2,1)}, u32[]{:S(2)}, u32[]{:S(2)}) async-start(bf16[4,2,128,896]{3,2,1,0:T(8,128)(2,1)} %bitcast), calls=%async_computation.1 | async-start | bytes 3670016 | tf_op jit(solution)/shard_map/all_to_all | solution.py:135
  123.2 8.4 %copy-start.64 = (bf16[512,4096]{1,0:T(8,128)(2,1)}, bf16[512,4096]{1,0:T(8,128)(2,1)S(1)}, u32[]{:S(2)}) copy-start(bf16[512,4096]{1,0:T(8,128)(2,1)S(1)} %bitcast_dynamic-update-slice_fusion.4) | copy-start | bytes 12582916
  139.1 87.9 %all-to-all-start.4 = ((bf16[4,4,128,896]{3,1,2,0:T(4,128)(2,1)}), bf16[4,4,128,896]{3,1,2,0:T(4,128)(2,1)}, u32[]{:S(2)}, u32[]{:S(2)}) async-start(bf16[4,4,128,896]{3,1,2,0:T(4,128)(2,1)} %copy.306), calls=%async_computation.4 | async-start | bytes 7340032 | tf_op jit(solution)/shard_map/all_to_all | solution.py:135
  159.2 9.8 %copy-start.19 = (f32[2,16,64,256]{3,2,1,0:T(8,128)}, f32[2,16,64,256]{3,2,1,0:T(8,128)S(1)}, u32[]{:S(2)}) copy-start(f32[2,16,64,256]{3,2,1,0:T(8,128)S(1)} %get-tuple-element.87) | copy-start | bytes 6291460
  159.2 9.8 %copy-start.77 = (f32[2,16,64]{2,1,0:T(8,128)}, f32[2,16,64]{2,1,0:T(8,128)S(1)}, u32[]{:S(2)}) copy-start(f32[2,16,64]{2,1,0:T(8,128)S(1)} %get-tuple-element.86) | copy-start | bytes 24580
  177.4 8.6 %copy-start.65 = (bf16[512,4096]{1,0:T(8,128)(2,1)}, bf16[512,4096]{1,0:T(8,128)(2,1)S(1)}, u32[]{:S(2)}) copy-start(bf16[512,4096]{1,0:T(8,128)(2,1)S(1)} %bitcast_dynamic-update-slice_fusion.6) | copy-start | bytes 12582916
  193.4 38.4 %copy-start.44 = (bf16[4,128,896]{2,1,0:T(8,128)(2,1)S(1)}, bf16[4,128,896]{2,1,0:T(8,128)(2,1)}, u32[]{:S(2)}) copy-start(bf16[4,128,896]{2,1,0:T(8,128)(2,1)} %copy-done.43) | copy-start | bytes 2752516
  227.0 86.3 %all-to-all-start.3 = ((bf16[4,4,128,896]{3,1,2,0:T(4,128)(2,1)}), bf16[4,4,128,896]{3,1,2,0:T(4,128)(2,1)}, u32[]{:S(2)}, u32[]{:S(2)}) async-start(bf16[4,4,128,896]{3,1,2,0:T(4,128)(2,1)} %copy.297), calls=%async_computation.3 | async-start | bytes 7340032 | tf_op jit(solution)/shard_map/all_to_all | solution.py:135
  231.8 302.6 %reduce-scatter.3.cloned.1.call-start = ((), (), s32[]{:S(2)}) async-start(), calls=%async_computation.9 | async-start | bytes 16515072 | tf_op jit(solution)/shard_map/reduce_scatter | solution.py:198
  340.4 30.3 %copy-start.4 = (bf16[64,8,16,128]{3,2,1,0:T(8,128)(2,1)}, bf16[64,8,16,128]{3,2,1,0:T(8,128)(2,1)S(1)}, u32[]{:S(2)}) copy-start(bf16[64,8,16,128]{3,2,1,0:T(8,128)(2,1)S(1)} %copy.358) | copy-start | bytes 6291460
  437.6 8.9 %copy-start.76 = (f32[2,16,64]{2,1,0:T(8,128)S(1)}, f32[2,16,64]{2,1,0:T(8,128)}, u32[]{:S(2)}) copy-start(f32[2,16,64]{2,1,0:T(8,128)} %copy-done.75) | copy-start | bytes 24580
  437.6 47.1 %all-to-all-start.5 = ((bf16[4,2,128,896]{3,1,2,0:T(2,128)(2,1)}), bf16[4,2,128,896]{3,1,2,0:T(2,128)(2,1)}, u32[]{:S(2)}, u32[]{:S(2)}) async-start(bf16[4,2,128,896]{3,1,2,0:T(2,128)(2,1)} %copy.324), calls=%async_computation.5 | async-start | bytes 3670016 | tf_op jit(solution)/shard_map/all_to_all | solution.py:135
  461.9 27.7 %copy-start.22 = (f32[2,16,64,256]{3,2,1,0:T(8,128)S(1)}, f32[2,16,64,256]{3,2,1,0:T(8,128)}, u32[]{:S(2)}) copy-start(f32[2,16,64,256]{3,2,1,0:T(8,128)} %copy-done.21) | copy-start | bytes 6291460
  484.7 52.8 %all-to-all-start.6 = ((bf16[4,2,128,896]{3,1,2,0:T(2,128)(2,1)}), bf16[4,2,128,896]{3,1,2,0:T(2,128)(2,1)}, u32[]{:S(2)}, u32[]{:S(2)}) async-start(bf16[4,2,128,896]{3,1,2,0:T(2,128)(2,1)} %copy.327), calls=%async_computation.6 | async-start | bytes 3670016 | tf_op jit(solution)/shard_map/all_to_all | solution.py:135
  489.1 115.1 %reduce-scatter.5.cloned.1.call-start = ((), (), s32[]{:S(2)}) async-start(), calls=%async_computation.10 | async-start | bytes 2621440 | tf_op jit(solution)/shard_map/reduce_scatter | solution.py:204
  496.5 8.7 %copy-start.7 = (bf16[64,8,16,128]{3,2,1,0:T(8,128)(2,1)S(1)}, bf16[64,8,16,128]{3,2,1,0:T(8,128)(2,1)}, u32[]{:S(2)}) copy-start(bf16[64,8,16,128]{3,2,1,0:T(8,128)(2,1)} %copy-done.6) | copy-start | bytes 6291460
  496.5 8.7 %copy-start.13 = (bf16[2,16,64,256]{3,2,1,0:T(8,128)(2,1)S(1)}, bf16[2,16,64,256]{3,2,1,0:T(8,128)(2,1)}, u32[]{:S(2)}) copy-start(bf16[2,16,64,256]{3,2,1,0:T(8,128)(2,1)} %copy-done.12) | copy-start | bytes 3145732
  502.8 13.8 %collective-permute-start.2 = (bf16[2,63,2048]{2,1,0:T(8,128)(2,1)}, bf16[2,63,2048]{2,1,0:T(8,128)(2,1)}, u32[]{:S(2)}, u32[]{:S(2)}) collective-permute-start(bf16[2,63,2048]{2,1,0:T(8,128)(2,1)} %slice.184), channel_id=1, source_target_pairs={{0,1},{1,2},{2,3},{3,4},{4,5},{5,6},{6,7},{8,9},{9,10},{10,11},{11... | collective-permute-start | bytes 1548296 | tf_op jit(solution)/shard_map/ppermute | solution.py:17
  513.2 7.6 %collective-permute-start.3 = (bf16[2,63,2048]{2,1,0:T(8,128)(2,1)S(1)}, bf16[2,63,2048]{2,1,0:T(8,128)(2,1)S(1)}, u32[]{:S(2)}, u32[]{:S(2)}) collective-permute-start(bf16[2,63,2048]{2,1,0:T(8,128)(2,1)S(1)} %slice.188), channel_id=1, source_target_pairs={{0,1},{1,2},{2,3},{3,4},{4,5},{5,6},{6,7},{8,9},{9,10},{10,11},{11... | collective-permute-start | bytes 1548296 | tf_op jit(solution)/shard_map/ppermute | solution.py:17
  522.6 14.9 %copy-start.30 = (bf16[4,1,2,128,896]{4,2,3,0,1:T(2,128)(2,1)S(1)}, bf16[4,1,2,128,896]{4,2,3,0,1:T(2,128)(2,1)}, u32[]{:S(2)}) copy-start(bf16[4,1,2,128,896]{4,2,3,0,1:T(2,128)(2,1)} %get-tuple-element.60) | copy-start | bytes 5505028
  (76 other events, 215.0 us)
Sparse Core Ops, SparseCore 0:
  422.7 111.6 reduce-scatter.2
  537.6 47.2 reduce-scatter.4

commit v6 on v4

--- a/solution.py
+++ b/solution.py
@@ -117,17 +117,24 @@
     )
 
     enc_share = ENC // (shard_count * seq_total)
+    fetched = []
+    link = None
+    for g in range(chunk_count):
+        rows = jnp.take(database, arrived[:, g, :].reshape(chunk_slots), axis=0)
+        if link is not None:
+            rows, _ = lax.optimization_barrier((rows, link))
+        link = lax.all_to_all(rows, "dp", split_axis=0, concat_axis=0, tiled=True)
+        fetched.append((rows, link))
+
     context_parts = []
     query_parts = []
-    database_grad = None
-    markers = []
+    grads_out = []
     seq_major = []
     proj_parts = []
     for g in range(chunk_count):
-        outgoing = jnp.take(database, arrived[:, g, :].reshape(chunk_slots), axis=0)
-        if g >= LEAD:
-            outgoing, _ = lax.optimization_barrier((outgoing, markers[g - LEAD]))
-        incoming = lax.all_to_all(outgoing, "dp", split_axis=0, concat_axis=0, tiled=True)
+        incoming = fetched[g][1]
+        if g + 1 < chunk_count:
+            incoming, _ = lax.optimization_barrier((incoming, fetched[g + 1][0]))
         neighbours = jnp.take(incoming, slot_indices[g], axis=0).reshape(
             chunk_refs * NB_LEN, ENC
         )
@@ -145,17 +152,7 @@
             ],
             axis=0,
         )
-        slot_grads = jnp.take(padded, slot_refs[g], axis=0)
-        returned = lax.all_to_all(slot_grads, "dp", split_axis=0, concat_axis=0, tiled=True)
-        markers.append(returned)
-        row_hits = one_hot(arrived[:, g, :].reshape(chunk_slots), database.shape[0])
-        part = jnp.einsum(
-            "sr,sax->rax",
-            row_hits.astype(jnp.bfloat16),
-            returned,
-            preferred_element_type=jnp.float32,
-        )
-        database_grad = part if database_grad is None else database_grad + part
+        grads_out.append(jnp.take(padded, slot_refs[g], axis=0))
         seq_major.append(
             neighbours.reshape(chunk_refs * NB_LEN, shard_count, seq_total, enc_share)
             .transpose(0, 2, 1, 3)
@@ -175,6 +172,17 @@
     if chunk_count > 1:
         weight_terms = weight_term(0, chunk_count - 1) + weight_terms
 
+    database_grad = None
+    for g in range(chunk_count):
+        sent, _ = lax.optimization_barrier((grads_out[g], link))
+        link = lax.all_to_all(sent, "dp", split_axis=0, concat_axis=0, tiled=True)
+        row_hits = one_hot(arrived[:, g, :].reshape(chunk_slots), database.shape[0])
+        part = jnp.sum(
+            row_hits.astype(jnp.float32)[:, :, None, None]
+            * link.astype(jnp.float32)[:, None, :, :],
+            axis=0,
+        )
+        database_grad = part if database_grad is None else database_grad + part
 
     context_shift = jnp.concatenate(context_parts, axis=0).reshape(seq_count, seq_span, feat_width)
     query_shift = jnp.concatenate(query_parts, axis=0).reshape(seq_count, seq_span, feat_width)

time: 662 us -> 601 us (0.908)
  waiting for transfers between devices: 181 us -> 74.5 us
  other arithmetic: 44.7 us -> 143 us
  matrix products: 180 us -> 140 us
  local copies, waits for them, and re-layouts: 189 us -> 168 us
    all_to_all x8, waiting for transfers between devices: 176 us -> 52.7 us  [the longest x4 27.4 us: local(): link = lax.all_to_all(sent, 'dp', split_axis=0, concat_axis=0, tiled=True)]
    reduce_sum x0 -> x4, other arithmetic: none -> 75.5 us  [local(): jnp.sum(row_hits.astype(jnp.float32)[:, :, None, None] * link.astype(jnp....]
    dot_general x4 -> x0, matrix products: 47.1 us -> none  [local(): jnp.einsum('sr,sax->rax', row_hits.astype(jnp.bfloat16), returned, prefer...]
    add x0 -> x1, other arithmetic: none -> 24.8 us  [local(): database_grad = part if database_grad is None else database_grad + part]
    reduce_scatter x1, waiting for transfers between devices: 0.01 us -> 21.7 us  [local(): lax.psum_scatter(plane_sums.reshape(shard_count, enc_share, 2 * feat_widt...]
    unnamed x206 -> x191, local copies, waits for them, and re-layouts: 67.6 us -> 49.4 us
    convert_element_type x0 -> x8, other arithmetic: none -> 13.1 us  [the longest x4 12.8 us: local(): link.astype(jnp.float32)[:, None, :, :]]
    dot_general x4, matrix products: 28.2 us -> 38.7 us  [attend_chunk(): jnp.einsum('pz,xz->px', proj_grads, both_weights, preferred_element_type=...]
  transfers between devices with their start and end apart: 15 -> 15, of which waited for: 9 -> 8; matrix products, arithmetic and copies ran while one was open for 34% -> 60% of each run, Pallas kernels for 0% -> 0%
where the time goes in v6:
time: 601 us; the launch traced here: 594 us
  local copies, waits for them, and re-layouts  168 us (28%)
  other arithmetic  143 us (24%)
  matrix products  140 us (23%)
  waiting for transfers between devices  74.5 us (12%)
  starting transfers between devices  51.3 us (9%)
  between operations  15.7 us (3%)
    reduce_sum x4, other arithmetic, local(): jnp.sum(row_hits.astype(jnp.float32)[:, :, None, None] * link.astype(jnp....  75.5 us
    unnamed x191, local copies, waits for them, and re-layouts  49.4 us
    dot_general x4, matrix products, attend_chunk(): jnp.einsum('pz,xz->px', proj_grads, both_weights, preferred_element_type=...  38.7 us
    dot_general x2, matrix products, weight_term(): jnp.einsum('px,pz->xz', jnp.concatenate(seq_major[first:last], axis=0), j...  28.1 us
    all_to_all x4, waiting for transfers between devices, local(): link = lax.all_to_all(sent, 'dp', split_axis=0, concat_axis=0, tiled=True)  27.4 us
    all_to_all x4, waiting for transfers between devices, local(): link = lax.all_to_all(rows, 'dp', split_axis=0, concat_axis=0, tiled=True)  25.3 us
    add x1, other arithmetic, local(): database_grad = part if database_grad is None else database_grad + part  24.8 us
    dot_general x4, matrix products, attend_chunk(): jnp.dot(neighbours, key_weight, preferred_element_type=jnp.float32)  21.9 us
  transfers between devices with their start and end apart: 15, of which 8 were waited for; matrix products, arithmetic and copies ran while one was open for 60% of the time, Pallas kernels for 0%

profile of v6, /device:TPU:0, one launch (start us, length us, event | category | flops | bytes accessed | tf_op | source)
XLA Modules:
  0.0 593.6 jit_solution(6523039064960628647)
XLA Ops:
  15.0 6.3 %all-to-all-start = ((s32[4,4,2]{1,2,0:T(2,128)}), s32[4,4,2]{1,2,0:T(2,128)S(1)}, u32[]{:S(2)}, u32[]{:S(2)}) async-start(s32[4,4,2]{1,2,0:T(2,128)} %copy.145), calls=%async_computation | async-start | bytes 8192 | tf_op jit(solution)/shard_map/all_to_all | solution.py:109
  36.3 5.1 all-to-all-start.1
  45.4 5.1 gather_fusion.3
  50.5 5.1 gather_fusion.5
  68.2 16.9 %all-to-all-done.1 = bf16[8,128,896]{2,1,0:T(8,128)(2,1)} async-done(((bf16[8,128,896]{2,1,0:T(8,128)(2,1)}), bf16[8,128,896]{2,1,0:T(8,128)(2,1)}, u32[]{:S(2)}, u32[]{:S(2)}) %all-to-all-start.1) | async-done | bytes 1835040 | tf_op jit(solution)/shard_map/all_to_all | solution.py:126
  126.8 6.3 %all-to-all-done.2 = bf16[8,128,896]{2,1,0:T(8,128)(2,1)} async-done(((bf16[8,128,896]{2,1,0:T(8,128)(2,1)}), bf16[8,128,896]{2,1,0:T(8,128)(2,1)}, u32[]{:S(2)}, u32[]{:S(2)}) %all-to-all-start.2) | async-done | bytes 1835040 | tf_op jit(solution)/shard_map/all_to_all | solution.py:126
  141.4 5.8 fusion.57
  188.5 5.8 fusion.59
  230.6 5.8 fusion.61
  267.7 7.6 %fusion.152 = f32[896,4096]{1,0:T(8,128)} fusion(bf16[512,896]{0,1:T(8,128)(2,1)S(1)} %copy-done.66, bf16[512,4096]{1,0:T(8,128)(2,1)S(1)} %bitcast_dynamic-update-slice_fusion), kind=kOutput, calls=%fused_computation.261 | convolution fusion | flops 3758096384 | bytes 19791872 | tf_op jit(solution)/shard_map/px,pz->xz/dot_general | solution.py:164
  275.3 20.5 %fusion.6 = f32[896,4096]{1,0:T(8,128)} fusion(f32[896,4096]{1,0:T(8,128)} %fusion.152, bf16[512,4096]{1,0:T(8,128)(2,1)} %bitcast_dynamic-update-slice_fusion.2, bf16[512,4096]{1,0:T(8,128)(2,1)} %bitcast_dynamic-update-slice_fusion.4, bf16[512,4096]{1,0:T(8,128)(2,1)} %bitcast_dynamic-update-slice_fusion.6, bf16[512,896]{0,1:T(8,128)(2,1)S(1)} %copy-done.65, ...), kind=kOutput, calls=%fused_computation.23 | convolution fusion | flops 11323965440 | bytes 44695552 | tf_op jit(solution)/shard_map/px,pz->xz/dot_general | solution.py:164
  300.6 9.3 %convolution_convert_fusion.11 = bf16[512,896]{1,0:T(8,128)(2,1)S(1)} fusion(bf16[512,4096]{1,0:T(8,128)(2,1)} %bitcast_dynamic-update-slice_fusion.6, bf16[896,4096]{1,0:T(8,128)(2,1)S(1)} %constant_dynamic-update-slice_fusion), kind=kOutput, calls=%fused_computation.130 | convolution fusion | flops 3758555136 | bytes 12451840 | tf_op jit(solution)/shard_map/pz,xz->px/dot_general | solution.py:69
  325.9 10.1 %convolution_convert_fusion.10 = bf16[512,896]{1,0:T(8,128)(2,1)S(1)} fusion(bf16[512,4096]{1,0:T(8,128)(2,1)} %bitcast_dynamic-update-slice_fusion.4, bf16[896,4096]{1,0:T(8,128)(2,1)} %copy-done.60), kind=kOutput, calls=%fused_computation.129 | convolution fusion | flops 3758555136 | bytes 12451840 | tf_op jit(solution)/shard_map/pz,xz->px/dot_general | solution.py:69
  346.6 9.3 %convolution_convert_fusion.9 = bf16[512,896]{1,0:T(8,128)(2,1)S(1)} fusion(bf16[512,4096]{1,0:T(8,128)(2,1)} %bitcast_dynamic-update-slice_fusion.2, bf16[896,4096]{1,0:T(8,128)(2,1)} %copy-done.60), kind=kOutput, calls=%fused_computation.128 | convolution fusion | flops 3758555136 | bytes 12451840 | tf_op jit(solution)/shard_map/pz,xz->px/dot_general | solution.py:69
  358.1 10.3 %all-to-all-done.5 = bf16[8,128,896]{2,1,0:T(8,128)(2,1)} async-done(((bf16[8,128,896]{2,1,0:T(8,128)(2,1)}), bf16[8,128,896]{2,1,0:T(8,128)(2,1)}, u32[]{:S(2)}, u32[]{:S(2)}) %all-to-all-start.5) | async-done | bytes 1835040 | tf_op jit(solution)/shard_map/all_to_all | solution.py:178
  390.2 10.0 %convolution_convert_fusion.8 = bf16[512,896]{1,0:T(8,128)(2,1)} fusion(bf16[512,4096]{1,0:T(8,128)(2,1)} %copy-done.61, bf16[896,4096]{1,0:T(8,128)(2,1)} %copy-done.60), kind=kOutput, calls=%fused_computation.127 | convolution fusion | flops 3758555136 | bytes 12451840 | tf_op jit(solution)/shard_map/pz,xz->px/dot_general | solution.py:69
  400.2 14.9 %all-to-all-done.6 = bf16[8,128,896]{2,1,0:T(8,128)(2,1)} async-done(((bf16[8,128,896]{2,1,0:T(8,128)(2,1)}), bf16[8,128,896]{2,1,0:T(8,128)(2,1)}, u32[]{:S(2)}, u32[]{:S(2)}) %all-to-all-start.6) | async-done | bytes 1835040 | tf_op jit(solution)/shard_map/all_to_all | solution.py:178
  442.8 18.8 %multiply_reduce_fusion.3 = f32[32,128,896]{2,1,0:T(8,128)} fusion(f32[8,128,896]{2,1,0:T(8,128)} %convert_element_type.283, f32[8,32]{1,0:T(8,128)S(1)} %convert_convert_fusion.3), kind=kLoop, calls=%fused_computation.15 | loop fusion | flops 55050240 | bytes 18351104 | tf_op jit(solution)/shard_map/reduce_sum | solution.py:180
  465.2 5.0 all-to-all-start.8
  470.2 18.8 %multiply_reduce_fusion.2 = f32[32,128,896]{2,1,0:T(8,128)} fusion(f32[8,128,896]{2,1,0:T(8,128)} %convert_element_type.291, f32[8,32]{1,0:T(8,128)S(1)} %convert_convert_fusion.2), kind=kLoop, calls=%fused_computation.14 | loop fusion | flops 55050240 | bytes 18351104 | tf_op jit(solution)/shard_map/reduce_sum | solution.py:180
  492.6 18.8 %multiply_reduce_fusion.1 = f32[32,128,896]{2,1,0:T(8,128)} fusion(f32[8,128,896]{2,1,0:T(8,128)} %convert_element_type.299, f32[8,32]{1,0:T(8,128)S(1)} %convert_convert_fusion.1), kind=kLoop, calls=%fused_computation.13 | loop fusion | flops 55050240 | bytes 18351104 | tf_op jit(solution)/shard_map/reduce_sum | solution.py:180
  515.7 19.1 %multiply_reduce_fusion = f32[32,128,896]{2,1,0:T(8,128)} fusion(f32[8,128,896]{2,1,0:T(8,128)} %convert_element_type.307, f32[8,32]{1,0:T(8,128)S(1)} %convert_convert_fusion), kind=kLoop, calls=%fused_computation.12 | loop fusion | flops 55050240 | bytes 18351104 | tf_op jit(solution)/shard_map/reduce_sum | solution.py:180
  537.9 24.8 %add_add_fusion = f32[32,128,896]{2,1,0:T(8,128)} fusion(f32[32,128,896]{2,1,0:T(8,128)} %multiply_reduce_fusion, f32[32,128,896]{2,1,0:T(8,128)} %multiply_reduce_fusion.1, f32[32,128,896]{2,1,0:T(8,128)} %multiply_reduce_fusion.3, f32[32,128,896]{2,1,0:T(8,128)} %multiply_reduce_fusion.2), kind=kLoop, calls=%fused_computation.16 | loop fusion | flops 11010048 | bytes 73400320 | tf_op jit(solution)/shard_map/add | solution.py:185
  562.7 21.7 %reduce-scatter.5.cloned.1.call-done = f32[1,28,4096]{2,1,0:T(8,128)} async-done(((f32[4,28,4096]{2,1,0:T(8,128)}), f32[1,28,4096]{2,1,0:T(8,128)}) %reduce-scatter.5.cloned.1.call-update) | async-done | bytes 458768 | tf_op jit(solution)/shard_map/reduce_scatter | solution.py:202
  (409 shorter events, 296.6 us)
Async XLA Ops:
  7.2 20.7 %copy-start.47 = (bf16[2,256,2048]{2,1,0:T(8,128)(2,1)S(1)}, bf16[2,256,2048]{2,1,0:T(8,128)(2,1)}, u32[]{:S(2)}) copy-start(bf16[2,256,2048]{2,1,0:T(8,128)(2,1)} %param.13) | copy-start | bytes 6291460
  15.0 14.9 %all-to-all-start = ((s32[4,4,2]{1,2,0:T(2,128)}), s32[4,4,2]{1,2,0:T(2,128)S(1)}, u32[]{:S(2)}, u32[]{:S(2)}) async-start(s32[4,4,2]{1,2,0:T(2,128)} %copy.145), calls=%async_computation | async-start | bytes 8192 | tf_op jit(solution)/shard_map/all_to_all | solution.py:109
  23.2 40.2 %collective-permute-start.2 = (bf16[2,63,2048]{2,1,0:T(8,128)(2,1)}, bf16[2,63,2048]{2,1,0:T(8,128)(2,1)}, u32[]{:S(2)}, u32[]{:S(2)}) collective-permute-start(bf16[2,63,2048]{2,1,0:T(8,128)(2,1)} %slice.127), channel_id=1, source_target_pairs={{1,0},{2,1},{3,2},{4,3},{5,4},{6,5},{7,6},{9,8},{10,9},{11,10},{12... | collective-permute-start | bytes 1548296 | tf_op jit(solution)/shard_map/ppermute | solution.py:17
  26.5 34.8 %collective-permute-start = (bf16[2,63,2048]{2,1,0:T(8,128)(2,1)}, bf16[2,63,2048]{2,1,0:T(8,128)(2,1)}, u32[]{:S(2)}, u32[]{:S(2)}) collective-permute-start(bf16[2,63,2048]{2,1,0:T(8,128)(2,1)} %slice.117), channel_id=1, source_target_pairs={{1,0},{2,1},{3,2},{4,3},{5,4},{6,5},{7,6},{9,8},{10,9},{11,10},{12... | collective-permute-start | bytes 1548296 | tf_op jit(solution)/shard_map/ppermute | solution.py:17
  30.5 28.7 %copy-start.75 = (s32[8]{0:T(128)}, s32[8]{0:T(128)S(1)}, u32[]{:S(2)}) copy-start(s32[8]{0:T(128)S(1)} %reshape_squeeze.15) | copy-start | bytes 100
  30.5 25.0 %copy-start.77 = (s32[8]{0:T(128)}, s32[8]{0:T(128)S(1)}, u32[]{:S(2)}) copy-start(s32[8]{0:T(128)S(1)} %reshape_squeeze.14) | copy-start | bytes 100
  30.6 24.9 %copy-start.79 = (s32[8]{0:T(128)}, s32[8]{0:T(128)S(1)}, u32[]{:S(2)}) copy-start(s32[8]{0:T(128)S(1)} %reshape_squeeze.13) | copy-start | bytes 100
  36.3 48.8 %all-to-all-start.1 = ((bf16[8,128,896]{2,1,0:T(8,128)(2,1)}), bf16[8,128,896]{2,1,0:T(8,128)(2,1)}, u32[]{:S(2)}, u32[]{:S(2)}) async-start(bf16[8,128,896]{2,1,0:T(8,128)(2,1)} %broadcast_select_fusion.7), calls=%async_computation.1 | async-start | bytes 3670016 | tf_op jit(solution)/shard_map/all_to_all | solution.py:126
  66.7 39.0 %copy-start.40 = (bf16[2,64,16,128]{3,2,1,0:T(8,128)(2,1)}, bf16[2,64,16,128]{3,2,1,0:T(8,128)(2,1)S(1)}, u32[]{:S(2)}) copy-start(bf16[2,64,16,128]{3,2,1,0:T(8,128)(2,1)S(1)} %get-tuple-element.52) | copy-start | bytes 1572868
  68.2 23.7 %copy-start.87 = (pred[4]{0:T(512)(128)(4,1)S(1)}, pred[4]{0:T(512)(128)(4,1)}, u32[]{:S(2)}) copy-start(pred[4]{0:T(512)(128)(4,1)} %get-tuple-element.40) | copy-start | bytes 16
  85.1 48.0 %all-to-all-start.2 = ((bf16[8,128,896]{2,1,0:T(8,128)(2,1)}), bf16[8,128,896]{2,1,0:T(8,128)(2,1)}, u32[]{:S(2)}, u32[]{:S(2)}) async-start(bf16[8,128,896]{2,1,0:T(8,128)(2,1)} %broadcast_select_fusion.6), calls=%async_computation.2 | async-start | bytes 3670016 | tf_op jit(solution)/shard_map/all_to_all | solution.py:126
  133.1 47.3 %all-to-all-start.3 = ((bf16[8,128,896]{2,1,0:T(8,128)(2,1)}), bf16[8,128,896]{2,1,0:T(8,128)(2,1)}, u32[]{:S(2)}, u32[]{:S(2)}) async-start(bf16[8,128,896]{2,1,0:T(8,128)(2,1)} %broadcast_select_fusion.5), calls=%async_computation.3 | async-start | bytes 3670016 | tf_op jit(solution)/shard_map/all_to_all | solution.py:126
  180.4 46.5 %all-to-all-start.4 = ((bf16[8,128,896]{2,1,0:T(8,128)(2,1)}), bf16[8,128,896]{2,1,0:T(8,128)(2,1)}, u32[]{:S(2)}, u32[]{:S(2)}) async-start(bf16[8,128,896]{2,1,0:T(8,128)(2,1)} %broadcast_select_fusion.4), calls=%async_computation.4 | async-start | bytes 3670016 | tf_op jit(solution)/shard_map/all_to_all | solution.py:126
  184.8 350.0 %reduce-scatter.3.cloned.1.call-start = ((), (), s32[]{:S(2)}) async-start(), calls=%async_computation.11 | async-start | bytes 16515072 | tf_op jit(solution)/shard_map/reduce_scatter | solution.py:196
  321.4 47.0 %all-to-all-start.5 = ((bf16[8,128,896]{2,1,0:T(8,128)(2,1)}), bf16[8,128,896]{2,1,0:T(8,128)(2,1)}, u32[]{:S(2)}, u32[]{:S(2)}) async-start(bf16[8,128,896]{2,1,0:T(8,128)(2,1)} %broadcast_select_fusion.3), calls=%async_computation.5 | async-start | bytes 3670016 | tf_op jit(solution)/shard_map/all_to_all | solution.py:178
  358.1 14.9 %copy-start.11 = (bf16[2,16,64,256]{3,2,1,0:T(8,128)(2,1)S(1)}, bf16[2,16,64,256]{3,2,1,0:T(8,128)(2,1)}, u32[]{:S(2)}) copy-start(bf16[2,16,64,256]{3,2,1,0:T(8,128)(2,1)} %copy-done.10) | copy-start | bytes 3145732
  368.3 46.8 %all-to-all-start.6 = ((bf16[8,128,896]{2,1,0:T(8,128)(2,1)}), bf16[8,128,896]{2,1,0:T(8,128)(2,1)}, u32[]{:S(2)}, u32[]{:S(2)}) async-start(bf16[8,128,896]{2,1,0:T(8,128)(2,1)} %broadcast_select_fusion.2), calls=%async_computation.6 | async-start | bytes 3670016 | tf_op jit(solution)/shard_map/all_to_all | solution.py:178
  388.2 44.9 %collective-permute-start.1 = (bf16[2,63,2048]{2,1,0:T(8,128)(2,1)}, bf16[2,63,2048]{2,1,0:T(8,128)(2,1)}, u32[]{:S(2)}, u32[]{:S(2)}) collective-permute-start(bf16[2,63,2048]{2,1,0:T(8,128)(2,1)} %slice.168), channel_id=1, source_target_pairs={{0,1},{1,2},{2,3},{3,4},{4,5},{5,6},{6,7},{8,9},{9,10},{10,11},{11... | collective-permute-start | bytes 1548296 | tf_op jit(solution)/shard_map/ppermute | solution.py:17
  400.2 19.3 %copy-start.7 = (bf16[64,8,16,128]{3,2,1,0:T(8,128)(2,1)S(1)}, bf16[64,8,16,128]{3,2,1,0:T(8,128)(2,1)}, u32[]{:S(2)}) copy-start(bf16[64,8,16,128]{3,2,1,0:T(8,128)(2,1)} %copy-done.6) | copy-start | bytes 6291460
  400.2 19.3 %copy-start.13 = (bf16[2,16,64,256]{3,2,1,0:T(8,128)(2,1)S(1)}, bf16[2,16,64,256]{3,2,1,0:T(8,128)(2,1)}, u32[]{:S(2)}) copy-start(bf16[2,16,64,256]{3,2,1,0:T(8,128)(2,1)} %copy-done.12) | copy-start | bytes 3145732
  415.1 50.1 %all-to-all-start.7 = ((bf16[8,128,896]{2,1,0:T(8,128)(2,1)}), bf16[8,128,896]{2,1,0:T(8,128)(2,1)}, u32[]{:S(2)}, u32[]{:S(2)}) async-start(bf16[8,128,896]{2,1,0:T(8,128)(2,1)} %broadcast_select_fusion.1), calls=%async_computation.7 | async-start | bytes 3670016 | tf_op jit(solution)/shard_map/all_to_all | solution.py:178
  428.0 8.3 %collective-permute-start.3 = (bf16[2,63,2048]{2,1,0:T(8,128)(2,1)S(1)}, bf16[2,63,2048]{2,1,0:T(8,128)(2,1)}, u32[]{:S(2)}, u32[]{:S(2)}) collective-permute-start(bf16[2,63,2048]{2,1,0:T(8,128)(2,1)S(1)} %slice.174), channel_id=1, source_target_pairs={{0,1},{1,2},{2,3},{3,4},{4,5},{5,6},{6,7},{8,9},{9,10},{10,11},{11... | collective-permute-start | bytes 1548296 | tf_op jit(solution)/shard_map/ppermute | solution.py:17
  465.2 48.5 %all-to-all-start.8 = ((bf16[8,128,896]{2,1,0:T(8,128)(2,1)}), bf16[8,128,896]{2,1,0:T(8,128)(2,1)S(1)}, u32[]{:S(2)}, u32[]{:S(2)}) async-start(bf16[8,128,896]{2,1,0:T(8,128)(2,1)} %broadcast_select_fusion), calls=%async_computation.8 | async-start | bytes 3670016 | tf_op jit(solution)/shard_map/all_to_all | solution.py:178
  470.2 114.2 %reduce-scatter.5.cloned.1.call-start = ((), (), s32[]{:S(2)}) async-start(), calls=%async_computation.12 | async-start | bytes 2621440 | tf_op jit(solution)/shard_map/reduce_scatter | solution.py:202
  (81 other events, 265.6 us)
Sparse Core Ops, SparseCore 0:
  295.9 107.3 reduce-scatter.2
  538.0 46.3 reduce-scatter.4

commit v7 on v6

--- a/solution.py
+++ b/solution.py
@@ -1,6 +1,8 @@
 import jax
 import jax.numpy as jnp
 from jax import lax
+from jax.experimental import pallas as pl
+from jax.experimental.pallas import tpu as pltpu
 from jax.sharding import PartitionSpec as P
 
 HD = 128
@@ -19,6 +21,39 @@
 
 def one_hot(index, count):
     return (index[:, None] == jnp.arange(count, dtype=jnp.int32)[None, :]).astype(jnp.int32)
+
+
+def _row_sum_kernel(rows_ref, *refs):
+    part_refs, out_ref = refs[:-1], refs[-1]
+    row = pl.program_id(0)
+    out_ref[...] = jnp.zeros(out_ref.shape, out_ref.dtype)
+    base = 0
+    for part in part_refs:
+
+        def body(s, carry, part=part, base=base):
+            @pl.when(rows_ref[base + s] == row)
+            def _():
+                out_ref[0] += part[s].astype(jnp.float32)
+
+            return carry
+
+        lax.fori_loop(0, part.shape[0], body, 0)
+        base += part.shape[0]
+
+
+def row_sums(rows, parts, row_count):
+    width = parts[0].shape[1:]
+    whole = lambda r, rows_ref: (0, 0, 0)
+    return pl.pallas_call(
+        _row_sum_kernel,
+        grid_spec=pltpu.PrefetchScalarGridSpec(
+            num_scalar_prefetch=1,
+            grid=(row_count,),
+            in_specs=[pl.BlockSpec(p.shape, whole) for p in parts],
+            out_specs=pl.BlockSpec((1,) + width, lambda r, rows_ref: (r, 0, 0)),
+        ),
+        out_shape=jax.ShapeDtypeStruct((row_count,) + width, jnp.float32),
+    )(rows, *parts)
 
 
 def attend_chunk(query_blocks, grad_blocks, neighbours, key_weight, value_weight, head_count):
@@ -172,17 +207,21 @@
     if chunk_count > 1:
         weight_terms = weight_term(0, chunk_count - 1) + weight_terms
 
-    database_grad = None
+    plane_sums = lax.psum_scatter(
+        weight_terms.reshape(seq_total, shard_count * enc_share, 2 * feat_width),
+        "seq",
+        scatter_dimension=0,
+        tiled=True,
+    )
+    returned_parts = []
     for g in range(chunk_count):
         sent, _ = lax.optimization_barrier((grads_out[g], link))
+        if g == chunk_count // 2:
+            sent, plane_sums = lax.optimization_barrier((sent, plane_sums))
         link = lax.all_to_all(sent, "dp", split_axis=0, concat_axis=0, tiled=True)
-        row_hits = one_hot(arrived[:, g, :].reshape(chunk_slots), database.shape[0])
-        part = jnp.sum(
-            row_hits.astype(jnp.float32)[:, :, None, None]
-            * link.astype(jnp.float32)[:, None, :, :],
-            axis=0,
-        )
-        database_grad = part if database_grad is None else database_grad + part
+        returned_parts.append(link)
+    slot_rows = arrived.transpose(1, 0, 2).reshape(-1)
+    database_grad = row_sums(slot_rows, returned_parts, database.shape[0])
 
     context_shift = jnp.concatenate(context_parts, axis=0).reshape(seq_count, seq_span, feat_width)
     query_shift = jnp.concatenate(query_parts, axis=0).reshape(seq_count, seq_span, feat_width)
@@ -193,12 +232,6 @@
     context = jnp.concatenate([prior_context, context_shift[:, :keep_rows]], axis=1)
     query_grad = jnp.concatenate([prior_grads, query_shift[:, :keep_rows]], axis=1)
 
-    plane_sums = lax.psum_scatter(
-        weight_terms.reshape(seq_total, shard_count * enc_share, 2 * feat_width),
-        "seq",
-        scatter_dimension=0,
-        tiled=True,
-    )
     owned_grads = lax.psum_scatter(
         plane_sums.reshape(shard_count, enc_share, 2 * feat_width),
         "dp",

time: 601 us -> 563 us (0.937)
  other arithmetic: 143 us -> 27 us
  waiting for transfers between devices: 74.5 us -> 138 us
  Pallas kernels: 0 us -> 25.4 us
  local copies, waits for them, and re-layouts: 168 us -> 155 us
    all_to_all x4, waiting for transfers between devices: 27.4 us -> 114 us  [local(): link = lax.all_to_all(sent, 'dp', split_axis=0, concat_axis=0, tiled=True)]
    reduce_sum x4 -> x0, other arithmetic: 75.5 us -> none  [local(): jnp.sum(row_hits.astype(jnp.float32)[:, :, None, None] * link.astype(jnp....]
    pallas_call x0 -> x1, Pallas kernels: none -> 25.4 us  [row_sums(): pl.pallas_call(_row_sum_kernel, grid_spec=pltpu.PrefetchScalarGridSpec(nu...]
    add x1 -> x0, other arithmetic: 24.8 us -> none  [local(): database_grad = part if database_grad is None else database_grad + part]
    reduce_scatter x1, waiting for transfers between devices: 21.7 us -> 0.01 us  [local(): lax.psum_scatter(plane_sums.reshape(shard_count, enc_share, 2 * feat_widt...]
    convert_element_type x8 -> x0, other arithmetic: 13.1 us -> none  [the longest x4 12.8 us: local(): link.astype(jnp.float32)[:, None, :, :]]
    gather x4, local copies, waits for them, and re-layouts: 10.4 us -> 3.41 us  [local(): grads_out.append(jnp.take(padded, slot_refs[g], axis=0))]
    unnamed x191 -> x173, local copies, waits for them, and re-layouts: 49.4 us -> 43.9 us
  transfers between devices with their start and end apart: 15 -> 15, of which waited for: 8 -> 8; matrix products, arithmetic and copies ran while one was open for 60% -> 43% of each run, Pallas kernels for 0% -> 0%
where the time goes in v7:
time: 563 us; the launch traced here: 555 us
  local copies, waits for them, and re-layouts  155 us (28%)
  matrix products  144 us (26%)
  waiting for transfers between devices  138 us (25%)
  starting transfers between devices  50.2 us (9%)
  other arithmetic  27 us (5%)
  Pallas kernels  25.4 us (5%)
  between operations  15.7 us (3%)
    all_to_all x4, waiting for transfers between devices, local(): link = lax.all_to_all(sent, 'dp', split_axis=0, concat_axis=0, tiled=True)  114 us
    unnamed x173, local copies, waits for them, and re-layouts  43.9 us
    dot_general x4, matrix products, attend_chunk(): jnp.einsum('pz,xz->px', proj_grads, both_weights, preferred_element_type=...  37.1 us
    dot_general x2, matrix products, weight_term(): jnp.einsum('px,pz->xz', jnp.concatenate(seq_major[first:last], axis=0), j...  28.1 us
    pallas_call x1, Pallas kernels, row_sums(): pl.pallas_call(_row_sum_kernel, grid_spec=pltpu.PrefetchScalarGridSpec(nu...  25.4 us
    all_to_all x4, waiting for transfers between devices, local(): link = lax.all_to_all(rows, 'dp', split_axis=0, concat_axis=0, tiled=True)  23.6 us
    dot_general x4, matrix products, attend_chunk(): jnp.dot(neighbours, key_weight, preferred_element_type=jnp.float32)  22.3 us
    all_to_all x4, starting transfers between devices, local(): link = lax.all_to_all(rows, 'dp', split_axis=0, concat_axis=0, tiled=True)  18.7 us
  transfers between devices with their start and end apart: 15, of which 8 were waited for; matrix products, arithmetic and copies ran while one was open for 43% of the time, Pallas kernels for 0%

profile of v7, /device:TPU:0, one launch (start us, length us, event | category | flops | bytes accessed | tf_op | source)
XLA Modules:
  0.0 555.0 jit_solution(11325185354259821998)
XLA Ops:
  13.4 6.3 %all-to-all-start = ((s32[4,4,2]{1,2,0:T(2,128)}), s32[4,4,2]{1,2,0:T(2,128)S(1)}, u32[]{:S(2)}, u32[]{:S(2)}) async-start(s32[4,4,2]{1,2,0:T(2,128)} %copy.146), calls=%async_computation | async-start | bytes 8192 | tf_op jit(solution)/shard_map/all_to_all | solution.py:144
  34.6 5.1 all-to-all-start.1
  43.6 5.1 gather_fusion.3
  48.7 5.1 gather_fusion.5
  66.4 16.9 %all-to-all-done.1 = bf16[8,128,896]{2,1,0:T(8,128)(2,1)} async-done(((bf16[8,128,896]{2,1,0:T(8,128)(2,1)}), bf16[8,128,896]{2,1,0:T(8,128)(2,1)}, u32[]{:S(2)}, u32[]{:S(2)}) %all-to-all-start.1) | async-done | bytes 1835040 | tf_op jit(solution)/shard_map/all_to_all | solution.py:161
  83.3 4.6 all-to-all-start.2
  93.9 4.7 fusion.55
  131.2 4.6 all-to-all-start.3
  139.4 5.8 %fusion.57 = bf16[64,8,16,128]{3,1,2,0:T(8,128)(2,1)} fusion(bf16[512,896]{1,0:T(8,128)(2,1)S(1)} %bitcast.200, bf16[896,2048]{1,0:T(8,128)(2,1)} %param.16), kind=kOutput, calls=%fused_computation.117 | convolution fusion | flops 1880096768 | bytes 6684672 | tf_op jit(solution)/shard_map/dot_general | solution.py:62
  186.7 5.8 %fusion.59 = bf16[64,8,16,128]{3,1,2,0:T(8,128)(2,1)} fusion(bf16[512,896]{1,0:T(8,128)(2,1)S(1)} %bitcast.202, bf16[896,2048]{1,0:T(8,128)(2,1)} %param.16), kind=kOutput, calls=%fused_computation.119 | convolution fusion | flops 1880096768 | bytes 6684672 | tf_op jit(solution)/shard_map/dot_general | solution.py:62
  228.6 5.8 %fusion.61 = bf16[64,8,16,128]{3,1,2,0:T(8,128)(2,1)} fusion(bf16[512,896]{1,0:T(8,128)(2,1)S(1)} %bitcast.204, bf16[896,2048]{1,0:T(8,128)(2,1)} %param.16), kind=kOutput, calls=%fused_computation.121 | convolution fusion | flops 1880096768 | bytes 6684672 | tf_op jit(solution)/shard_map/dot_general | solution.py:62
  249.0 4.5 copy.189
  265.0 7.6 %fusion.152 = f32[896,4096]{1,0:T(8,128)} fusion(bf16[512,896]{0,1:T(8,128)(2,1)S(1)} %reshape.252, bf16[512,4096]{1,0:T(8,128)(2,1)S(1)} %bitcast_dynamic-update-slice_fusion), kind=kOutput, calls=%fused_computation.248 | convolution fusion | flops 3758096384 | bytes 19791872 | tf_op jit(solution)/shard_map/px,pz->xz/dot_general | solution.py:199
  272.6 20.5 %fusion.6 = f32[896,4096]{1,0:T(8,128)} fusion(f32[896,4096]{1,0:T(8,128)} %fusion.152, bf16[512,4096]{1,0:T(8,128)(2,1)} %bitcast_dynamic-update-slice_fusion.2, bf16[512,4096]{1,0:T(8,128)(2,1)} %bitcast_dynamic-update-slice_fusion.4, bf16[512,4096]{1,0:T(8,128)(2,1)} %bitcast_dynamic-update-slice_fusion.6, bf16[512,896]{0,1:T(8,128)(2,1)S(1)} %copy-done.59, ...), kind=kOutput, calls=%fused_computation.18 | convolution fusion | flops 11323965440 | bytes 44695552 | tf_op jit(solution)/shard_map/px,pz->xz/dot_general | solution.py:199
  297.5 9.7 %convolution_convert_fusion.11 = bf16[512,896]{1,0:T(8,128)(2,1)S(1)} fusion(bf16[512,4096]{1,0:T(8,128)(2,1)} %bitcast_dynamic-update-slice_fusion.6, bf16[896,4096]{1,0:T(8,128)(2,1)S(1)} %constant_dynamic-update-slice_fusion), kind=kOutput, calls=%fused_computation.125 | convolution fusion | flops 3758555136 | bytes 12451840 | tf_op jit(solution)/shard_map/pz,xz->px/dot_general | solution.py:104
  314.1 9.6 %convolution_convert_fusion.10 = bf16[512,896]{1,0:T(8,128)(2,1)S(1)} fusion(bf16[512,4096]{1,0:T(8,128)(2,1)} %bitcast_dynamic-update-slice_fusion.4, bf16[896,4096]{1,0:T(8,128)(2,1)} %copy-done.54), kind=kOutput, calls=%fused_computation.124 | convolution fusion | flops 3758555136 | bytes 12451840 | tf_op jit(solution)/shard_map/pz,xz->px/dot_general | solution.py:104
  326.1 30.0 %all-to-all-done.5.refs_0_ = bf16[8,128,896]{2,1,0:T(8,128)(2,1)} async-done(((bf16[8,128,896]{2,1,0:T(8,128)(2,1)}), bf16[8,128,896]{2,1,0:T(8,128)(2,1)}, u32[]{:S(2)}, u32[]{:S(2)}) %all-to-all-start.5) | async-done | bytes 1835040 | tf_op jit(solution)/shard_map/all_to_all | solution.py:221
  356.1 4.6 all-to-all-start.6
  364.0 8.9 %convolution_convert_fusion.9 = bf16[512,896]{1,0:T(8,128)(2,1)S(1)} fusion(bf16[512,4096]{1,0:T(8,128)(2,1)} %bitcast_dynamic-update-slice_fusion.2, bf16[896,4096]{1,0:T(8,128)(2,1)} %copy-done.54), kind=kOutput, calls=%fused_computation.123 | convolution fusion | flops 3758555136 | bytes 12451840 | tf_op jit(solution)/shard_map/pz,xz->px/dot_general | solution.py:104
  375.4 27.3 %all-to-all-done.6.refs_1_ = bf16[8,128,896]{2,1,0:T(8,128)(2,1)} async-done(((bf16[8,128,896]{2,1,0:T(8,128)(2,1)}), bf16[8,128,896]{2,1,0:T(8,128)(2,1)}, u32[]{:S(2)}, u32[]{:S(2)}) %all-to-all-start.6) | async-done | bytes 1835040 | tf_op jit(solution)/shard_map/all_to_all | solution.py:221
  416.7 8.9 %convolution_convert_fusion.8 = bf16[512,896]{1,0:T(8,128)(2,1)S(1)} fusion(bf16[512,4096]{1,0:T(8,128)(2,1)} %copy-done.56, bf16[896,4096]{1,0:T(8,128)(2,1)} %copy-done.54), kind=kOutput, calls=%fused_computation.122 | convolution fusion | flops 3758555136 | bytes 12451840 | tf_op jit(solution)/shard_map/pz,xz->px/dot_general | solution.py:104
  428.0 50.2 %all-to-all-done.7.refs_2_ = bf16[8,128,896]{2,1,0:T(8,128)(2,1)} async-done(((bf16[8,128,896]{2,1,0:T(8,128)(2,1)}), bf16[8,128,896]{2,1,0:T(8,128)(2,1)}, u32[]{:S(2)}, u32[]{:S(2)}) %all-to-all-start.7) | async-done | bytes 1835040 | tf_op jit(solution)/shard_map/all_to_all | solution.py:221
  516.0 6.6 %all-to-all-done.8.refs_3_ = bf16[8,128,896]{2,1,0:T(8,128)(2,1)} async-done(((bf16[8,128,896]{2,1,0:T(8,128)(2,1)}), bf16[8,128,896]{2,1,0:T(8,128)(2,1)}, u32[]{:S(2)}, u32[]{:S(2)}) %all-to-all-start.8) | async-done | bytes 1835040 | tf_op jit(solution)/shard_map/all_to_all | solution.py:221
  522.6 25.4 %shard_map.110 = f32[32,128,896]{2,1,0:T(8,128)} custom-call(s32[32]{0:T(128)} %reshape.239.rows_ref, bf16[8,128,896]{2,1,0:T(8,128)(2,1)} %all-to-all-done.5.refs_0_, bf16[8,128,896]{2,1,0:T(8,128)(2,1)} %all-to-all-done.6.refs_1_, bf16[8,128,896]{2,1,0:T(8,128)(2,1)} %all-to-all-done.7.refs_2_, bf16[8,128,896]{2,1,0:T(8,128)(2,1)} %all-to-all-done.8.refs_3_), custom_call_target="tpu_custom_call" | custom-call | tf_op jit(solution)/shard_map/pallas_call | solution.py:47
  (381 shorter events, 255.8 us)
Async XLA Ops:
  7.2 19.1 %copy-start.43 = (bf16[2,256,2048]{2,1,0:T(8,128)(2,1)S(1)}, bf16[2,256,2048]{2,1,0:T(8,128)(2,1)}, u32[]{:S(2)}) copy-start(bf16[2,256,2048]{2,1,0:T(8,128)(2,1)} %param.13) | copy-start | bytes 6291460
  13.4 14.9 %all-to-all-start = ((s32[4,4,2]{1,2,0:T(2,128)}), s32[4,4,2]{1,2,0:T(2,128)S(1)}, u32[]{:S(2)}, u32[]{:S(2)}) async-start(s32[4,4,2]{1,2,0:T(2,128)} %copy.146), calls=%async_computation | async-start | bytes 8192 | tf_op jit(solution)/shard_map/all_to_all | solution.py:144
  21.7 39.9 %collective-permute-start.2 = (bf16[2,63,2048]{2,1,0:T(8,128)(2,1)}, bf16[2,63,2048]{2,1,0:T(8,128)(2,1)}, u32[]{:S(2)}, u32[]{:S(2)}) collective-permute-start(bf16[2,63,2048]{2,1,0:T(8,128)(2,1)} %slice.123), channel_id=1, source_target_pairs={{1,0},{2,1},{3,2},{4,3},{5,4},{6,5},{7,6},{9,8},{10,9},{11,10},{12... | collective-permute-start | bytes 1548296 | tf_op jit(solution)/shard_map/ppermute | solution.py:19
  25.0 34.6 %collective-permute-start = (bf16[2,63,2048]{2,1,0:T(8,128)(2,1)}, bf16[2,63,2048]{2,1,0:T(8,128)(2,1)}, u32[]{:S(2)}, u32[]{:S(2)}) collective-permute-start(bf16[2,63,2048]{2,1,0:T(8,128)(2,1)} %slice.113), channel_id=1, source_target_pairs={{1,0},{2,1},{3,2},{4,3},{5,4},{6,5},{7,6},{9,8},{10,9},{11,10},{12... | collective-permute-start | bytes 1548296 | tf_op jit(solution)/shard_map/ppermute | solution.py:19
  34.6 48.8 %all-to-all-start.1 = ((bf16[8,128,896]{2,1,0:T(8,128)(2,1)}), bf16[8,128,896]{2,1,0:T(8,128)(2,1)}, u32[]{:S(2)}, u32[]{:S(2)}) async-start(bf16[8,128,896]{2,1,0:T(8,128)(2,1)} %broadcast_select_fusion.7), calls=%async_computation.1 | async-start | bytes 3670016 | tf_op jit(solution)/shard_map/all_to_all | solution.py:161
  83.3 47.9 %all-to-all-start.2 = ((bf16[8,128,896]{2,1,0:T(8,128)(2,1)}), bf16[8,128,896]{2,1,0:T(8,128)(2,1)}, u32[]{:S(2)}, u32[]{:S(2)}) async-start(bf16[8,128,896]{2,1,0:T(8,128)(2,1)} %broadcast_select_fusion.6), calls=%async_computation.2 | async-start | bytes 3670016 | tf_op jit(solution)/shard_map/all_to_all | solution.py:161
  131.2 47.1 %all-to-all-start.3 = ((bf16[8,128,896]{2,1,0:T(8,128)(2,1)}), bf16[8,128,896]{2,1,0:T(8,128)(2,1)}, u32[]{:S(2)}, u32[]{:S(2)}) async-start(bf16[8,128,896]{2,1,0:T(8,128)(2,1)} %broadcast_select_fusion.5), calls=%async_computation.3 | async-start | bytes 3670016 | tf_op jit(solution)/shard_map/all_to_all | solution.py:161
  178.4 46.5 %all-to-all-start.4 = ((bf16[8,128,896]{2,1,0:T(8,128)(2,1)}), bf16[8,128,896]{2,1,0:T(8,128)(2,1)}, u32[]{:S(2)}, u32[]{:S(2)}) async-start(bf16[8,128,896]{2,1,0:T(8,128)(2,1)} %broadcast_select_fusion.4), calls=%async_computation.4 | async-start | bytes 3670016 | tf_op jit(solution)/shard_map/all_to_all | solution.py:161
  182.8 220.0 %reduce-scatter.3.cloned.1.call-start = ((), (), s32[]{:S(2)}) async-start(), calls=%async_computation.11 | async-start | bytes 16515072 | tf_op jit(solution)/shard_map/reduce_scatter | solution.py:210
  309.6 46.5 %all-to-all-start.5 = ((bf16[8,128,896]{2,1,0:T(8,128)(2,1)}), bf16[8,128,896]{2,1,0:T(8,128)(2,1)}, u32[]{:S(2)}, u32[]{:S(2)}) async-start(bf16[8,128,896]{2,1,0:T(8,128)(2,1)} %broadcast_select_fusion.3), calls=%async_computation.5 | async-start | bytes 3670016 | tf_op jit(solution)/shard_map/all_to_all | solution.py:221
  326.1 34.5 %copy-start.75 = (s32[8]{0:T(128)S(1)}, s32[8]{0:T(128)}, u32[]{:S(2)}) copy-start(s32[8]{0:T(128)} %get-tuple-element.40) | copy-start | bytes 100
  326.1 34.5 %copy-start.76 = (s32[8]{0:T(128)S(1)}, s32[8]{0:T(128)}, u32[]{:S(2)}) copy-start(s32[8]{0:T(128)} %get-tuple-element.36) | copy-start | bytes 100
  326.1 34.6 %copy-start.18 = (f32[2,16,64,256]{3,2,1,0:T(8,128)S(1)}, f32[2,16,64,256]{3,2,1,0:T(8,128)}, u32[]{:S(2)}) copy-start(f32[2,16,64,256]{3,2,1,0:T(8,128)} %copy-done.17) | copy-start | bytes 6291460
  326.1 34.6 %copy-start.70 = (f32[2,16,64]{2,1,0:T(8,128)S(1)}, f32[2,16,64]{2,1,0:T(8,128)}, u32[]{:S(2)}) copy-start(f32[2,16,64]{2,1,0:T(8,128)} %copy-done.69) | copy-start | bytes 24580
  356.1 46.7 %all-to-all-start.6 = ((bf16[8,128,896]{2,1,0:T(8,128)(2,1)}), bf16[8,128,896]{2,1,0:T(8,128)(2,1)}, u32[]{:S(2)}, u32[]{:S(2)}) async-start(bf16[8,128,896]{2,1,0:T(8,128)(2,1)} %broadcast_select_fusion.2), calls=%async_computation.6 | async-start | bytes 3670016 | tf_op jit(solution)/shard_map/all_to_all | solution.py:221
  375.4 31.8 %copy-start.1 = (bf16[64,8,16,128]{3,2,1,0:T(8,128)(2,1)S(1)}, bf16[64,8,16,128]{3,2,1,0:T(8,128)(2,1)}, u32[]{:S(2)}) copy-start(bf16[64,8,16,128]{3,2,1,0:T(8,128)(2,1)} %copy-done) | copy-start | bytes 6291460
  375.4 31.8 %copy-start.9 = (bf16[2,16,64,256]{3,2,1,0:T(8,128)(2,1)S(1)}, bf16[2,16,64,256]{3,2,1,0:T(8,128)(2,1)}, u32[]{:S(2)}) copy-start(bf16[2,16,64,256]{3,2,1,0:T(8,128)(2,1)} %copy-done.8) | copy-start | bytes 3145732
  402.8 75.4 %all-to-all-start.7 = ((bf16[8,128,896]{2,1,0:T(8,128)(2,1)}), bf16[8,128,896]{2,1,0:T(8,128)(2,1)}, u32[]{:S(2)}, u32[]{:S(2)}) async-start(bf16[8,128,896]{2,1,0:T(8,128)(2,1)} %broadcast_select_fusion.1), calls=%async_computation.8 | async-start | bytes 3670016 | tf_op jit(solution)/shard_map/all_to_all | solution.py:221
  407.2 107.0 %reduce-scatter.5.cloned.1.call-start = ((), (), s32[]{:S(2)}) async-start(), calls=%async_computation.12 | async-start | bytes 2621440 | tf_op jit(solution)/shard_map/reduce_scatter | solution.py:235
  428.0 54.6 %copy-start.5 = (bf16[64,8,16,128]{3,2,1,0:T(8,128)(2,1)S(1)}, bf16[64,8,16,128]{3,2,1,0:T(8,128)(2,1)}, u32[]{:S(2)}) copy-start(bf16[64,8,16,128]{3,2,1,0:T(8,128)(2,1)} %copy-done.4) | copy-start | bytes 6291460
  428.0 54.6 %copy-start.13 = (bf16[2,16,64,256]{3,2,1,0:T(8,128)(2,1)S(1)}, bf16[2,16,64,256]{3,2,1,0:T(8,128)(2,1)}, u32[]{:S(2)}) copy-start(bf16[2,16,64,256]{3,2,1,0:T(8,128)(2,1)} %copy-done.12) | copy-start | bytes 3145732
  478.2 44.4 %all-to-all-start.8 = ((bf16[8,128,896]{2,1,0:T(8,128)(2,1)}), bf16[8,128,896]{2,1,0:T(8,128)(2,1)}, u32[]{:S(2)}, u32[]{:S(2)}) async-start(bf16[8,128,896]{2,1,0:T(8,128)(2,1)} %broadcast_select_fusion), calls=%async_computation.9 | async-start | bytes 3670016 | tf_op jit(solution)/shard_map/all_to_all | solution.py:221
  496.3 11.9 %collective-permute-start.1 = (bf16[2,63,2048]{2,1,0:T(8,128)(2,1)}, bf16[2,63,2048]{2,1,0:T(8,128)(2,1)}, u32[]{:S(2)}, u32[]{:S(2)}) collective-permute-start(bf16[2,63,2048]{2,1,0:T(8,128)(2,1)} %slice.164), channel_id=1, source_target_pairs={{0,1},{1,2},{2,3},{3,4},{4,5},{5,6},{6,7},{8,9},{9,10},{10,11},{11... | collective-permute-start | bytes 1548296 | tf_op jit(solution)/shard_map/ppermute | solution.py:19
  505.4 7.0 %collective-permute-start.3 = (bf16[2,63,2048]{2,1,0:T(8,128)(2,1)S(1)}, bf16[2,63,2048]{2,1,0:T(8,128)(2,1)S(1)}, u32[]{:S(2)}, u32[]{:S(2)}) collective-permute-start(bf16[2,63,2048]{2,1,0:T(8,128)(2,1)S(1)} %slice.170), channel_id=1, source_target_pairs={{0,1},{1,2},{2,3},{3,4},{4,5},{5,6},{6,7},{8,9},{9,10},{10,11},{11... | collective-permute-start | bytes 1548296 | tf_op jit(solution)/shard_map/ppermute | solution.py:19
  (72 other events, 269.0 us)
Sparse Core Ops, SparseCore 0:
  293.3 105.2 reduce-scatter.2
  416.8 64.2 reduce-scatter.4

commit v8 on v7

--- a/solution.py
+++ b/solution.py
@@ -163,13 +163,31 @@
 
     context_parts = []
     query_parts = []
+    returned_parts = []
     grads_out = []
     seq_major = []
     proj_parts = []
+
+    def weight_term(first, last):
+        return jnp.einsum(
+            "px,pz->xz",
+            jnp.concatenate(seq_major[first:last], axis=0),
+            jnp.concatenate(proj_parts[first:last], axis=0),
+            preferred_element_type=jnp.float32,
+        )
+
     for g in range(chunk_count):
         incoming = fetched[g][1]
         if g + 1 < chunk_count:
             incoming, _ = lax.optimization_barrier((incoming, fetched[g + 1][0]))
+        if g >= 1:
+            incoming, _ = lax.optimization_barrier((incoming, grads_out[g - 1]))
+        if g >= 1 and g == chunk_count - 1:
+            early_terms = weight_term(0, g)
+            sent, _ = lax.optimization_barrier((grads_out[0], link))
+            link = lax.all_to_all(sent, "dp", split_axis=0, concat_axis=0, tiled=True)
+            returned_parts.append(link)
+            incoming, early_terms, _ = lax.optimization_barrier((incoming, early_terms, sent))
         neighbours = jnp.take(incoming, slot_indices[g], axis=0).reshape(
             chunk_refs * NB_LEN, ENC
         )
@@ -195,17 +213,9 @@
         )
         proj_parts.append(proj_grads)
 
-    def weight_term(first, last):
-        return jnp.einsum(
-            "px,pz->xz",
-            jnp.concatenate(seq_major[first:last], axis=0),
-            jnp.concatenate(proj_parts[first:last], axis=0),
-            preferred_element_type=jnp.float32,
-        )
-
     weight_terms = weight_term(chunk_count - 1, chunk_count)
     if chunk_count > 1:
-        weight_terms = weight_term(0, chunk_count - 1) + weight_terms
+        weight_terms = early_terms + weight_terms
 
     plane_sums = lax.psum_scatter(
         weight_terms.reshape(seq_total, shard_count * enc_share, 2 * feat_width),
@@ -213,8 +223,7 @@
         scatter_dimension=0,
         tiled=True,
     )
-    returned_parts = []
-    for g in range(chunk_count):
+    for g in range(len(returned_parts), chunk_count):
         sent, _ = lax.optimization_barrier((grads_out[g], link))
         if g == chunk_count // 2:
             sent, plane_sums = lax.optimization_barrier((sent, plane_sums))

time: 563 us -> 609 us (1.082)
  blocking collectives: 0 us -> 46.8 us
  other arithmetic: 27 us -> 35.7 us
    all_to_all x0 -> x1, blocking collectives: none -> 46.8 us  [local(): link = lax.all_to_all(sent, 'dp', split_axis=0, concat_axis=0, tiled=True)]
    all_to_all x4 -> x3, waiting for transfers between devices: 114 us -> 97.5 us  [local(): link = lax.all_to_all(sent, 'dp', split_axis=0, concat_axis=0, tiled=True)]
    reduce_scatter x1, waiting for transfers between devices: 0.01 us -> 12.4 us  [local(): lax.psum_scatter(weight_terms.reshape(seq_total, shard_count * enc_share,...]
    all_to_all x4, waiting for transfers between devices: 23.6 us -> 30 us  [local(): link = lax.all_to_all(rows, 'dp', split_axis=0, concat_axis=0, tiled=True)]
    unnamed x173 -> x175, local copies, waits for them, and re-layouts: 43.9 us -> 38.7 us
    all_to_all x4 -> x3, starting transfers between devices: 17.8 us -> 13.8 us  [local(): link = lax.all_to_all(sent, 'dp', split_axis=0, concat_axis=0, tiled=True)]
  transfers between devices with their start and end apart: 15 -> 14, of which waited for: 8 -> 5; matrix products, arithmetic and copies ran while one was open for 43% -> 42% of each run, Pallas kernels for 0% -> 0%
where the time goes in v8:
time: 609 us; the launch traced here: 601 us
  local copies, waits for them, and re-layouts  150 us (25%)
  waiting for transfers between devices  140 us (23%)
  matrix products  140 us (23%)
  starting transfers between devices  47.7 us (8%)
  blocking collectives  46.8 us (8%)
  other arithmetic  35.7 us (6%)
  Pallas kernels  25.3 us (4%)
  between operations  15.6 us (3%)
    all_to_all x3, waiting for transfers between devices, local(): link = lax.all_to_all(sent, 'dp', split_axis=0, concat_axis=0, tiled=True)  97.5 us
    all_to_all x1, blocking collectives, local(): link = lax.all_to_all(sent, 'dp', split_axis=0, concat_axis=0, tiled=True)  46.8 us
    unnamed x175, local copies, waits for them, and re-layouts  38.7 us
    dot_general x4, matrix products, attend_chunk(): jnp.einsum('pz,xz->px', proj_grads, both_weights, preferred_element_type=...  33.5 us
    dot_general x2, matrix products, weight_term(): jnp.einsum('px,pz->xz', jnp.concatenate(seq_major[first:last], axis=0), j...  30.3 us
    all_to_all x4, waiting for transfers between devices, local(): link = lax.all_to_all(rows, 'dp', split_axis=0, concat_axis=0, tiled=True)  30 us
    pallas_call x1, Pallas kernels, row_sums(): pl.pallas_call(_row_sum_kernel, grid_spec=pltpu.PrefetchScalarGridSpec(nu...  25.3 us
    dot_general x4, matrix products, attend_chunk(): jnp.dot(neighbours, key_weight, preferred_element_type=jnp.float32)  22.3 us
  transfers between devices with their start and end apart: 14, of which 5 were waited for; matrix products, arithmetic and copies ran while one was open for 42% of the time, Pallas kernels for 0%

profile of v8, /device:TPU:0, one launch (start us, length us, event | category | flops | bytes accessed | tf_op | source)
XLA Modules:
  0.0 601.3 jit_solution(11878404299666759522)
XLA Ops:
  13.3 6.3 %all-to-all-start = ((s32[4,4,2]{1,2,0:T(2,128)}), s32[4,4,2]{1,2,0:T(2,128)S(1)}, u32[]{:S(2)}, u32[]{:S(2)}) async-start(s32[4,4,2]{1,2,0:T(2,128)} %copy.146), calls=%async_computation | async-start | bytes 8192 | tf_op jit(solution)/shard_map/all_to_all | solution.py:144
  36.5 5.1 gather_fusion.3
  45.5 5.1 gather_fusion.1
  50.6 5.1 gather_fusion
  58.6 5.1 all-to-all-start.1
  77.3 30.0 %all-to-all-done.1 = bf16[8,128,896]{2,1,0:T(8,128)(2,1)} async-done(((bf16[8,128,896]{2,1,0:T(8,128)(2,1)}), bf16[8,128,896]{2,1,0:T(8,128)(2,1)}, u32[]{:S(2)}, u32[]{:S(2)}) %all-to-all-start.1) | async-done | bytes 1835040 | tf_op jit(solution)/shard_map/all_to_all | solution.py:161
  115.5 5.8 fusion.52
  150.2 8.4 %convolution_convert_fusion.11 = bf16[512,896]{1,0:T(8,128)(2,1)S(1)} fusion(bf16[512,4096]{1,0:T(8,128)(2,1)S(1)} %bitcast_dynamic-update-slice_fusion.6, bf16[896,4096]{1,0:T(8,128)(2,1)} %copy-done.57), kind=kOutput, calls=%fused_computation.125 | convolution fusion | flops 3758555136 | bytes 12451840 | tf_op jit(solution)/shard_map/pz,xz->px/dot_general | solution.py:104
  161.1 5.1 all-to-all-start.3
  169.7 5.8 fusion.54
  204.6 8.4 %convolution_convert_fusion.10 = bf16[512,896]{1,0:T(8,128)(2,1)S(1)} fusion(bf16[512,4096]{1,0:T(8,128)(2,1)S(1)} %bitcast_dynamic-update-slice_fusion.4, bf16[896,4096]{1,0:T(8,128)(2,1)} %copy-done.57), kind=kOutput, calls=%fused_computation.124 | convolution fusion | flops 3758555136 | bytes 12451840 | tf_op jit(solution)/shard_map/pz,xz->px/dot_general | solution.py:104
  215.5 5.1 all-to-all-start.4
  223.0 4.8 fusion.56
  254.3 7.9 %convolution_convert_fusion.9 = bf16[512,896]{1,0:T(8,128)(2,1)} fusion(bf16[512,4096]{1,0:T(8,128)(2,1)S(1)} %bitcast_dynamic-update-slice_fusion.2, bf16[896,4096]{1,0:T(8,128)(2,1)} %copy-done.57), kind=kOutput, calls=%fused_computation.123 | convolution fusion | flops 3758555136 | bytes 12451840 | tf_op jit(solution)/shard_map/pz,xz->px/dot_general | solution.py:104
  268.5 18.1 %fusion = f32[896,4096]{1,0:T(8,128)} fusion(bf16[512,4096]{1,0:T(8,128)(2,1)} %copy-done.61, bf16[512,4096]{1,0:T(8,128)(2,1)} %copy-done.60, bf16[512,4096]{1,0:T(8,128)(2,1)} %copy-done.59, bf16[512,896]{0,1:T(8,128)(2,1)} %reshape.245, bf16[512,896]{0,1:T(8,128)(2,1)} %reshape.244, bf16[512,896]{0,1:T(8,128)(2,1)S(1)} %copy-done.62), kind=kOutput, calls=%fused_computation.12 | convolution fusion | flops 11320295424 | bytes 30015488 | tf_op jit(solution)/shard_map/px,pz->xz/dot_general | solution.py:172
  290.6 5.8 fusion.58
  326.2 12.2 %convolution_add_fusion = f32[896,4096]{1,0:T(8,128)} fusion(f32[896,4096]{1,0:T(8,128)} %fusion, bf16[512,896]{0,1:T(8,128)(2,1)S(1)} %copy-done.35, bf16[512,4096]{1,0:T(8,128)(2,1)S(1)} %bitcast_dynamic-update-slice_fusion), kind=kOutput, calls=%fused_computation.18 | convolution fusion | flops 3761766400 | bytes 34471936 | tf_op jit(solution)/shard_map/px,pz->xz/dot_general | solution.py:172
  339.8 46.8 %all_to_all.45.refs_0_ = bf16[8,128,896]{2,1,0:T(8,128)(2,1)} all-to-all(bf16[8,128,896]{2,1,0:T(8,128)(2,1)S(1)} %copy-done.30), channel_id=1, replica_groups=mesh['dp'=4,'seq'=8] {'dp'}, dimensions={0} | all-to-all | bytes 3670016 | tf_op jit(solution)/shard_map/all_to_all | solution.py:188
  394.8 38.2 %all-to-all-done.6.refs_1_ = bf16[8,128,896]{2,1,0:T(8,128)(2,1)} async-done(((bf16[8,128,896]{2,1,0:T(8,128)(2,1)}), bf16[8,128,896]{2,1,0:T(8,128)(2,1)}, u32[]{:S(2)}, u32[]{:S(2)}) %all-to-all-start.6) | async-done | bytes 1835040 | tf_op jit(solution)/shard_map/all_to_all | solution.py:230
  433.0 12.4 %reduce-scatter.3.cloned.1.call-done = f32[1,112,4096]{2,1,0:T(8,128)} async-done(((f32[8,112,4096]{2,1,0:T(8,128)}), f32[1,112,4096]{2,1,0:T(8,128)}) %reduce-scatter.3.cloned.1.call-update) | async-done | bytes 1835024 | tf_op jit(solution)/shard_map/reduce_scatter | solution.py:220
  459.4 8.9 %convolution_convert_fusion.8 = bf16[512,896]{1,0:T(8,128)(2,1)S(1)} fusion(bf16[512,4096]{1,0:T(8,128)(2,1)} %copy-done.16, bf16[896,4096]{1,0:T(8,128)(2,1)} %copy-done.57), kind=kOutput, calls=%fused_computation.122 | convolution fusion | flops 3758555136 | bytes 12451840 | tf_op jit(solution)/shard_map/pz,xz->px/dot_general | solution.py:104
  470.8 53.5 %all-to-all-done.7.refs_2_ = bf16[8,128,896]{2,1,0:T(8,128)(2,1)} async-done(((bf16[8,128,896]{2,1,0:T(8,128)(2,1)}), bf16[8,128,896]{2,1,0:T(8,128)(2,1)}, u32[]{:S(2)}, u32[]{:S(2)}) %all-to-all-start.7) | async-done | bytes 1835040 | tf_op jit(solution)/shard_map/all_to_all | solution.py:230
  563.2 5.8 all-to-all-done.8.refs_3_
  569.0 25.3 %shard_map.110 = f32[32,128,896]{2,1,0:T(8,128)} custom-call(s32[32]{0:T(128)} %reshape.251.rows_ref, bf16[8,128,896]{2,1,0:T(8,128)(2,1)} %all_to_all.45.refs_0_, bf16[8,128,896]{2,1,0:T(8,128)(2,1)} %all-to-all-done.6.refs_1_, bf16[8,128,896]{2,1,0:T(8,128)(2,1)} %all-to-all-done.7.refs_2_, bf16[8,128,896]{2,1,0:T(8,128)(2,1)} %all-to-all-done.8.refs_3_), custom_call_target="tpu_custom_call" | custom-call | tf_op jit(solution)/shard_map/pallas_call | solution.py:47
  (381 shorter events, 250.9 us)
Async XLA Ops:
  12.3 18.1 %copy-start.74 = (s32[8]{0:T(128)}, s32[8]{0:T(128)S(1)}, u32[]{:S(2)}) copy-start(s32[8]{0:T(128)S(1)} %get-tuple-element.46) | copy-start | bytes 100
  13.3 22.4 %all-to-all-start = ((s32[4,4,2]{1,2,0:T(2,128)}), s32[4,4,2]{1,2,0:T(2,128)S(1)}, u32[]{:S(2)}, u32[]{:S(2)}) async-start(s32[4,4,2]{1,2,0:T(2,128)} %copy.146), calls=%async_computation | async-start | bytes 8192 | tf_op jit(solution)/shard_map/all_to_all | solution.py:144
  21.5 51.0 %collective-permute-start.1 = (bf16[2,63,2048]{2,1,0:T(8,128)(2,1)}, bf16[2,63,2048]{2,1,0:T(8,128)(2,1)}, u32[]{:S(2)}, u32[]{:S(2)}) collective-permute-start(bf16[2,63,2048]{2,1,0:T(8,128)(2,1)} %slice.117), channel_id=1, source_target_pairs={{1,0},{2,1},{3,2},{4,3},{5,4},{6,5},{7,6},{9,8},{10,9},{11,10},{12... | collective-permute-start | bytes 1548296 | tf_op jit(solution)/shard_map/ppermute | solution.py:19
  24.7 45.8 %collective-permute-start = (bf16[2,63,2048]{2,1,0:T(8,128)(2,1)}, bf16[2,63,2048]{2,1,0:T(8,128)(2,1)}, u32[]{:S(2)}, u32[]{:S(2)}) collective-permute-start(bf16[2,63,2048]{2,1,0:T(8,128)(2,1)} %slice.113), channel_id=1, source_target_pairs={{1,0},{2,1},{3,2},{4,3},{5,4},{6,5},{7,6},{9,8},{10,9},{11,10},{12... | collective-permute-start | bytes 1548296 | tf_op jit(solution)/shard_map/ppermute | solution.py:19
  58.6 48.8 %all-to-all-start.1 = ((bf16[8,128,896]{2,1,0:T(8,128)(2,1)}), bf16[8,128,896]{2,1,0:T(8,128)(2,1)}, u32[]{:S(2)}, u32[]{:S(2)}) async-start(bf16[8,128,896]{2,1,0:T(8,128)(2,1)} %broadcast_select_fusion.7), calls=%async_computation.1 | async-start | bytes 3670016 | tf_op jit(solution)/shard_map/all_to_all | solution.py:161
  107.4 53.7 %all-to-all-start.2 = ((bf16[8,128,896]{2,1,0:T(8,128)(2,1)}), bf16[8,128,896]{2,1,0:T(8,128)(2,1)}, u32[]{:S(2)}, u32[]{:S(2)}) async-start(bf16[8,128,896]{2,1,0:T(8,128)(2,1)} %broadcast_select_fusion.6), calls=%async_computation.2 | async-start | bytes 3670016 | tf_op jit(solution)/shard_map/all_to_all | solution.py:161
  161.1 54.4 %all-to-all-start.3 = ((bf16[8,128,896]{2,1,0:T(8,128)(2,1)}), bf16[8,128,896]{2,1,0:T(8,128)(2,1)}, u32[]{:S(2)}, u32[]{:S(2)}) async-start(bf16[8,128,896]{2,1,0:T(8,128)(2,1)} %broadcast_select_fusion.5), calls=%async_computation.3 | async-start | bytes 3670016 | tf_op jit(solution)/shard_map/all_to_all | solution.py:161
  185.7 9.3 %copy-start.20 = (f32[2,16,64,256]{3,2,1,0:T(8,128)}, f32[2,16,64,256]{3,2,1,0:T(8,128)S(1)}, u32[]{:S(2)}) copy-start(f32[2,16,64,256]{3,2,1,0:T(8,128)S(1)} %get-tuple-element.85) | copy-start | bytes 6291460
  215.5 71.1 %all-to-all-start.4 = ((bf16[8,128,896]{2,1,0:T(8,128)(2,1)}), bf16[8,128,896]{2,1,0:T(8,128)(2,1)}, u32[]{:S(2)}, u32[]{:S(2)}) async-start(bf16[8,128,896]{2,1,0:T(8,128)(2,1)} %broadcast_select_fusion.3), calls=%async_computation.4 | async-start | bytes 3670016 | tf_op jit(solution)/shard_map/all_to_all | solution.py:161
  220.6 224.9 %reduce-scatter.3.cloned.1.call-start = ((), (), s32[]{:S(2)}) async-start(), calls=%async_computation.11 | async-start | bytes 16515072 | tf_op jit(solution)/shard_map/reduce_scatter | solution.py:220
  233.2 9.5 %copy-start.22 = (f32[2,16,64,256]{3,2,1,0:T(8,128)}, f32[2,16,64,256]{3,2,1,0:T(8,128)S(1)}, u32[]{:S(2)}) copy-start(f32[2,16,64,256]{3,2,1,0:T(8,128)S(1)} %get-tuple-element.89) | copy-start | bytes 6291460
  268.5 20.4 %copy-start.77 = (pred[4]{0:T(512)(128)(4,1)S(1)}, pred[4]{0:T(512)(128)(4,1)}, u32[]{:S(2)}) copy-start(pred[4]{0:T(512)(128)(4,1)} %get-tuple-element.54) | copy-start | bytes 16
  306.6 9.3 %copy-start.24 = (f32[2,16,64,256]{3,2,1,0:T(8,128)}, f32[2,16,64,256]{3,2,1,0:T(8,128)S(1)}, u32[]{:S(2)}) copy-start(f32[2,16,64,256]{3,2,1,0:T(8,128)S(1)} %get-tuple-element.93) | copy-start | bytes 6291460
  326.1 12.2 %copy-start.16 = (bf16[512,4096]{1,0:T(8,128)(2,1)}, bf16[512,4096]{1,0:T(8,128)(2,1)S(1)}, u32[]{:S(2)}) copy-start(bf16[512,4096]{1,0:T(8,128)(2,1)S(1)} %bitcast_dynamic-update-slice_fusion) | copy-start | bytes 12582916
  386.6 46.4 %all-to-all-start.6 = ((bf16[8,128,896]{2,1,0:T(8,128)(2,1)}), bf16[8,128,896]{2,1,0:T(8,128)(2,1)}, u32[]{:S(2)}, u32[]{:S(2)}) async-start(bf16[8,128,896]{2,1,0:T(8,128)(2,1)} %broadcast_select_fusion.2), calls=%async_computation.6 | async-start | bytes 3670016 | tf_op jit(solution)/shard_map/all_to_all | solution.py:230
  394.8 55.2 %copy-start.1 = (bf16[64,8,16,128]{3,2,1,0:T(8,128)(2,1)S(1)}, bf16[64,8,16,128]{3,2,1,0:T(8,128)(2,1)}, u32[]{:S(2)}) copy-start(bf16[64,8,16,128]{3,2,1,0:T(8,128)(2,1)} %copy-done) | copy-start | bytes 6291460
  394.8 55.2 %copy-start.9 = (bf16[2,16,64,256]{3,2,1,0:T(8,128)(2,1)S(1)}, bf16[2,16,64,256]{3,2,1,0:T(8,128)(2,1)}, u32[]{:S(2)}) copy-start(bf16[2,16,64,256]{3,2,1,0:T(8,128)(2,1)} %copy-done.8) | copy-start | bytes 3145732
  445.4 78.9 %all-to-all-start.7 = ((bf16[8,128,896]{2,1,0:T(8,128)(2,1)}), bf16[8,128,896]{2,1,0:T(8,128)(2,1)}, u32[]{:S(2)}, u32[]{:S(2)}) async-start(bf16[8,128,896]{2,1,0:T(8,128)(2,1)} %broadcast_select_fusion.1), calls=%async_computation.8 | async-start | bytes 3670016 | tf_op jit(solution)/shard_map/all_to_all | solution.py:230
  450.0 111.3 %reduce-scatter.5.cloned.1.call-start = ((), (), s32[]{:S(2)}) async-start(), calls=%async_computation.12 | async-start | bytes 2621440 | tf_op jit(solution)/shard_map/reduce_scatter | solution.py:244
  470.8 58.1 %copy-start.5 = (bf16[64,8,16,128]{3,2,1,0:T(8,128)(2,1)S(1)}, bf16[64,8,16,128]{3,2,1,0:T(8,128)(2,1)}, u32[]{:S(2)}) copy-start(bf16[64,8,16,128]{3,2,1,0:T(8,128)(2,1)} %copy-done.4) | copy-start | bytes 6291460
  470.8 58.1 %copy-start.13 = (bf16[2,16,64,256]{3,2,1,0:T(8,128)(2,1)S(1)}, bf16[2,16,64,256]{3,2,1,0:T(8,128)(2,1)}, u32[]{:S(2)}) copy-start(bf16[2,16,64,256]{3,2,1,0:T(8,128)(2,1)} %copy-done.12) | copy-start | bytes 3145732
  524.3 44.6 %all-to-all-start.8 = ((bf16[8,128,896]{2,1,0:T(8,128)(2,1)}), bf16[8,128,896]{2,1,0:T(8,128)(2,1)}, u32[]{:S(2)}, u32[]{:S(2)}) async-start(bf16[8,128,896]{2,1,0:T(8,128)(2,1)} %broadcast_select_fusion), calls=%async_computation.9 | async-start | bytes 3670016 | tf_op jit(solution)/shard_map/all_to_all | solution.py:230
  542.6 12.7 %collective-permute-start.2 = (bf16[2,63,2048]{2,1,0:T(8,128)(2,1)}, bf16[2,63,2048]{2,1,0:T(8,128)(2,1)}, u32[]{:S(2)}, u32[]{:S(2)}) collective-permute-start(bf16[2,63,2048]{2,1,0:T(8,128)(2,1)} %slice.167), channel_id=1, source_target_pairs={{0,1},{1,2},{2,3},{3,4},{4,5},{5,6},{6,7},{8,9},{9,10},{10,11},{11... | collective-permute-start | bytes 1548296 | tf_op jit(solution)/shard_map/ppermute | solution.py:19
  551.5 8.1 %collective-permute-start.3 = (bf16[2,63,2048]{2,1,0:T(8,128)(2,1)S(1)}, bf16[2,63,2048]{2,1,0:T(8,128)(2,1)S(1)}, u32[]{:S(2)}, u32[]{:S(2)}) collective-permute-start(bf16[2,63,2048]{2,1,0:T(8,128)(2,1)S(1)} %slice.170), channel_id=1, source_target_pairs={{0,1},{1,2},{2,3},{3,4},{4,5},{5,6},{6,7},{8,9},{9,10},{10,11},{11... | collective-permute-start | bytes 1548296 | tf_op jit(solution)/shard_map/ppermute | solution.py:19
  (72 other events, 241.3 us)
Sparse Core Ops, SparseCore 0:
  338.5 106.9 reduce-scatter.2
  459.6 65.3 reduce-scatter.4

commit v9 on v7

--- a/solution.py
+++ b/solution.py
@@ -25,15 +25,18 @@
 
 def _row_sum_kernel(rows_ref, *refs):
     part_refs, out_ref = refs[:-1], refs[-1]
-    row = pl.program_id(0)
+    block_rows = out_ref.shape[0]
+    first = pl.program_id(0) * block_rows
     out_ref[...] = jnp.zeros(out_ref.shape, out_ref.dtype)
     base = 0
     for part in part_refs:
 
         def body(s, carry, part=part, base=base):
-            @pl.when(rows_ref[base + s] == row)
+            local = rows_ref[base + s] - first
+
+            @pl.when((local >= 0) & (local < block_rows))
             def _():
-                out_ref[0] += part[s].astype(jnp.float32)
+                out_ref[local] += part[s].astype(jnp.float32)
 
             return carry
 
@@ -43,14 +46,15 @@
 
 def row_sums(rows, parts, row_count):
     width = parts[0].shape[1:]
+    block_rows = 8 if row_count % 8 == 0 else row_count
     whole = lambda r, rows_ref: (0, 0, 0)
     return pl.pallas_call(
         _row_sum_kernel,
         grid_spec=pltpu.PrefetchScalarGridSpec(
             num_scalar_prefetch=1,
-            grid=(row_count,),
+            grid=(row_count // block_rows,),
             in_specs=[pl.BlockSpec(p.shape, whole) for p in parts],
-            out_specs=pl.BlockSpec((1,) + width, lambda r, rows_ref: (r, 0, 0)),
+            out_specs=pl.BlockSpec((block_rows,) + width, lambda r, rows_ref: (r, 0, 0)),
         ),
         out_shape=jax.ShapeDtypeStruct((row_count,) + width, jnp.float32),
     )(rows, *parts)

time: 563 us -> 549 us (0.975)
  Pallas kernels: 25.4 us -> 11.2 us
    pallas_call x1, Pallas kernels: 25.4 us -> 11.2 us  [row_sums(): pl.pallas_call(_row_sum_kernel, grid_spec=pltpu.PrefetchScalarGridSpec(nu...]
  transfers between devices with their start and end apart: 15 -> 15, of which waited for: 8 -> 8; matrix products, arithmetic and copies ran while one was open for 43% -> 45% of each run, Pallas kernels for 0% -> 0%
where the time goes in v9:
time: 549 us; the launch traced here: 541 us
  local copies, waits for them, and re-layouts  155 us (28%)
  matrix products  144 us (26%)
  waiting for transfers between devices  138 us (25%)
  starting transfers between devices  50.2 us (9%)
  other arithmetic  27 us (5%)
  between operations  15.7 us (3%)
  Pallas kernels  11.2 us (2%)
    all_to_all x4, waiting for transfers between devices, local(): link = lax.all_to_all(sent, 'dp', split_axis=0, concat_axis=0, tiled=True)  114 us
    unnamed x173, local copies, waits for them, and re-layouts  43.9 us
    dot_general x4, matrix products, attend_chunk(): jnp.einsum('pz,xz->px', proj_grads, both_weights, preferred_element_type=...  37.1 us
    dot_general x2, matrix products, weight_term(): jnp.einsum('px,pz->xz', jnp.concatenate(seq_major[first:last], axis=0), j...  28.1 us
    all_to_all x4, waiting for transfers between devices, local(): link = lax.all_to_all(rows, 'dp', split_axis=0, concat_axis=0, tiled=True)  23.6 us
    dot_general x4, matrix products, attend_chunk(): jnp.dot(neighbours, key_weight, preferred_element_type=jnp.float32)  22.3 us
    all_to_all x4, starting transfers between devices, local(): link = lax.all_to_all(rows, 'dp', split_axis=0, concat_axis=0, tiled=True)  18.7 us
    gather x4, local copies, waits for them, and re-layouts, local(): rows = jnp.take(database, arrived[:, g, :].reshape(chunk_slots), axis=0)  18 us
  transfers between devices with their start and end apart: 15, of which 8 were waited for; matrix products, arithmetic and copies ran while one was open for 45% of the time, Pallas kernels for 0%

profile of v9, /device:TPU:0, one launch (start us, length us, event | category | flops | bytes accessed | tf_op | source)
XLA Modules:
  0.0 540.9 jit_solution(15251053548929279599)
XLA Ops:
  13.4 6.3 %all-to-all-start = ((s32[4,4,2]{1,2,0:T(2,128)}), s32[4,4,2]{1,2,0:T(2,128)S(1)}, u32[]{:S(2)}, u32[]{:S(2)}) async-start(s32[4,4,2]{1,2,0:T(2,128)} %copy.146), calls=%async_computation | async-start | bytes 8192 | tf_op jit(solution)/shard_map/all_to_all | solution.py:148
  34.6 5.1 all-to-all-start.1
  43.6 5.1 gather_fusion.3
  48.7 5.1 gather_fusion.5
  66.4 16.9 %all-to-all-done.1 = bf16[8,128,896]{2,1,0:T(8,128)(2,1)} async-done(((bf16[8,128,896]{2,1,0:T(8,128)(2,1)}), bf16[8,128,896]{2,1,0:T(8,128)(2,1)}, u32[]{:S(2)}, u32[]{:S(2)}) %all-to-all-start.1) | async-done | bytes 1835040 | tf_op jit(solution)/shard_map/all_to_all | solution.py:165
  83.3 4.6 all-to-all-start.2
  93.9 4.7 fusion.55
  131.2 4.6 all-to-all-start.3
  139.4 5.8 %fusion.57 = bf16[64,8,16,128]{3,1,2,0:T(8,128)(2,1)} fusion(bf16[512,896]{1,0:T(8,128)(2,1)S(1)} %bitcast.200, bf16[896,2048]{1,0:T(8,128)(2,1)} %param.16), kind=kOutput, calls=%fused_computation.117 | convolution fusion | flops 1880096768 | bytes 6684672 | tf_op jit(solution)/shard_map/dot_general | solution.py:66
  186.7 5.8 %fusion.59 = bf16[64,8,16,128]{3,1,2,0:T(8,128)(2,1)} fusion(bf16[512,896]{1,0:T(8,128)(2,1)S(1)} %bitcast.202, bf16[896,2048]{1,0:T(8,128)(2,1)} %param.16), kind=kOutput, calls=%fused_computation.119 | convolution fusion | flops 1880096768 | bytes 6684672 | tf_op jit(solution)/shard_map/dot_general | solution.py:66
  228.6 5.8 %fusion.61 = bf16[64,8,16,128]{3,1,2,0:T(8,128)(2,1)} fusion(bf16[512,896]{1,0:T(8,128)(2,1)S(1)} %bitcast.204, bf16[896,2048]{1,0:T(8,128)(2,1)} %param.16), kind=kOutput, calls=%fused_computation.121 | convolution fusion | flops 1880096768 | bytes 6684672 | tf_op jit(solution)/shard_map/dot_general | solution.py:66
  249.0 4.5 copy.189
  265.0 7.6 %fusion.152 = f32[896,4096]{1,0:T(8,128)} fusion(bf16[512,896]{0,1:T(8,128)(2,1)S(1)} %reshape.252, bf16[512,4096]{1,0:T(8,128)(2,1)S(1)} %bitcast_dynamic-update-slice_fusion), kind=kOutput, calls=%fused_computation.248 | convolution fusion | flops 3758096384 | bytes 19791872 | tf_op jit(solution)/shard_map/px,pz->xz/dot_general | solution.py:203
  272.6 20.5 %fusion.6 = f32[896,4096]{1,0:T(8,128)} fusion(f32[896,4096]{1,0:T(8,128)} %fusion.152, bf16[512,4096]{1,0:T(8,128)(2,1)} %bitcast_dynamic-update-slice_fusion.2, bf16[512,4096]{1,0:T(8,128)(2,1)} %bitcast_dynamic-update-slice_fusion.4, bf16[512,4096]{1,0:T(8,128)(2,1)} %bitcast_dynamic-update-slice_fusion.6, bf16[512,896]{0,1:T(8,128)(2,1)S(1)} %copy-done.59, ...), kind=kOutput, calls=%fused_computation.18 | convolution fusion | flops 11323965440 | bytes 44695552 | tf_op jit(solution)/shard_map/px,pz->xz/dot_general | solution.py:203
  297.5 9.7 %convolution_convert_fusion.11 = bf16[512,896]{1,0:T(8,128)(2,1)S(1)} fusion(bf16[512,4096]{1,0:T(8,128)(2,1)} %bitcast_dynamic-update-slice_fusion.6, bf16[896,4096]{1,0:T(8,128)(2,1)S(1)} %constant_dynamic-update-slice_fusion), kind=kOutput, calls=%fused_computation.125 | convolution fusion | flops 3758555136 | bytes 12451840 | tf_op jit(solution)/shard_map/pz,xz->px/dot_general | solution.py:108
  314.1 9.6 %convolution_convert_fusion.10 = bf16[512,896]{1,0:T(8,128)(2,1)S(1)} fusion(bf16[512,4096]{1,0:T(8,128)(2,1)} %bitcast_dynamic-update-slice_fusion.4, bf16[896,4096]{1,0:T(8,128)(2,1)} %copy-done.54), kind=kOutput, calls=%fused_computation.124 | convolution fusion | flops 3758555136 | bytes 12451840 | tf_op jit(solution)/shard_map/pz,xz->px/dot_general | solution.py:108
  326.1 30.0 %all-to-all-done.5.refs_0_ = bf16[8,128,896]{2,1,0:T(8,128)(2,1)} async-done(((bf16[8,128,896]{2,1,0:T(8,128)(2,1)}), bf16[8,128,896]{2,1,0:T(8,128)(2,1)}, u32[]{:S(2)}, u32[]{:S(2)}) %all-to-all-start.5) | async-done | bytes 1835040 | tf_op jit(solution)/shard_map/all_to_all | solution.py:225
  356.1 4.6 all-to-all-start.6
  364.0 8.9 %convolution_convert_fusion.9 = bf16[512,896]{1,0:T(8,128)(2,1)S(1)} fusion(bf16[512,4096]{1,0:T(8,128)(2,1)} %bitcast_dynamic-update-slice_fusion.2, bf16[896,4096]{1,0:T(8,128)(2,1)} %copy-done.54), kind=kOutput, calls=%fused_computation.123 | convolution fusion | flops 3758555136 | bytes 12451840 | tf_op jit(solution)/shard_map/pz,xz->px/dot_general | solution.py:108
  375.4 27.3 %all-to-all-done.6.refs_1_ = bf16[8,128,896]{2,1,0:T(8,128)(2,1)} async-done(((bf16[8,128,896]{2,1,0:T(8,128)(2,1)}), bf16[8,128,896]{2,1,0:T(8,128)(2,1)}, u32[]{:S(2)}, u32[]{:S(2)}) %all-to-all-start.6) | async-done | bytes 1835040 | tf_op jit(solution)/shard_map/all_to_all | solution.py:225
  416.7 8.9 %convolution_convert_fusion.8 = bf16[512,896]{1,0:T(8,128)(2,1)S(1)} fusion(bf16[512,4096]{1,0:T(8,128)(2,1)} %copy-done.56, bf16[896,4096]{1,0:T(8,128)(2,1)} %copy-done.54), kind=kOutput, calls=%fused_computation.122 | convolution fusion | flops 3758555136 | bytes 12451840 | tf_op jit(solution)/shard_map/pz,xz->px/dot_general | solution.py:108
  428.0 50.2 %all-to-all-done.7.refs_2_ = bf16[8,128,896]{2,1,0:T(8,128)(2,1)} async-done(((bf16[8,128,896]{2,1,0:T(8,128)(2,1)}), bf16[8,128,896]{2,1,0:T(8,128)(2,1)}, u32[]{:S(2)}, u32[]{:S(2)}) %all-to-all-start.7) | async-done | bytes 1835040 | tf_op jit(solution)/shard_map/all_to_all | solution.py:225
  516.0 6.6 %all-to-all-done.8.refs_3_ = bf16[8,128,896]{2,1,0:T(8,128)(2,1)} async-done(((bf16[8,128,896]{2,1,0:T(8,128)(2,1)}), bf16[8,128,896]{2,1,0:T(8,128)(2,1)}, u32[]{:S(2)}, u32[]{:S(2)}) %all-to-all-start.8) | async-done | bytes 1835040 | tf_op jit(solution)/shard_map/all_to_all | solution.py:225
  522.6 11.2 %shard_map.110 = f32[32,128,896]{2,1,0:T(8,128)} custom-call(s32[32]{0:T(128)} %reshape.239.rows_ref, bf16[8,128,896]{2,1,0:T(8,128)(2,1)} %all-to-all-done.5.refs_0_, bf16[8,128,896]{2,1,0:T(8,128)(2,1)} %all-to-all-done.6.refs_1_, bf16[8,128,896]{2,1,0:T(8,128)(2,1)} %all-to-all-done.7.refs_2_, bf16[8,128,896]{2,1,0:T(8,128)(2,1)} %all-to-all-done.8.refs_3_), custom_call_target="tpu_custom_call" | custom-call | tf_op jit(solution)/shard_map/pallas_call | solution.py:51
  (381 shorter events, 255.8 us)
Async XLA Ops:
  7.2 19.1 %copy-start.43 = (bf16[2,256,2048]{2,1,0:T(8,128)(2,1)S(1)}, bf16[2,256,2048]{2,1,0:T(8,128)(2,1)}, u32[]{:S(2)}) copy-start(bf16[2,256,2048]{2,1,0:T(8,128)(2,1)} %param.13) | copy-start | bytes 6291460
  13.4 14.9 %all-to-all-start = ((s32[4,4,2]{1,2,0:T(2,128)}), s32[4,4,2]{1,2,0:T(2,128)S(1)}, u32[]{:S(2)}, u32[]{:S(2)}) async-start(s32[4,4,2]{1,2,0:T(2,128)} %copy.146), calls=%async_computation | async-start | bytes 8192 | tf_op jit(solution)/shard_map/all_to_all | solution.py:148
  21.7 39.9 %collective-permute-start.2 = (bf16[2,63,2048]{2,1,0:T(8,128)(2,1)}, bf16[2,63,2048]{2,1,0:T(8,128)(2,1)}, u32[]{:S(2)}, u32[]{:S(2)}) collective-permute-start(bf16[2,63,2048]{2,1,0:T(8,128)(2,1)} %slice.123), channel_id=1, source_target_pairs={{1,0},{2,1},{3,2},{4,3},{5,4},{6,5},{7,6},{9,8},{10,9},{11,10},{12... | collective-permute-start | bytes 1548296 | tf_op jit(solution)/shard_map/ppermute | solution.py:19
  25.0 34.6 %collective-permute-start = (bf16[2,63,2048]{2,1,0:T(8,128)(2,1)}, bf16[2,63,2048]{2,1,0:T(8,128)(2,1)}, u32[]{:S(2)}, u32[]{:S(2)}) collective-permute-start(bf16[2,63,2048]{2,1,0:T(8,128)(2,1)} %slice.113), channel_id=1, source_target_pairs={{1,0},{2,1},{3,2},{4,3},{5,4},{6,5},{7,6},{9,8},{10,9},{11,10},{12... | collective-permute-start | bytes 1548296 | tf_op jit(solution)/shard_map/ppermute | solution.py:19
  34.6 48.8 %all-to-all-start.1 = ((bf16[8,128,896]{2,1,0:T(8,128)(2,1)}), bf16[8,128,896]{2,1,0:T(8,128)(2,1)}, u32[]{:S(2)}, u32[]{:S(2)}) async-start(bf16[8,128,896]{2,1,0:T(8,128)(2,1)} %broadcast_select_fusion.7), calls=%async_computation.1 | async-start | bytes 3670016 | tf_op jit(solution)/shard_map/all_to_all | solution.py:165
  83.3 47.9 %all-to-all-start.2 = ((bf16[8,128,896]{2,1,0:T(8,128)(2,1)}), bf16[8,128,896]{2,1,0:T(8,128)(2,1)}, u32[]{:S(2)}, u32[]{:S(2)}) async-start(bf16[8,128,896]{2,1,0:T(8,128)(2,1)} %broadcast_select_fusion.6), calls=%async_computation.2 | async-start | bytes 3670016 | tf_op jit(solution)/shard_map/all_to_all | solution.py:165
  131.2 47.1 %all-to-all-start.3 = ((bf16[8,128,896]{2,1,0:T(8,128)(2,1)}), bf16[8,128,896]{2,1,0:T(8,128)(2,1)}, u32[]{:S(2)}, u32[]{:S(2)}) async-start(bf16[8,128,896]{2,1,0:T(8,128)(2,1)} %broadcast_select_fusion.5), calls=%async_computation.3 | async-start | bytes 3670016 | tf_op jit(solution)/shard_map/all_to_all | solution.py:165
  178.4 46.5 %all-to-all-start.4 = ((bf16[8,128,896]{2,1,0:T(8,128)(2,1)}), bf16[8,128,896]{2,1,0:T(8,128)(2,1)}, u32[]{:S(2)}, u32[]{:S(2)}) async-start(bf16[8,128,896]{2,1,0:T(8,128)(2,1)} %broadcast_select_fusion.4), calls=%async_computation.4 | async-start | bytes 3670016 | tf_op jit(solution)/shard_map/all_to_all | solution.py:165
  182.8 220.0 %reduce-scatter.3.cloned.1.call-start = ((), (), s32[]{:S(2)}) async-start(), calls=%async_computation.11 | async-start | bytes 16515072 | tf_op jit(solution)/shard_map/reduce_scatter | solution.py:214
  309.6 46.5 %all-to-all-start.5 = ((bf16[8,128,896]{2,1,0:T(8,128)(2,1)}), bf16[8,128,896]{2,1,0:T(8,128)(2,1)}, u32[]{:S(2)}, u32[]{:S(2)}) async-start(bf16[8,128,896]{2,1,0:T(8,128)(2,1)} %broadcast_select_fusion.3), calls=%async_computation.5 | async-start | bytes 3670016 | tf_op jit(solution)/shard_map/all_to_all | solution.py:225
  326.1 34.5 %copy-start.75 = (s32[8]{0:T(128)S(1)}, s32[8]{0:T(128)}, u32[]{:S(2)}) copy-start(s32[8]{0:T(128)} %get-tuple-element.40) | copy-start | bytes 100
  326.1 34.5 %copy-start.76 = (s32[8]{0:T(128)S(1)}, s32[8]{0:T(128)}, u32[]{:S(2)}) copy-start(s32[8]{0:T(128)} %get-tuple-element.36) | copy-start | bytes 100
  326.1 34.6 %copy-start.18 = (f32[2,16,64,256]{3,2,1,0:T(8,128)S(1)}, f32[2,16,64,256]{3,2,1,0:T(8,128)}, u32[]{:S(2)}) copy-start(f32[2,16,64,256]{3,2,1,0:T(8,128)} %copy-done.17) | copy-start | bytes 6291460
  326.1 34.6 %copy-start.70 = (f32[2,16,64]{2,1,0:T(8,128)S(1)}, f32[2,16,64]{2,1,0:T(8,128)}, u32[]{:S(2)}) copy-start(f32[2,16,64]{2,1,0:T(8,128)} %copy-done.69) | copy-start | bytes 24580
  356.1 46.7 %all-to-all-start.6 = ((bf16[8,128,896]{2,1,0:T(8,128)(2,1)}), bf16[8,128,896]{2,1,0:T(8,128)(2,1)}, u32[]{:S(2)}, u32[]{:S(2)}) async-start(bf16[8,128,896]{2,1,0:T(8,128)(2,1)} %broadcast_select_fusion.2), calls=%async_computation.6 | async-start | bytes 3670016 | tf_op jit(solution)/shard_map/all_to_all | solution.py:225
  375.4 31.8 %copy-start.1 = (bf16[64,8,16,128]{3,2,1,0:T(8,128)(2,1)S(1)}, bf16[64,8,16,128]{3,2,1,0:T(8,128)(2,1)}, u32[]{:S(2)}) copy-start(bf16[64,8,16,128]{3,2,1,0:T(8,128)(2,1)} %copy-done) | copy-start | bytes 6291460
  375.4 31.8 %copy-start.9 = (bf16[2,16,64,256]{3,2,1,0:T(8,128)(2,1)S(1)}, bf16[2,16,64,256]{3,2,1,0:T(8,128)(2,1)}, u32[]{:S(2)}) copy-start(bf16[2,16,64,256]{3,2,1,0:T(8,128)(2,1)} %copy-done.8) | copy-start | bytes 3145732
  402.8 75.4 %all-to-all-start.7 = ((bf16[8,128,896]{2,1,0:T(8,128)(2,1)}), bf16[8,128,896]{2,1,0:T(8,128)(2,1)}, u32[]{:S(2)}, u32[]{:S(2)}) async-start(bf16[8,128,896]{2,1,0:T(8,128)(2,1)} %broadcast_select_fusion.1), calls=%async_computation.8 | async-start | bytes 3670016 | tf_op jit(solution)/shard_map/all_to_all | solution.py:225
  407.2 107.0 %reduce-scatter.5.cloned.1.call-start = ((), (), s32[]{:S(2)}) async-start(), calls=%async_computation.12 | async-start | bytes 2621440 | tf_op jit(solution)/shard_map/reduce_scatter | solution.py:239
  428.0 54.6 %copy-start.5 = (bf16[64,8,16,128]{3,2,1,0:T(8,128)(2,1)S(1)}, bf16[64,8,16,128]{3,2,1,0:T(8,128)(2,1)}, u32[]{:S(2)}) copy-start(bf16[64,8,16,128]{3,2,1,0:T(8,128)(2,1)} %copy-done.4) | copy-start | bytes 6291460
  428.0 54.6 %copy-start.13 = (bf16[2,16,64,256]{3,2,1,0:T(8,128)(2,1)S(1)}, bf16[2,16,64,256]{3,2,1,0:T(8,128)(2,1)}, u32[]{:S(2)}) copy-start(bf16[2,16,64,256]{3,2,1,0:T(8,128)(2,1)} %copy-done.12) | copy-start | bytes 3145732
  478.2 44.4 %all-to-all-start.8 = ((bf16[8,128,896]{2,1,0:T(8,128)(2,1)}), bf16[8,128,896]{2,1,0:T(8,128)(2,1)}, u32[]{:S(2)}, u32[]{:S(2)}) async-start(bf16[8,128,896]{2,1,0:T(8,128)(2,1)} %broadcast_select_fusion), calls=%async_computation.9 | async-start | bytes 3670016 | tf_op jit(solution)/shard_map/all_to_all | solution.py:225
  496.3 11.9 %collective-permute-start.1 = (bf16[2,63,2048]{2,1,0:T(8,128)(2,1)}, bf16[2,63,2048]{2,1,0:T(8,128)(2,1)}, u32[]{:S(2)}, u32[]{:S(2)}) collective-permute-start(bf16[2,63,2048]{2,1,0:T(8,128)(2,1)} %slice.164), channel_id=1, source_target_pairs={{0,1},{1,2},{2,3},{3,4},{4,5},{5,6},{6,7},{8,9},{9,10},{10,11},{11... | collective-permute-start | bytes 1548296 | tf_op jit(solution)/shard_map/ppermute | solution.py:19
  505.4 7.0 %collective-permute-start.3 = (bf16[2,63,2048]{2,1,0:T(8,128)(2,1)S(1)}, bf16[2,63,2048]{2,1,0:T(8,128)(2,1)S(1)}, u32[]{:S(2)}, u32[]{:S(2)}) collective-permute-start(bf16[2,63,2048]{2,1,0:T(8,128)(2,1)S(1)} %slice.170), channel_id=1, source_target_pairs={{0,1},{1,2},{2,3},{3,4},{4,5},{5,6},{6,7},{8,9},{9,10},{10,11},{11... | collective-permute-start | bytes 1548296 | tf_op jit(solution)/shard_map/ppermute | solution.py:19
  (72 other events, 269.0 us)
Sparse Core Ops, SparseCore 0:
  293.3 105.2 reduce-scatter.2
  416.8 64.2 reduce-scatter.4

commit v10 on v9

--- a/solution.py
+++ b/solution.py
@@ -167,6 +167,7 @@
 
     context_parts = []
     query_parts = []
+    returned_parts = []
     grads_out = []
     seq_major = []
     proj_parts = []
@@ -174,6 +175,13 @@
         incoming = fetched[g][1]
         if g + 1 < chunk_count:
             incoming, _ = lax.optimization_barrier((incoming, fetched[g + 1][0]))
+        if g >= 1:
+            incoming, _ = lax.optimization_barrier((incoming, grads_out[g - 1]))
+        if g >= 1 and g == chunk_count - 1:
+            sent, _ = lax.optimization_barrier((grads_out[0], link))
+            link = lax.all_to_all(sent, "dp", split_axis=0, concat_axis=0, tiled=True)
+            returned_parts.append(link)
+            incoming, _ = lax.optimization_barrier((incoming, link))
         neighbours = jnp.take(incoming, slot_indices[g], axis=0).reshape(
             chunk_refs * NB_LEN, ENC
         )
@@ -217,8 +225,7 @@
         scatter_dimension=0,
         tiled=True,
     )
-    returned_parts = []
-    for g in range(chunk_count):
+    for g in range(len(returned_parts), chunk_count):
         sent, _ = lax.optimization_barrier((grads_out[g], link))
         if g == chunk_count // 2:
             sent, plane_sums = lax.optimization_barrier((sent, plane_sums))

time: 549 us -> 631 us (1.15)
  waiting for transfers between devices: 138 us -> 224 us
  local copies, waits for them, and re-layouts: 155 us -> 148 us
  other arithmetic: 27 us -> 33.9 us
    reduce_scatter x1, waiting for transfers between devices: 0.01 us -> 57.5 us  [local(): lax.psum_scatter(weight_terms.reshape(seq_total, shard_count * enc_share,...]
    all_to_all x4, waiting for transfers between devices: 23.6 us -> 44.9 us  [local(): link = lax.all_to_all(rows, 'dp', split_axis=0, concat_axis=0, tiled=True)]
    all_to_all x4, waiting for transfers between devices: 114 us -> 121 us  [local(): link = lax.all_to_all(sent, 'dp', split_axis=0, concat_axis=0, tiled=True)]
    unnamed x173 -> x171, local copies, waits for them, and re-layouts: 43.9 us -> 38 us
  transfers between devices with their start and end apart: 15 -> 15, of which waited for: 8 -> 7; matrix products, arithmetic and copies ran while one was open for 45% -> 38% of each run, Pallas kernels for 0% -> 0%
where the time goes in v10:
time: 631 us; the launch traced here: 623 us
  waiting for transfers between devices  224 us (35%)
  local copies, waits for them, and re-layouts  148 us (23%)
  matrix products  139 us (22%)
  starting transfers between devices  52 us (8%)
  other arithmetic  33.9 us (5%)
  between operations  15.7 us (2%)
  Pallas kernels  10.9 us (2%)
    all_to_all x4, waiting for transfers between devices, local(): link = lax.all_to_all(sent, 'dp', split_axis=0, concat_axis=0, tiled=True)  121 us
    reduce_scatter x1, waiting for transfers between devices, local(): lax.psum_scatter(weight_terms.reshape(seq_total, shard_count * enc_share,...  57.5 us
    all_to_all x4, waiting for transfers between devices, local(): link = lax.all_to_all(rows, 'dp', split_axis=0, concat_axis=0, tiled=True)  44.9 us
    unnamed x171, local copies, waits for them, and re-layouts  38 us
    dot_general x4, matrix products, attend_chunk(): jnp.einsum('pz,xz->px', proj_grads, both_weights, preferred_element_type=...  34 us
    dot_general x2, matrix products, weight_term(): jnp.einsum('px,pz->xz', jnp.concatenate(seq_major[first:last], axis=0), j...  27.3 us
    dot_general x4, matrix products, attend_chunk(): jnp.dot(neighbours, key_weight, preferred_element_type=jnp.float32)  21.9 us
    all_to_all x4, starting transfers between devices, local(): link = lax.all_to_all(rows, 'dp', split_axis=0, concat_axis=0, tiled=True)  19.8 us
  transfers between devices with their start and end apart: 15, of which 7 were waited for; matrix products, arithmetic and copies ran while one was open for 38% of the time, Pallas kernels for 0%

profile of v10, /device:TPU:0, one launch (start us, length us, event | category | flops | bytes accessed | tf_op | source)
XLA Modules:
  0.0 623.1 jit_solution(15935373657904693063)
XLA Ops:
  12.8 6.3 %all-to-all-start = ((s32[4,4,2]{1,2,0:T(2,128)}), s32[4,4,2]{1,2,0:T(2,128)S(1)}, u32[]{:S(2)}, u32[]{:S(2)}) async-start(s32[4,4,2]{1,2,0:T(2,128)} %copy.146), calls=%async_computation | async-start | bytes 8192 | tf_op jit(solution)/shard_map/all_to_all | solution.py:148
  36.5 5.1 gather_fusion.3
  45.5 5.1 gather_fusion.1
  50.6 5.1 gather_fusion
  58.6 5.1 all-to-all-start.1
  77.4 30.0 %all-to-all-done.1 = bf16[8,128,896]{2,1,0:T(8,128)(2,1)} async-done(((bf16[8,128,896]{2,1,0:T(8,128)(2,1)}), bf16[8,128,896]{2,1,0:T(8,128)(2,1)}, u32[]{:S(2)}, u32[]{:S(2)}) %all-to-all-start.1) | async-done | bytes 1835040 | tf_op jit(solution)/shard_map/all_to_all | solution.py:165
  115.5 5.8 fusion.55
  150.2 8.4 %convolution_convert_fusion.11 = bf16[512,896]{1,0:T(8,128)(2,1)S(1)} fusion(bf16[512,4096]{1,0:T(8,128)(2,1)S(1)} %bitcast_dynamic-update-slice_fusion.6, bf16[896,4096]{1,0:T(8,128)(2,1)} %copy-done.51), kind=kOutput, calls=%fused_computation.125 | convolution fusion | flops 3758555136 | bytes 12451840 | tf_op jit(solution)/shard_map/pz,xz->px/dot_general | solution.py:108
  161.1 5.1 all-to-all-start.3
  169.7 5.8 fusion.57
  204.5 8.4 %convolution_convert_fusion.10 = bf16[512,896]{1,0:T(8,128)(2,1)S(1)} fusion(bf16[512,4096]{1,0:T(8,128)(2,1)S(1)} %bitcast_dynamic-update-slice_fusion.4, bf16[896,4096]{1,0:T(8,128)(2,1)} %copy-done.51), kind=kOutput, calls=%fused_computation.124 | convolution fusion | flops 3758555136 | bytes 12451840 | tf_op jit(solution)/shard_map/pz,xz->px/dot_general | solution.py:108
  215.3 5.1 all-to-all-start.4
  247.8 14.9 %all-to-all-done.4 = bf16[8,128,896]{2,1,0:T(8,128)(2,1)} async-done(((bf16[8,128,896]{2,1,0:T(8,128)(2,1)}), bf16[8,128,896]{2,1,0:T(8,128)(2,1)}, u32[]{:S(2)}, u32[]{:S(2)}) %all-to-all-start.4) | async-done | bytes 1835040 | tf_op jit(solution)/shard_map/all_to_all | solution.py:165
  274.8 8.4 %convolution_convert_fusion.9 = bf16[512,896]{1,0:T(8,128)(2,1)S(1)} fusion(bf16[512,4096]{1,0:T(8,128)(2,1)S(1)} %bitcast_dynamic-update-slice_fusion.2, bf16[896,4096]{1,0:T(8,128)(2,1)} %copy-done.51), kind=kOutput, calls=%fused_computation.123 | convolution fusion | flops 3758555136 | bytes 12451840 | tf_op jit(solution)/shard_map/pz,xz->px/dot_general | solution.py:108
  285.7 23.6 %all-to-all-done.5.refs_0_ = bf16[8,128,896]{2,1,0:T(8,128)(2,1)} async-done(((bf16[8,128,896]{2,1,0:T(8,128)(2,1)}), bf16[8,128,896]{2,1,0:T(8,128)(2,1)}, u32[]{:S(2)}, u32[]{:S(2)}) %all-to-all-start.5) | async-done | bytes 1835040 | tf_op jit(solution)/shard_map/all_to_all | solution.py:182
  313.1 5.8 fusion.61
  350.1 7.6 %fusion.152 = f32[896,4096]{1,0:T(8,128)} fusion(bf16[512,896]{0,1:T(8,128)(2,1)S(1)} %copy-done.60, bf16[512,4096]{1,0:T(8,128)(2,1)S(1)} %bitcast_dynamic-update-slice_fusion), kind=kOutput, calls=%fused_computation.248 | convolution fusion | flops 3758096384 | bytes 19791872 | tf_op jit(solution)/shard_map/px,pz->xz/dot_general | solution.py:211
  357.7 19.7 %fusion.6 = f32[896,4096]{1,0:T(8,128)} fusion(f32[896,4096]{1,0:T(8,128)} %fusion.152, bf16[512,4096]{1,0:T(8,128)(2,1)} %copy-done.56, bf16[512,4096]{1,0:T(8,128)(2,1)} %copy-done.55, bf16[512,4096]{1,0:T(8,128)(2,1)S(1)} %copy-done.54, bf16[512,896]{0,1:T(8,128)(2,1)} %reshape.251, bf16[512,896]{0,1:T(8,128)(2,1)S(1)} %copy-done.59, ...), kind=kOutput, calls=%fused_computation.18 | convolution fusion | flops 11323965440 | bytes 44695552 | tf_op jit(solution)/shard_map/px,pz->xz/dot_general | solution.py:211
  385.6 38.6 %all-to-all-done.6.refs_1_ = bf16[8,128,896]{2,1,0:T(8,128)(2,1)} async-done(((bf16[8,128,896]{2,1,0:T(8,128)(2,1)}), bf16[8,128,896]{2,1,0:T(8,128)(2,1)}, u32[]{:S(2)}, u32[]{:S(2)}) %all-to-all-start.6) | async-done | bytes 1835040 | tf_op jit(solution)/shard_map/all_to_all | solution.py:232
  424.2 57.5 %reduce-scatter.3.cloned.1.call-done = f32[1,112,4096]{2,1,0:T(8,128)} async-done(((f32[8,112,4096]{2,1,0:T(8,128)}), f32[1,112,4096]{2,1,0:T(8,128)}) %reduce-scatter.3.cloned.1.call-update) | async-done | bytes 1835024 | tf_op jit(solution)/shard_map/reduce_scatter | solution.py:222
  495.7 8.9 %convolution_convert_fusion.8 = bf16[512,896]{1,0:T(8,128)(2,1)S(1)} fusion(bf16[512,4096]{1,0:T(8,128)(2,1)} %copy-done.57, bf16[896,4096]{1,0:T(8,128)(2,1)} %copy-done.51), kind=kOutput, calls=%fused_computation.122 | convolution fusion | flops 3758555136 | bytes 12451840 | tf_op jit(solution)/shard_map/pz,xz->px/dot_general | solution.py:108
  507.0 53.5 %all-to-all-done.7.refs_2_ = bf16[8,128,896]{2,1,0:T(8,128)(2,1)} async-done(((bf16[8,128,896]{2,1,0:T(8,128)(2,1)}), bf16[8,128,896]{2,1,0:T(8,128)(2,1)}, u32[]{:S(2)}, u32[]{:S(2)}) %all-to-all-start.7) | async-done | bytes 1835040 | tf_op jit(solution)/shard_map/all_to_all | solution.py:232
  599.4 5.8 all-to-all-done.8.refs_3_
  605.2 10.9 %shard_map.110 = f32[32,128,896]{2,1,0:T(8,128)} custom-call(s32[32]{0:T(128)} %reshape.248.rows_ref, bf16[8,128,896]{2,1,0:T(8,128)(2,1)} %all-to-all-done.5.refs_0_, bf16[8,128,896]{2,1,0:T(8,128)(2,1)} %all-to-all-done.6.refs_1_, bf16[8,128,896]{2,1,0:T(8,128)(2,1)} %all-to-all-done.7.refs_2_, bf16[8,128,896]{2,1,0:T(8,128)(2,1)} %all-to-all-done.8.refs_3_), custom_call_target="tpu_custom_call" | custom-call | tf_op jit(solution)/shard_map/pallas_call | solution.py:51
  (378 shorter events, 257.2 us)
Async XLA Ops:
  11.7 18.7 %copy-start.72 = (s32[8]{0:T(128)}, s32[8]{0:T(128)S(1)}, u32[]{:S(2)}) copy-start(s32[8]{0:T(128)S(1)} %get-tuple-element.44) | copy-start | bytes 100
  12.8 22.9 %all-to-all-start = ((s32[4,4,2]{1,2,0:T(2,128)}), s32[4,4,2]{1,2,0:T(2,128)S(1)}, u32[]{:S(2)}, u32[]{:S(2)}) async-start(s32[4,4,2]{1,2,0:T(2,128)} %copy.146), calls=%async_computation | async-start | bytes 8192 | tf_op jit(solution)/shard_map/all_to_all | solution.py:148
  21.0 51.5 %collective-permute-start.1 = (bf16[2,63,2048]{2,1,0:T(8,128)(2,1)}, bf16[2,63,2048]{2,1,0:T(8,128)(2,1)}, u32[]{:S(2)}, u32[]{:S(2)}) collective-permute-start(bf16[2,63,2048]{2,1,0:T(8,128)(2,1)} %slice.117), channel_id=1, source_target_pairs={{1,0},{2,1},{3,2},{4,3},{5,4},{6,5},{7,6},{9,8},{10,9},{11,10},{12... | collective-permute-start | bytes 1548296 | tf_op jit(solution)/shard_map/ppermute | solution.py:19
  24.2 46.3 %collective-permute-start = (bf16[2,63,2048]{2,1,0:T(8,128)(2,1)}, bf16[2,63,2048]{2,1,0:T(8,128)(2,1)}, u32[]{:S(2)}, u32[]{:S(2)}) collective-permute-start(bf16[2,63,2048]{2,1,0:T(8,128)(2,1)} %slice.113), channel_id=1, source_target_pairs={{1,0},{2,1},{3,2},{4,3},{5,4},{6,5},{7,6},{9,8},{10,9},{11,10},{12... | collective-permute-start | bytes 1548296 | tf_op jit(solution)/shard_map/ppermute | solution.py:19
  58.6 48.8 %all-to-all-start.1 = ((bf16[8,128,896]{2,1,0:T(8,128)(2,1)}), bf16[8,128,896]{2,1,0:T(8,128)(2,1)}, u32[]{:S(2)}, u32[]{:S(2)}) async-start(bf16[8,128,896]{2,1,0:T(8,128)(2,1)} %broadcast_select_fusion.7), calls=%async_computation.1 | async-start | bytes 3670016 | tf_op jit(solution)/shard_map/all_to_all | solution.py:165
  107.4 53.7 %all-to-all-start.2 = ((bf16[8,128,896]{2,1,0:T(8,128)(2,1)}), bf16[8,128,896]{2,1,0:T(8,128)(2,1)}, u32[]{:S(2)}, u32[]{:S(2)}) async-start(bf16[8,128,896]{2,1,0:T(8,128)(2,1)} %broadcast_select_fusion.6), calls=%async_computation.2 | async-start | bytes 3670016 | tf_op jit(solution)/shard_map/all_to_all | solution.py:165
  161.1 54.2 %all-to-all-start.3 = ((bf16[8,128,896]{2,1,0:T(8,128)(2,1)}), bf16[8,128,896]{2,1,0:T(8,128)(2,1)}, u32[]{:S(2)}, u32[]{:S(2)}) async-start(bf16[8,128,896]{2,1,0:T(8,128)(2,1)} %broadcast_select_fusion.5), calls=%async_computation.3 | async-start | bytes 3670016 | tf_op jit(solution)/shard_map/all_to_all | solution.py:165
  185.6 9.3 %copy-start.19 = (f32[2,16,64,256]{3,2,1,0:T(8,128)}, f32[2,16,64,256]{3,2,1,0:T(8,128)S(1)}, u32[]{:S(2)}) copy-start(f32[2,16,64,256]{3,2,1,0:T(8,128)S(1)} %get-tuple-element.83) | copy-start | bytes 6291460
  215.3 47.4 %all-to-all-start.4 = ((bf16[8,128,896]{2,1,0:T(8,128)(2,1)}), bf16[8,128,896]{2,1,0:T(8,128)(2,1)}, u32[]{:S(2)}, u32[]{:S(2)}) async-start(bf16[8,128,896]{2,1,0:T(8,128)(2,1)} %broadcast_select_fusion.3), calls=%async_computation.4 | async-start | bytes 3670016 | tf_op jit(solution)/shard_map/all_to_all | solution.py:165
  237.4 9.6 %copy-start.21 = (f32[2,16,64,256]{3,2,1,0:T(8,128)}, f32[2,16,64,256]{3,2,1,0:T(8,128)S(1)}, u32[]{:S(2)}) copy-start(f32[2,16,64,256]{3,2,1,0:T(8,128)S(1)} %get-tuple-element.87) | copy-start | bytes 6291460
  247.8 21.2 %copy-start.12 = (bf16[2,16,64,256]{3,2,1,0:T(8,128)(2,1)}, bf16[2,16,64,256]{3,2,1,0:T(8,128)(2,1)S(1)}, u32[]{:S(2)}) copy-start(bf16[2,16,64,256]{3,2,1,0:T(8,128)(2,1)S(1)} %multiply_convert_fusion.1) | copy-start | bytes 3145732
  262.7 46.5 %all-to-all-start.5 = ((bf16[8,128,896]{2,1,0:T(8,128)(2,1)}), bf16[8,128,896]{2,1,0:T(8,128)(2,1)}, u32[]{:S(2)}, u32[]{:S(2)}) async-start(bf16[8,128,896]{2,1,0:T(8,128)(2,1)} %broadcast_select_fusion.4), calls=%async_computation.5 | async-start | bytes 3670016 | tf_op jit(solution)/shard_map/all_to_all | solution.py:182
  267.1 214.6 %reduce-scatter.3.cloned.1.call-start = ((), (), s32[]{:S(2)}) async-start(), calls=%async_computation.11 | async-start | bytes 16515072 | tf_op jit(solution)/shard_map/reduce_scatter | solution.py:222
  329.2 9.4 %copy-start.23 = (f32[2,16,64,256]{3,2,1,0:T(8,128)}, f32[2,16,64,256]{3,2,1,0:T(8,128)S(1)}, u32[]{:S(2)}) copy-start(f32[2,16,64,256]{3,2,1,0:T(8,128)S(1)} %get-tuple-element.91) | copy-start | bytes 6291460
  377.5 46.7 %all-to-all-start.6 = ((bf16[8,128,896]{2,1,0:T(8,128)(2,1)}), bf16[8,128,896]{2,1,0:T(8,128)(2,1)}, u32[]{:S(2)}, u32[]{:S(2)}) async-start(bf16[8,128,896]{2,1,0:T(8,128)(2,1)} %broadcast_select_fusion.2), calls=%async_computation.6 | async-start | bytes 3670016 | tf_op jit(solution)/shard_map/all_to_all | solution.py:232
  385.6 100.7 %copy-start.1 = (bf16[64,8,16,128]{3,2,1,0:T(8,128)(2,1)S(1)}, bf16[64,8,16,128]{3,2,1,0:T(8,128)(2,1)}, u32[]{:S(2)}) copy-start(bf16[64,8,16,128]{3,2,1,0:T(8,128)(2,1)} %copy-done) | copy-start | bytes 6291460
  385.6 100.7 %copy-start.9 = (bf16[2,16,64,256]{3,2,1,0:T(8,128)(2,1)S(1)}, bf16[2,16,64,256]{3,2,1,0:T(8,128)(2,1)}, u32[]{:S(2)}) copy-start(bf16[2,16,64,256]{3,2,1,0:T(8,128)(2,1)} %copy-done.8) | copy-start | bytes 3145732
  481.6 78.9 %all-to-all-start.7 = ((bf16[8,128,896]{2,1,0:T(8,128)(2,1)}), bf16[8,128,896]{2,1,0:T(8,128)(2,1)}, u32[]{:S(2)}, u32[]{:S(2)}) async-start(bf16[8,128,896]{2,1,0:T(8,128)(2,1)} %broadcast_select_fusion.1), calls=%async_computation.8 | async-start | bytes 3670016 | tf_op jit(solution)/shard_map/all_to_all | solution.py:232
  486.3 111.3 %reduce-scatter.5.cloned.1.call-start = ((), (), s32[]{:S(2)}) async-start(), calls=%async_computation.12 | async-start | bytes 2621440 | tf_op jit(solution)/shard_map/reduce_scatter | solution.py:246
  507.0 58.1 %copy-start.5 = (bf16[64,8,16,128]{3,2,1,0:T(8,128)(2,1)S(1)}, bf16[64,8,16,128]{3,2,1,0:T(8,128)(2,1)}, u32[]{:S(2)}) copy-start(bf16[64,8,16,128]{3,2,1,0:T(8,128)(2,1)} %copy-done.4) | copy-start | bytes 6291460
  507.0 58.1 %copy-start.13 = (bf16[2,16,64,256]{3,2,1,0:T(8,128)(2,1)S(1)}, bf16[2,16,64,256]{3,2,1,0:T(8,128)(2,1)}, u32[]{:S(2)}) copy-start(bf16[2,16,64,256]{3,2,1,0:T(8,128)(2,1)} %copy-done.12) | copy-start | bytes 3145732
  560.5 44.7 %all-to-all-start.8 = ((bf16[8,128,896]{2,1,0:T(8,128)(2,1)}), bf16[8,128,896]{2,1,0:T(8,128)(2,1)}, u32[]{:S(2)}, u32[]{:S(2)}) async-start(bf16[8,128,896]{2,1,0:T(8,128)(2,1)} %broadcast_select_fusion), calls=%async_computation.9 | async-start | bytes 3670016 | tf_op jit(solution)/shard_map/all_to_all | solution.py:232
  578.8 12.7 %collective-permute-start.2 = (bf16[2,63,2048]{2,1,0:T(8,128)(2,1)}, bf16[2,63,2048]{2,1,0:T(8,128)(2,1)}, u32[]{:S(2)}, u32[]{:S(2)}) collective-permute-start(bf16[2,63,2048]{2,1,0:T(8,128)(2,1)} %slice.167), channel_id=1, source_target_pairs={{0,1},{1,2},{2,3},{3,4},{4,5},{5,6},{6,7},{8,9},{9,10},{10,11},{11... | collective-permute-start | bytes 1548296 | tf_op jit(solution)/shard_map/ppermute | solution.py:19
  587.7 8.0 %collective-permute-start.3 = (bf16[2,63,2048]{2,1,0:T(8,128)(2,1)S(1)}, bf16[2,63,2048]{2,1,0:T(8,128)(2,1)S(1)}, u32[]{:S(2)}, u32[]{:S(2)}) collective-permute-start(bf16[2,63,2048]{2,1,0:T(8,128)(2,1)S(1)} %slice.170), channel_id=1, source_target_pairs={{0,1},{1,2},{2,3},{3,4},{4,5},{5,6},{6,7},{8,9},{9,10},{10,11},{11... | collective-permute-start | bytes 1548296 | tf_op jit(solution)/shard_map/ppermute | solution.py:19
  (71 other events, 254.0 us)
Sparse Core Ops, SparseCore 0:
  377.6 104.0 reduce-scatter.2
  495.8 65.2 reduce-scatter.4

commit v11 on v9

--- a/solution.py
+++ b/solution.py
@@ -170,10 +170,22 @@
     grads_out = []
     seq_major = []
     proj_parts = []
+
+    def weight_term(first, last):
+        return jnp.einsum(
+            "px,pz->xz",
+            jnp.concatenate(seq_major[first:last], axis=0),
+            jnp.concatenate(proj_parts[first:last], axis=0),
+            preferred_element_type=jnp.float32,
+        )
+
     for g in range(chunk_count):
         incoming = fetched[g][1]
         if g + 1 < chunk_count:
             incoming, _ = lax.optimization_barrier((incoming, fetched[g + 1][0]))
+        if g >= 1 and g == chunk_count - 1:
+            early_terms = weight_term(0, g)
+            incoming, early_terms = lax.optimization_barrier((incoming, early_terms))
         neighbours = jnp.take(incoming, slot_indices[g], axis=0).reshape(
             chunk_refs * NB_LEN, ENC
         )
@@ -199,17 +211,9 @@
         )
         proj_parts.append(proj_grads)
 
-    def weight_term(first, last):
-        return jnp.einsum(
-            "px,pz->xz",
-            jnp.concatenate(seq_major[first:last], axis=0),
-            jnp.concatenate(proj_parts[first:last], axis=0),
-            preferred_element_type=jnp.float32,
-        )
-
     weight_terms = weight_term(chunk_count - 1, chunk_count)
     if chunk_count > 1:
-        weight_terms = weight_term(0, chunk_count - 1) + weight_terms
+        weight_terms = early_terms + weight_terms
 
     plane_sums = lax.psum_scatter(
         weight_terms.reshape(seq_total, shard_count * enc_share, 2 * feat_width),

time: 549 us -> 560 us (1.020)
  waiting for transfers between devices: 138 us -> 150 us
    all_to_all x4, waiting for transfers between devices: 23.6 us -> 35.7 us  [local(): link = lax.all_to_all(rows, 'dp', split_axis=0, concat_axis=0, tiled=True)]
    unnamed x173 -> x177, local copies, waits for them, and re-layouts: 43.9 us -> 39.2 us
  transfers between devices with their start and end apart: 15 -> 15, of which waited for: 8 -> 7; matrix products, arithmetic and copies ran while one was open for 45% -> 46% of each run, Pallas kernels for 0% -> 0%
where the time goes in v11:
time: 560 us; the launch traced here: 551 us
  local copies, waits for them, and re-layouts  151 us (27%)
  waiting for transfers between devices  150 us (27%)
  matrix products  141 us (25%)
  starting transfers between devices  51.1 us (9%)
  other arithmetic  31.1 us (6%)
  between operations  15.7 us (3%)
  Pallas kernels  11.1 us (2%)
    all_to_all x4, waiting for transfers between devices, local(): link = lax.all_to_all(sent, 'dp', split_axis=0, concat_axis=0, tiled=True)  115 us
    unnamed x177, local copies, waits for them, and re-layouts  39.2 us
    all_to_all x4, waiting for transfers between devices, local(): link = lax.all_to_all(rows, 'dp', split_axis=0, concat_axis=0, tiled=True)  35.7 us
    dot_general x4, matrix products, attend_chunk(): jnp.einsum('pz,xz->px', proj_grads, both_weights, preferred_element_type=...  35.4 us
    dot_general x2, matrix products, weight_term(): jnp.einsum('px,pz->xz', jnp.concatenate(seq_major[first:last], axis=0), j...  30.6 us
    dot_general x4, matrix products, attend_chunk(): jnp.dot(neighbours, key_weight, preferred_element_type=jnp.float32)  21.2 us
    gather x4, local copies, waits for them, and re-layouts, local(): rows = jnp.take(database, arrived[:, g, :].reshape(chunk_slots), axis=0)  19.1 us
    all_to_all x4, starting transfers between devices, local(): link = lax.all_to_all(rows, 'dp', split_axis=0, concat_axis=0, tiled=True)  18.9 us
  transfers between devices with their start and end apart: 15, of which 7 were waited for; matrix products, arithmetic and copies ran while one was open for 46% of the time, Pallas kernels for 0%

profile of v11, /device:TPU:0, one launch (start us, length us, event | category | flops | bytes accessed | tf_op | source)
XLA Modules:
  0.0 551.4 jit_solution(8661276335198948348)
XLA Ops:
  14.0 6.3 %all-to-all-start = ((s32[4,4,2]{1,2,0:T(2,128)}), s32[4,4,2]{1,2,0:T(2,128)S(1)}, u32[]{:S(2)}, u32[]{:S(2)}) async-start(s32[4,4,2]{1,2,0:T(2,128)} %copy.146), calls=%async_computation | async-start | bytes 8192 | tf_op jit(solution)/shard_map/all_to_all | solution.py:148
  30.3 5.1 gather_fusion.3
  39.3 5.1 gather_fusion.1
  44.4 5.1 gather_fusion
  52.4 5.1 all-to-all-start.1
  71.1 30.1 %all-to-all-done.1 = bf16[8,128,896]{2,1,0:T(8,128)(2,1)} async-done(((bf16[8,128,896]{2,1,0:T(8,128)(2,1)}), bf16[8,128,896]{2,1,0:T(8,128)(2,1)}, u32[]{:S(2)}, u32[]{:S(2)}) %all-to-all-start.1) | async-done | bytes 1835040 | tf_op jit(solution)/shard_map/all_to_all | solution.py:165
  111.8 4.7 fusion.52
  149.1 4.8 all-to-all-start.3
  157.4 5.8 %fusion.54 = bf16[64,8,16,128]{3,1,2,0:T(8,128)(2,1)} fusion(bf16[512,896]{1,0:T(8,128)(2,1)S(1)} %bitcast.202, bf16[896,2048]{1,0:T(8,128)(2,1)} %param.16), kind=kOutput, calls=%fused_computation.117 | convolution fusion | flops 1880096768 | bytes 6684672 | tf_op jit(solution)/shard_map/dot_general | solution.py:66
  203.5 4.8 fusion.56
  234.7 18.1 %fusion = f32[896,4096]{1,0:T(8,128)} fusion(bf16[512,4096]{1,0:T(8,128)(2,1)} %bitcast_dynamic-update-slice_fusion.2, bf16[512,4096]{1,0:T(8,128)(2,1)} %bitcast_dynamic-update-slice_fusion.4, bf16[512,4096]{1,0:T(8,128)(2,1)} %bitcast_dynamic-update-slice_fusion.6, bf16[512,896]{0,1:T(8,128)(2,1)} %reshape.235, bf16[512,896]{0,1:T(8,128)(2,1)} %reshape.234, ...), kind=kOutput, calls=%fused_computation.12 | convolution fusion | flops 11320295424 | bytes 30015488 | tf_op jit(solution)/shard_map/px,pz->xz/dot_general | solution.py:175
  256.6 5.8 %fusion.58 = bf16[64,8,16,128]{3,1,2,0:T(8,128)(2,1)} fusion(bf16[512,896]{1,0:T(8,128)(2,1)S(1)} %bitcast.204, bf16[896,2048]{1,0:T(8,128)(2,1)} %param.16), kind=kOutput, calls=%fused_computation.121 | convolution fusion | flops 1880096768 | bytes 6684672 | tf_op jit(solution)/shard_map/dot_general | solution.py:66
  291.2 12.6 %convolution_add_fusion = f32[896,4096]{1,0:T(8,128)} fusion(f32[896,4096]{1,0:T(8,128)} %fusion, bf16[512,896]{0,1:T(8,128)(2,1)S(1)} %reshape.252, bf16[512,4096]{1,0:T(8,128)(2,1)S(1)} %bitcast_dynamic-update-slice_fusion), kind=kOutput, calls=%fused_computation.18 | convolution fusion | flops 3761766400 | bytes 34471936 | tf_op jit(solution)/shard_map/px,pz->xz/dot_general | solution.py:175
  308.0 9.6 %convolution_convert_fusion.11 = bf16[512,896]{1,0:T(8,128)(2,1)S(1)} fusion(bf16[512,4096]{1,0:T(8,128)(2,1)} %bitcast_dynamic-update-slice_fusion.6, bf16[896,4096]{1,0:T(8,128)(2,1)S(1)} %constant_dynamic-update-slice_fusion), kind=kOutput, calls=%fused_computation.125 | convolution fusion | flops 3758555136 | bytes 12451840 | tf_op jit(solution)/shard_map/pz,xz->px/dot_general | solution.py:108
  320.1 5.0 all-to-all-start.5
  325.2 9.8 %convolution_convert_fusion.10 = bf16[512,896]{1,0:T(8,128)(2,1)S(1)} fusion(bf16[512,4096]{1,0:T(8,128)(2,1)} %bitcast_dynamic-update-slice_fusion.4, bf16[896,4096]{1,0:T(8,128)(2,1)} %copy-done.56), kind=kOutput, calls=%fused_computation.124 | convolution fusion | flops 3758555136 | bytes 12451840 | tf_op jit(solution)/shard_map/pz,xz->px/dot_general | solution.py:108
  337.5 29.1 %all-to-all-done.5.refs_0_ = bf16[8,128,896]{2,1,0:T(8,128)(2,1)} async-done(((bf16[8,128,896]{2,1,0:T(8,128)(2,1)}), bf16[8,128,896]{2,1,0:T(8,128)(2,1)}, u32[]{:S(2)}, u32[]{:S(2)}) %all-to-all-start.5) | async-done | bytes 1835040 | tf_op jit(solution)/shard_map/all_to_all | solution.py:229
  374.6 7.0 %convolution_convert_fusion.9 = bf16[512,896]{1,0:T(8,128)(2,1)S(1)} fusion(bf16[512,4096]{1,0:T(8,128)(2,1)S(1)} %copy-done.58, bf16[896,4096]{1,0:T(8,128)(2,1)} %copy-done.56), kind=kOutput, calls=%fused_computation.123 | convolution fusion | flops 3758555136 | bytes 12451840 | tf_op jit(solution)/shard_map/pz,xz->px/dot_general | solution.py:108
  384.2 29.1 %all-to-all-done.6.refs_1_ = bf16[8,128,896]{2,1,0:T(8,128)(2,1)} async-done(((bf16[8,128,896]{2,1,0:T(8,128)(2,1)}), bf16[8,128,896]{2,1,0:T(8,128)(2,1)}, u32[]{:S(2)}, u32[]{:S(2)}) %all-to-all-start.6) | async-done | bytes 1835040 | tf_op jit(solution)/shard_map/all_to_all | solution.py:229
  427.2 8.9 %convolution_convert_fusion.8 = bf16[512,896]{1,0:T(8,128)(2,1)S(1)} fusion(bf16[512,4096]{1,0:T(8,128)(2,1)} %copy-done.16, bf16[896,4096]{1,0:T(8,128)(2,1)} %copy-done.56), kind=kOutput, calls=%fused_computation.122 | convolution fusion | flops 3758555136 | bytes 12451840 | tf_op jit(solution)/shard_map/pz,xz->px/dot_general | solution.py:108
  438.5 50.1 %all-to-all-done.7.refs_2_ = bf16[8,128,896]{2,1,0:T(8,128)(2,1)} async-done(((bf16[8,128,896]{2,1,0:T(8,128)(2,1)}), bf16[8,128,896]{2,1,0:T(8,128)(2,1)}, u32[]{:S(2)}, u32[]{:S(2)}) %all-to-all-start.7) | async-done | bytes 1835040 | tf_op jit(solution)/shard_map/all_to_all | solution.py:229
  488.6 4.6 all-to-all-start.8
  526.7 6.5 %all-to-all-done.8.refs_3_ = bf16[8,128,896]{2,1,0:T(8,128)(2,1)} async-done(((bf16[8,128,896]{2,1,0:T(8,128)(2,1)}), bf16[8,128,896]{2,1,0:T(8,128)(2,1)}, u32[]{:S(2)}, u32[]{:S(2)}) %all-to-all-start.8) | async-done | bytes 1835040 | tf_op jit(solution)/shard_map/all_to_all | solution.py:229
  533.2 11.1 %shard_map.110 = f32[32,128,896]{2,1,0:T(8,128)} custom-call(s32[32]{0:T(128)} %reshape.248.rows_ref, bf16[8,128,896]{2,1,0:T(8,128)(2,1)} %all-to-all-done.5.refs_0_, bf16[8,128,896]{2,1,0:T(8,128)(2,1)} %all-to-all-done.6.refs_1_, bf16[8,128,896]{2,1,0:T(8,128)(2,1)} %all-to-all-done.7.refs_2_, bf16[8,128,896]{2,1,0:T(8,128)(2,1)} %all-to-all-done.8.refs_3_), custom_call_target="tpu_custom_call" | custom-call | tf_op jit(solution)/shard_map/pallas_call | solution.py:51
  (384 shorter events, 251.5 us)
Async XLA Ops:
  14.0 15.5 %all-to-all-start = ((s32[4,4,2]{1,2,0:T(2,128)}), s32[4,4,2]{1,2,0:T(2,128)S(1)}, u32[]{:S(2)}, u32[]{:S(2)}) async-start(s32[4,4,2]{1,2,0:T(2,128)} %copy.146), calls=%async_computation | async-start | bytes 8192 | tf_op jit(solution)/shard_map/all_to_all | solution.py:148
  22.2 44.0 %collective-permute-start.1 = (bf16[2,63,2048]{2,1,0:T(8,128)(2,1)}, bf16[2,63,2048]{2,1,0:T(8,128)(2,1)}, u32[]{:S(2)}, u32[]{:S(2)}) collective-permute-start(bf16[2,63,2048]{2,1,0:T(8,128)(2,1)} %slice.120), channel_id=1, source_target_pairs={{1,0},{2,1},{3,2},{4,3},{5,4},{6,5},{7,6},{9,8},{10,9},{11,10},{12... | collective-permute-start | bytes 1548296 | tf_op jit(solution)/shard_map/ppermute | solution.py:19
  25.5 38.7 %collective-permute-start = (bf16[2,63,2048]{2,1,0:T(8,128)(2,1)}, bf16[2,63,2048]{2,1,0:T(8,128)(2,1)}, u32[]{:S(2)}, u32[]{:S(2)}) collective-permute-start(bf16[2,63,2048]{2,1,0:T(8,128)(2,1)} %slice.113), channel_id=1, source_target_pairs={{1,0},{2,1},{3,2},{4,3},{5,4},{6,5},{7,6},{9,8},{10,9},{11,10},{12... | collective-permute-start | bytes 1548296 | tf_op jit(solution)/shard_map/ppermute | solution.py:19
  52.4 48.8 %all-to-all-start.1 = ((bf16[8,128,896]{2,1,0:T(8,128)(2,1)}), bf16[8,128,896]{2,1,0:T(8,128)(2,1)}, u32[]{:S(2)}, u32[]{:S(2)}) async-start(bf16[8,128,896]{2,1,0:T(8,128)(2,1)} %broadcast_select_fusion.7), calls=%async_computation.1 | async-start | bytes 3670016 | tf_op jit(solution)/shard_map/all_to_all | solution.py:165
  101.2 47.9 %all-to-all-start.2 = ((bf16[8,128,896]{2,1,0:T(8,128)(2,1)}), bf16[8,128,896]{2,1,0:T(8,128)(2,1)}, u32[]{:S(2)}, u32[]{:S(2)}) async-start(bf16[8,128,896]{2,1,0:T(8,128)(2,1)} %broadcast_select_fusion.6), calls=%async_computation.2 | async-start | bytes 3670016 | tf_op jit(solution)/shard_map/all_to_all | solution.py:165
  149.1 47.3 %all-to-all-start.3 = ((bf16[8,128,896]{2,1,0:T(8,128)(2,1)}), bf16[8,128,896]{2,1,0:T(8,128)(2,1)}, u32[]{:S(2)}, u32[]{:S(2)}) async-start(bf16[8,128,896]{2,1,0:T(8,128)(2,1)} %broadcast_select_fusion.5), calls=%async_computation.3 | async-start | bytes 3670016 | tf_op jit(solution)/shard_map/all_to_all | solution.py:165
  196.4 56.3 %all-to-all-start.4 = ((bf16[8,128,896]{2,1,0:T(8,128)(2,1)}), bf16[8,128,896]{2,1,0:T(8,128)(2,1)}, u32[]{:S(2)}, u32[]{:S(2)}) async-start(bf16[8,128,896]{2,1,0:T(8,128)(2,1)} %broadcast_select_fusion.4), calls=%async_computation.4 | async-start | bytes 3670016 | tf_op jit(solution)/shard_map/all_to_all | solution.py:165
  200.8 212.4 %reduce-scatter.3.cloned.1.call-start = ((), (), s32[]{:S(2)}) async-start(), calls=%async_computation.11 | async-start | bytes 16515072 | tf_op jit(solution)/shard_map/reduce_scatter | solution.py:218
  234.7 20.4 %copy-start.80 = (pred[4]{0:T(512)(128)(4,1)S(1)}, pred[4]{0:T(512)(128)(4,1)}, u32[]{:S(2)}) copy-start(pred[4]{0:T(512)(128)(4,1)} %get-tuple-element.48) | copy-start | bytes 16
  320.1 46.4 %all-to-all-start.5 = ((bf16[8,128,896]{2,1,0:T(8,128)(2,1)}), bf16[8,128,896]{2,1,0:T(8,128)(2,1)}, u32[]{:S(2)}, u32[]{:S(2)}) async-start(bf16[8,128,896]{2,1,0:T(8,128)(2,1)} %broadcast_select_fusion.3), calls=%async_computation.5 | async-start | bytes 3670016 | tf_op jit(solution)/shard_map/all_to_all | solution.py:229
  337.5 33.7 %copy-start.76 = (s32[8]{0:T(128)S(1)}, s32[8]{0:T(128)}, u32[]{:S(2)}) copy-start(s32[8]{0:T(128)} %get-tuple-element.44) | copy-start | bytes 100
  337.5 33.7 %copy-start.77 = (s32[8]{0:T(128)S(1)}, s32[8]{0:T(128)}, u32[]{:S(2)}) copy-start(s32[8]{0:T(128)} %get-tuple-element.40) | copy-start | bytes 100
  337.5 33.7 %copy-start.19 = (f32[2,16,64,256]{3,2,1,0:T(8,128)S(1)}, f32[2,16,64,256]{3,2,1,0:T(8,128)}, u32[]{:S(2)}) copy-start(f32[2,16,64,256]{3,2,1,0:T(8,128)} %copy-done.18) | copy-start | bytes 6291460
  337.5 33.7 %copy-start.71 = (f32[2,16,64]{2,1,0:T(8,128)S(1)}, f32[2,16,64]{2,1,0:T(8,128)}, u32[]{:S(2)}) copy-start(f32[2,16,64]{2,1,0:T(8,128)} %copy-done.70) | copy-start | bytes 24580
  366.5 46.7 %all-to-all-start.6 = ((bf16[8,128,896]{2,1,0:T(8,128)(2,1)}), bf16[8,128,896]{2,1,0:T(8,128)(2,1)}, u32[]{:S(2)}, u32[]{:S(2)}) async-start(bf16[8,128,896]{2,1,0:T(8,128)(2,1)} %broadcast_select_fusion.2), calls=%async_computation.6 | async-start | bytes 3670016 | tf_op jit(solution)/shard_map/all_to_all | solution.py:229
  384.2 33.5 %copy-start.1 = (bf16[64,8,16,128]{3,2,1,0:T(8,128)(2,1)S(1)}, bf16[64,8,16,128]{3,2,1,0:T(8,128)(2,1)}, u32[]{:S(2)}) copy-start(bf16[64,8,16,128]{3,2,1,0:T(8,128)(2,1)} %copy-done) | copy-start | bytes 6291460
  384.2 33.5 %copy-start.9 = (bf16[2,16,64,256]{3,2,1,0:T(8,128)(2,1)S(1)}, bf16[2,16,64,256]{3,2,1,0:T(8,128)(2,1)}, u32[]{:S(2)}) copy-start(bf16[2,16,64,256]{3,2,1,0:T(8,128)(2,1)} %copy-done.8) | copy-start | bytes 3145732
  413.2 75.4 %all-to-all-start.7 = ((bf16[8,128,896]{2,1,0:T(8,128)(2,1)}), bf16[8,128,896]{2,1,0:T(8,128)(2,1)}, u32[]{:S(2)}, u32[]{:S(2)}) async-start(bf16[8,128,896]{2,1,0:T(8,128)(2,1)} %broadcast_select_fusion.1), calls=%async_computation.8 | async-start | bytes 3670016 | tf_op jit(solution)/shard_map/all_to_all | solution.py:229
  417.7 107.2 %reduce-scatter.5.cloned.1.call-start = ((), (), s32[]{:S(2)}) async-start(), calls=%async_computation.12 | async-start | bytes 2621440 | tf_op jit(solution)/shard_map/reduce_scatter | solution.py:243
  438.5 54.7 %copy-start.5 = (bf16[64,8,16,128]{3,2,1,0:T(8,128)(2,1)S(1)}, bf16[64,8,16,128]{3,2,1,0:T(8,128)(2,1)}, u32[]{:S(2)}) copy-start(bf16[64,8,16,128]{3,2,1,0:T(8,128)(2,1)} %copy-done.4) | copy-start | bytes 6291460
  438.5 54.7 %copy-start.13 = (bf16[2,16,64,256]{3,2,1,0:T(8,128)(2,1)S(1)}, bf16[2,16,64,256]{3,2,1,0:T(8,128)(2,1)}, u32[]{:S(2)}) copy-start(bf16[2,16,64,256]{3,2,1,0:T(8,128)(2,1)} %copy-done.12) | copy-start | bytes 3145732
  488.6 44.6 %all-to-all-start.8 = ((bf16[8,128,896]{2,1,0:T(8,128)(2,1)}), bf16[8,128,896]{2,1,0:T(8,128)(2,1)}, u32[]{:S(2)}, u32[]{:S(2)}) async-start(bf16[8,128,896]{2,1,0:T(8,128)(2,1)} %broadcast_select_fusion), calls=%async_computation.9 | async-start | bytes 3670016 | tf_op jit(solution)/shard_map/all_to_all | solution.py:229
  506.9 11.9 %collective-permute-start.2 = (bf16[2,63,2048]{2,1,0:T(8,128)(2,1)}, bf16[2,63,2048]{2,1,0:T(8,128)(2,1)}, u32[]{:S(2)}, u32[]{:S(2)}) collective-permute-start(bf16[2,63,2048]{2,1,0:T(8,128)(2,1)} %slice.167), channel_id=1, source_target_pairs={{0,1},{1,2},{2,3},{3,4},{4,5},{5,6},{6,7},{8,9},{9,10},{10,11},{11... | collective-permute-start | bytes 1548296 | tf_op jit(solution)/shard_map/ppermute | solution.py:19
  515.8 7.3 %collective-permute-start.3 = (bf16[2,63,2048]{2,1,0:T(8,128)(2,1)S(1)}, bf16[2,63,2048]{2,1,0:T(8,128)(2,1)S(1)}, u32[]{:S(2)}, u32[]{:S(2)}) collective-permute-start(bf16[2,63,2048]{2,1,0:T(8,128)(2,1)S(1)} %slice.170), channel_id=1, source_target_pairs={{0,1},{1,2},{2,3},{3,4},{4,5},{5,6},{6,7},{8,9},{9,10},{10,11},{11... | collective-permute-start | bytes 1548296 | tf_op jit(solution)/shard_map/ppermute | solution.py:19
  (74 other events, 285.5 us)
Sparse Core Ops, SparseCore 0:
  303.9 105.9 reduce-scatter.2
  427.3 64.3 reduce-scatter.4

commit v12 on v9

--- a/solution.py
+++ b/solution.py
@@ -207,6 +207,8 @@
             preferred_element_type=jnp.float32,
         )
 
+    first_sent, _ = lax.optimization_barrier((grads_out[0], link))
+    proj_parts[-1], first_sent = lax.optimization_barrier((proj_parts[-1], first_sent))
     weight_terms = weight_term(chunk_count - 1, chunk_count)
     if chunk_count > 1:
         weight_terms = weight_term(0, chunk_count - 1) + weight_terms
@@ -219,7 +221,10 @@
     )
     returned_parts = []
     for g in range(chunk_count):
-        sent, _ = lax.optimization_barrier((grads_out[g], link))
+        if g == 0:
+            sent = first_sent
+        else:
+            sent, _ = lax.optimization_barrier((grads_out[g], link))
         if g == chunk_count // 2:
             sent, plane_sums = lax.optimization_barrier((sent, plane_sums))
         link = lax.all_to_all(sent, "dp", split_axis=0, concat_axis=0, tiled=True)

time: 549 us -> 561 us (1.022)
  waiting for transfers between devices: 138 us -> 147 us
    reduce_scatter x1, waiting for transfers between devices: 0.01 us -> 12.4 us  [local(): lax.psum_scatter(weight_terms.reshape(seq_total, shard_count * enc_share,...]
    unnamed x173 -> x167, local copies, waits for them, and re-layouts: 43.9 us -> 43 us
  transfers between devices with their start and end apart: 15 -> 15, of which waited for: 8 -> 8; matrix products, arithmetic and copies ran while one was open for 45% -> 44% of each run, Pallas kernels for 0% -> 0%
where the time goes in v12:
time: 561 us; the launch traced here: 553 us
  local copies, waits for them, and re-layouts  155 us (28%)
  waiting for transfers between devices  147 us (26%)
  matrix products  144 us (26%)
  starting transfers between devices  52 us (9%)
  other arithmetic  28.9 us (5%)
  between operations  15.9 us (3%)
  Pallas kernels  10.8 us (2%)
    all_to_all x4, waiting for transfers between devices, local(): link = lax.all_to_all(sent, 'dp', split_axis=0, concat_axis=0, tiled=True)  115 us
    unnamed x167, local copies, waits for them, and re-layouts  43 us
    dot_general x4, matrix products, attend_chunk(): jnp.einsum('pz,xz->px', proj_grads, both_weights, preferred_element_type=...  36.7 us
    dot_general x2, matrix products, weight_term(): jnp.einsum('px,pz->xz', jnp.concatenate(seq_major[first:last], axis=0), j...  27.3 us
    dot_general x4, matrix products, attend_chunk(): jnp.dot(neighbours, key_weight, preferred_element_type=jnp.float32)  23.4 us
    all_to_all x4, starting transfers between devices, local(): link = lax.all_to_all(rows, 'dp', split_axis=0, concat_axis=0, tiled=True)  19.7 us
    all_to_all x4, waiting for transfers between devices, local(): link = lax.all_to_all(rows, 'dp', split_axis=0, concat_axis=0, tiled=True)  19.5 us
    gather x4, local copies, waits for them, and re-layouts, local(): rows = jnp.take(database, arrived[:, g, :].reshape(chunk_slots), axis=0)  18 us
  transfers between devices with their start and end apart: 15, of which 8 were waited for; matrix products, arithmetic and copies ran while one was open for 44% of the time, Pallas kernels for 0%

profile of v12, /device:TPU:0, one launch (start us, length us, event | category | flops | bytes accessed | tf_op | source)
XLA Modules:
  0.0 553.1 jit_solution(11619419863822793429)
XLA Ops:
  13.4 6.3 %all-to-all-start = ((s32[4,4,2]{1,2,0:T(2,128)}), s32[4,4,2]{1,2,0:T(2,128)S(1)}, u32[]{:S(2)}, u32[]{:S(2)}) async-start(s32[4,4,2]{1,2,0:T(2,128)} %copy.146), calls=%async_computation | async-start | bytes 8192 | tf_op jit(solution)/shard_map/all_to_all | solution.py:148
  40.8 5.1 all-to-all-start.1
  49.9 5.1 gather_fusion.3
  55.0 5.1 gather_fusion.5
  72.7 16.9 %all-to-all-done.1 = bf16[8,128,896]{2,1,0:T(8,128)(2,1)} async-done(((bf16[8,128,896]{2,1,0:T(8,128)(2,1)}), bf16[8,128,896]{2,1,0:T(8,128)(2,1)}, u32[]{:S(2)}, u32[]{:S(2)}) %all-to-all-start.1) | async-done | bytes 1835040 | tf_op jit(solution)/shard_map/all_to_all | solution.py:165
  89.6 4.6 all-to-all-start.2
  97.7 5.8 %fusion.55 = bf16[64,8,16,128]{3,1,2,0:T(8,128)(2,1)} fusion(bf16[512,896]{1,0:T(8,128)(2,1)S(1)} %bitcast.198, bf16[896,2048]{1,0:T(8,128)(2,1)} %param.16), kind=kOutput, calls=%fused_computation.115 | convolution fusion | flops 1880096768 | bytes 6684672 | tf_op jit(solution)/shard_map/dot_general | solution.py:66
  132.5 8.4 %convolution_convert_fusion.11 = bf16[512,896]{1,0:T(8,128)(2,1)S(1)} fusion(bf16[512,4096]{1,0:T(8,128)(2,1)S(1)} %bitcast_dynamic-update-slice_fusion.4, bf16[896,4096]{1,0:T(8,128)(2,1)} %copy-done.52), kind=kOutput, calls=%fused_computation.125 | convolution fusion | flops 3758555136 | bytes 12451840 | tf_op jit(solution)/shard_map/pz,xz->px/dot_general | solution.py:108
  143.4 5.5 %all-to-all-start.3 = ((bf16[8,128,896]{2,1,0:T(8,128)(2,1)}), bf16[8,128,896]{2,1,0:T(8,128)(2,1)}, u32[]{:S(2)}, u32[]{:S(2)}) async-start(bf16[8,128,896]{2,1,0:T(8,128)(2,1)} %broadcast_select_fusion.5), calls=%async_computation.3 | async-start | bytes 3670016 | tf_op jit(solution)/shard_map/all_to_all | solution.py:165
  152.5 5.8 %fusion.57 = bf16[64,8,16,128]{3,1,2,0:T(8,128)(2,1)} fusion(bf16[512,896]{1,0:T(8,128)(2,1)S(1)} %bitcast.200, bf16[896,2048]{1,0:T(8,128)(2,1)} %param.16), kind=kOutput, calls=%fused_computation.117 | convolution fusion | flops 1880096768 | bytes 6684672 | tf_op jit(solution)/shard_map/dot_general | solution.py:66
  199.9 5.8 %fusion.59 = bf16[64,8,16,128]{3,1,2,0:T(8,128)(2,1)} fusion(bf16[512,896]{1,0:T(8,128)(2,1)S(1)} %bitcast.202, bf16[896,2048]{1,0:T(8,128)(2,1)} %param.16), kind=kOutput, calls=%fused_computation.119 | convolution fusion | flops 1880096768 | bytes 6684672 | tf_op jit(solution)/shard_map/dot_general | solution.py:66
  242.3 5.8 %fusion.61 = bf16[64,8,16,128]{3,1,2,0:T(8,128)(2,1)} fusion(bf16[512,896]{1,0:T(8,128)(2,1)S(1)} %bitcast.204, bf16[896,2048]{1,0:T(8,128)(2,1)} %param.16), kind=kOutput, calls=%fused_computation.121 | convolution fusion | flops 1880096768 | bytes 6684672 | tf_op jit(solution)/shard_map/dot_general | solution.py:66
  279.0 7.6 %fusion.152 = f32[896,4096]{1,0:T(8,128)} fusion(bf16[512,896]{0,1:T(8,128)(2,1)S(1)} %copy-done.59, bf16[512,4096]{1,0:T(8,128)(2,1)S(1)} %bitcast_dynamic-update-slice_fusion.6), kind=kOutput, calls=%fused_computation.248 | convolution fusion | flops 3758096384 | bytes 19791872 | tf_op jit(solution)/shard_map/px,pz->xz/dot_general | solution.py:203
  286.5 19.7 %fusion.6 = f32[896,4096]{1,0:T(8,128)} fusion(f32[896,4096]{1,0:T(8,128)} %fusion.152, bf16[512,4096]{1,0:T(8,128)(2,1)} %bitcast_dynamic-update-slice_fusion, bf16[512,4096]{1,0:T(8,128)(2,1)} %bitcast_dynamic-update-slice_fusion.2, bf16[512,4096]{1,0:T(8,128)(2,1)S(1)} %copy-done.55, bf16[512,896]{0,1:T(8,128)(2,1)} %reshape.253, ...), kind=kOutput, calls=%fused_computation.18 | convolution fusion | flops 11323965440 | bytes 44695552 | tf_op jit(solution)/shard_map/px,pz->xz/dot_general | solution.py:203
  310.8 10.1 %convolution_convert_fusion.10 = bf16[512,896]{1,0:T(8,128)(2,1)S(1)} fusion(bf16[512,4096]{1,0:T(8,128)(2,1)} %bitcast_dynamic-update-slice_fusion.2, bf16[896,4096]{1,0:T(8,128)(2,1)} %copy-done.52), kind=kOutput, calls=%fused_computation.124 | convolution fusion | flops 3758555136 | bytes 12451840 | tf_op jit(solution)/shard_map/pz,xz->px/dot_general | solution.py:108
  323.4 29.5 %all-to-all-done.5.refs_0_ = bf16[8,128,896]{2,1,0:T(8,128)(2,1)} async-done(((bf16[8,128,896]{2,1,0:T(8,128)(2,1)}), bf16[8,128,896]{2,1,0:T(8,128)(2,1)}, u32[]{:S(2)}, u32[]{:S(2)}) %all-to-all-start.5) | async-done | bytes 1835040 | tf_op jit(solution)/shard_map/all_to_all | solution.py:230
  361.0 9.3 %convolution_convert_fusion.9 = bf16[512,896]{1,0:T(8,128)(2,1)S(1)} fusion(bf16[512,4096]{1,0:T(8,128)(2,1)} %bitcast_dynamic-update-slice_fusion, bf16[896,4096]{1,0:T(8,128)(2,1)} %copy-done.52), kind=kOutput, calls=%fused_computation.123 | convolution fusion | flops 3758555136 | bytes 12451840 | tf_op jit(solution)/shard_map/pz,xz->px/dot_general | solution.py:108
  372.9 26.5 %all-to-all-done.6.refs_1_ = bf16[8,128,896]{2,1,0:T(8,128)(2,1)} async-done(((bf16[8,128,896]{2,1,0:T(8,128)(2,1)}), bf16[8,128,896]{2,1,0:T(8,128)(2,1)}, u32[]{:S(2)}, u32[]{:S(2)}) %all-to-all-start.6) | async-done | bytes 1835040 | tf_op jit(solution)/shard_map/all_to_all | solution.py:230
  399.4 12.4 %reduce-scatter.3.cloned.1.call-done = f32[1,112,4096]{2,1,0:T(8,128)} async-done(((f32[8,112,4096]{2,1,0:T(8,128)}), f32[1,112,4096]{2,1,0:T(8,128)}) %reduce-scatter.3.cloned.1.call-update) | async-done | bytes 1835024 | tf_op jit(solution)/shard_map/reduce_scatter | solution.py:216
  411.9 4.6 all-to-all-start.7
  426.2 8.9 %convolution_convert_fusion.8 = bf16[512,896]{1,0:T(8,128)(2,1)S(1)} fusion(bf16[512,4096]{1,0:T(8,128)(2,1)} %copy-done.56, bf16[896,4096]{1,0:T(8,128)(2,1)} %copy-done.52), kind=kOutput, calls=%fused_computation.122 | convolution fusion | flops 3758555136 | bytes 12451840 | tf_op jit(solution)/shard_map/pz,xz->px/dot_general | solution.py:108
  437.5 53.0 %all-to-all-done.7.refs_2_ = bf16[8,128,896]{2,1,0:T(8,128)(2,1)} async-done(((bf16[8,128,896]{2,1,0:T(8,128)(2,1)}), bf16[8,128,896]{2,1,0:T(8,128)(2,1)}, u32[]{:S(2)}, u32[]{:S(2)}) %all-to-all-start.7) | async-done | bytes 1835040 | tf_op jit(solution)/shard_map/all_to_all | solution.py:230
  529.4 5.6 %all-to-all-done.8.refs_3_ = bf16[8,128,896]{2,1,0:T(8,128)(2,1)} async-done(((bf16[8,128,896]{2,1,0:T(8,128)(2,1)}), bf16[8,128,896]{2,1,0:T(8,128)(2,1)}, u32[]{:S(2)}, u32[]{:S(2)}) %all-to-all-start.8) | async-done | bytes 1835040 | tf_op jit(solution)/shard_map/all_to_all | solution.py:230
  535.0 10.8 %shard_map.110 = f32[32,128,896]{2,1,0:T(8,128)} custom-call(s32[32]{0:T(128)} %reshape.239.rows_ref, bf16[8,128,896]{2,1,0:T(8,128)(2,1)} %all-to-all-done.5.refs_0_, bf16[8,128,896]{2,1,0:T(8,128)(2,1)} %all-to-all-done.6.refs_1_, bf16[8,128,896]{2,1,0:T(8,128)(2,1)} %all-to-all-done.7.refs_2_, bf16[8,128,896]{2,1,0:T(8,128)(2,1)} %all-to-all-done.8.refs_3_), custom_call_target="tpu_custom_call" | custom-call | tf_op jit(solution)/shard_map/pallas_call | solution.py:51
  (375 shorter events, 258.8 us)
Async XLA Ops:
  12.3 17.0 %copy-start.73 = (s32[8]{0:T(128)}, s32[8]{0:T(128)S(1)}, u32[]{:S(2)}) copy-start(s32[8]{0:T(128)S(1)} %get-tuple-element.42) | copy-start | bytes 100
  13.4 21.3 %all-to-all-start = ((s32[4,4,2]{1,2,0:T(2,128)}), s32[4,4,2]{1,2,0:T(2,128)S(1)}, u32[]{:S(2)}, u32[]{:S(2)}) async-start(s32[4,4,2]{1,2,0:T(2,128)} %copy.146), calls=%async_computation | async-start | bytes 8192 | tf_op jit(solution)/shard_map/all_to_all | solution.py:148
  21.6 46.3 %collective-permute-start.2 = (bf16[2,63,2048]{2,1,0:T(8,128)(2,1)}, bf16[2,63,2048]{2,1,0:T(8,128)(2,1)}, u32[]{:S(2)}, u32[]{:S(2)}) collective-permute-start(bf16[2,63,2048]{2,1,0:T(8,128)(2,1)} %slice.123), channel_id=1, source_target_pairs={{1,0},{2,1},{3,2},{4,3},{5,4},{6,5},{7,6},{9,8},{10,9},{11,10},{12... | collective-permute-start | bytes 1548296 | tf_op jit(solution)/shard_map/ppermute | solution.py:19
  24.8 41.1 %collective-permute-start = (bf16[2,63,2048]{2,1,0:T(8,128)(2,1)}, bf16[2,63,2048]{2,1,0:T(8,128)(2,1)}, u32[]{:S(2)}, u32[]{:S(2)}) collective-permute-start(bf16[2,63,2048]{2,1,0:T(8,128)(2,1)} %slice.113), channel_id=1, source_target_pairs={{1,0},{2,1},{3,2},{4,3},{5,4},{6,5},{7,6},{9,8},{10,9},{11,10},{12... | collective-permute-start | bytes 1548296 | tf_op jit(solution)/shard_map/ppermute | solution.py:19
  40.8 48.8 %all-to-all-start.1 = ((bf16[8,128,896]{2,1,0:T(8,128)(2,1)}), bf16[8,128,896]{2,1,0:T(8,128)(2,1)}, u32[]{:S(2)}, u32[]{:S(2)}) async-start(bf16[8,128,896]{2,1,0:T(8,128)(2,1)} %broadcast_select_fusion.7), calls=%async_computation.1 | async-start | bytes 3670016 | tf_op jit(solution)/shard_map/all_to_all | solution.py:165
  89.6 53.8 %all-to-all-start.2 = ((bf16[8,128,896]{2,1,0:T(8,128)(2,1)}), bf16[8,128,896]{2,1,0:T(8,128)(2,1)}, u32[]{:S(2)}, u32[]{:S(2)}) async-start(bf16[8,128,896]{2,1,0:T(8,128)(2,1)} %broadcast_select_fusion.6), calls=%async_computation.2 | async-start | bytes 3670016 | tf_op jit(solution)/shard_map/all_to_all | solution.py:165
  143.4 48.4 %all-to-all-start.3 = ((bf16[8,128,896]{2,1,0:T(8,128)(2,1)}), bf16[8,128,896]{2,1,0:T(8,128)(2,1)}, u32[]{:S(2)}, u32[]{:S(2)}) async-start(bf16[8,128,896]{2,1,0:T(8,128)(2,1)} %broadcast_select_fusion.5), calls=%async_computation.3 | async-start | bytes 3670016 | tf_op jit(solution)/shard_map/all_to_all | solution.py:165
  191.8 46.6 %all-to-all-start.4 = ((bf16[8,128,896]{2,1,0:T(8,128)(2,1)}), bf16[8,128,896]{2,1,0:T(8,128)(2,1)}, u32[]{:S(2)}, u32[]{:S(2)}) async-start(bf16[8,128,896]{2,1,0:T(8,128)(2,1)} %broadcast_select_fusion.4), calls=%async_computation.4 | async-start | bytes 3670016 | tf_op jit(solution)/shard_map/all_to_all | solution.py:165
  196.2 215.7 %reduce-scatter.3.cloned.1.call-start = ((), (), s32[]{:S(2)}) async-start(), calls=%async_computation.11 | async-start | bytes 16515072 | tf_op jit(solution)/shard_map/reduce_scatter | solution.py:216
  306.3 46.6 %all-to-all-start.5 = ((bf16[8,128,896]{2,1,0:T(8,128)(2,1)}), bf16[8,128,896]{2,1,0:T(8,128)(2,1)}, u32[]{:S(2)}, u32[]{:S(2)}) async-start(bf16[8,128,896]{2,1,0:T(8,128)(2,1)} %broadcast_select_fusion.3), calls=%async_computation.5 | async-start | bytes 3670016 | tf_op jit(solution)/shard_map/all_to_all | solution.py:230
  323.4 33.9 %copy-start.71 = (s32[8]{0:T(128)S(1)}, s32[8]{0:T(128)}, u32[]{:S(2)}) copy-start(s32[8]{0:T(128)} %get-tuple-element.44) | copy-start | bytes 100
  323.4 33.9 %copy-start.72 = (s32[8]{0:T(128)S(1)}, s32[8]{0:T(128)}, u32[]{:S(2)}) copy-start(s32[8]{0:T(128)} %get-tuple-element.40) | copy-start | bytes 100
  323.4 34.0 %copy-start.18 = (f32[2,16,64,256]{3,2,1,0:T(8,128)S(1)}, f32[2,16,64,256]{3,2,1,0:T(8,128)}, u32[]{:S(2)}) copy-start(f32[2,16,64,256]{3,2,1,0:T(8,128)} %copy-done.17) | copy-start | bytes 6291460
  323.4 34.0 %copy-start.70 = (f32[2,16,64]{2,1,0:T(8,128)S(1)}, f32[2,16,64]{2,1,0:T(8,128)}, u32[]{:S(2)}) copy-start(f32[2,16,64]{2,1,0:T(8,128)} %copy-done.69) | copy-start | bytes 24580
  352.9 46.5 %all-to-all-start.6 = ((bf16[8,128,896]{2,1,0:T(8,128)(2,1)}), bf16[8,128,896]{2,1,0:T(8,128)(2,1)}, u32[]{:S(2)}, u32[]{:S(2)}) async-start(bf16[8,128,896]{2,1,0:T(8,128)(2,1)} %broadcast_select_fusion.2), calls=%async_computation.6 | async-start | bytes 3670016 | tf_op jit(solution)/shard_map/all_to_all | solution.py:230
  372.9 43.8 %copy-start.1 = (bf16[64,8,16,128]{3,2,1,0:T(8,128)(2,1)S(1)}, bf16[64,8,16,128]{3,2,1,0:T(8,128)(2,1)}, u32[]{:S(2)}) copy-start(bf16[64,8,16,128]{3,2,1,0:T(8,128)(2,1)} %copy-done) | copy-start | bytes 6291460
  372.9 43.8 %copy-start.9 = (bf16[2,16,64,256]{3,2,1,0:T(8,128)(2,1)S(1)}, bf16[2,16,64,256]{3,2,1,0:T(8,128)(2,1)}, u32[]{:S(2)}) copy-start(bf16[2,16,64,256]{3,2,1,0:T(8,128)(2,1)} %copy-done.8) | copy-start | bytes 3145732
  411.9 78.7 %all-to-all-start.7 = ((bf16[8,128,896]{2,1,0:T(8,128)(2,1)}), bf16[8,128,896]{2,1,0:T(8,128)(2,1)}, u32[]{:S(2)}, u32[]{:S(2)}) async-start(bf16[8,128,896]{2,1,0:T(8,128)(2,1)} %broadcast_select_fusion.1), calls=%async_computation.8 | async-start | bytes 3670016 | tf_op jit(solution)/shard_map/all_to_all | solution.py:230
  416.5 111.1 %reduce-scatter.5.cloned.1.call-start = ((), (), s32[]{:S(2)}) async-start(), calls=%async_computation.12 | async-start | bytes 2621440 | tf_op jit(solution)/shard_map/reduce_scatter | solution.py:244
  437.5 57.4 %copy-start.5 = (bf16[64,8,16,128]{3,2,1,0:T(8,128)(2,1)S(1)}, bf16[64,8,16,128]{3,2,1,0:T(8,128)(2,1)}, u32[]{:S(2)}) copy-start(bf16[64,8,16,128]{3,2,1,0:T(8,128)(2,1)} %copy-done.4) | copy-start | bytes 6291460
  437.5 57.4 %copy-start.13 = (bf16[2,16,64,256]{3,2,1,0:T(8,128)(2,1)S(1)}, bf16[2,16,64,256]{3,2,1,0:T(8,128)(2,1)}, u32[]{:S(2)}) copy-start(bf16[2,16,64,256]{3,2,1,0:T(8,128)(2,1)} %copy-done.12) | copy-start | bytes 3145732
  490.5 44.5 %all-to-all-start.8 = ((bf16[8,128,896]{2,1,0:T(8,128)(2,1)}), bf16[8,128,896]{2,1,0:T(8,128)(2,1)}, u32[]{:S(2)}, u32[]{:S(2)}) async-start(bf16[8,128,896]{2,1,0:T(8,128)(2,1)} %broadcast_select_fusion), calls=%async_computation.9 | async-start | bytes 3670016 | tf_op jit(solution)/shard_map/all_to_all | solution.py:230
  508.6 12.9 %collective-permute-start.1 = (bf16[2,63,2048]{2,1,0:T(8,128)(2,1)}, bf16[2,63,2048]{2,1,0:T(8,128)(2,1)}, u32[]{:S(2)}, u32[]{:S(2)}) collective-permute-start(bf16[2,63,2048]{2,1,0:T(8,128)(2,1)} %slice.164), channel_id=1, source_target_pairs={{0,1},{1,2},{2,3},{3,4},{4,5},{5,6},{6,7},{8,9},{9,10},{10,11},{11... | collective-permute-start | bytes 1548296 | tf_op jit(solution)/shard_map/ppermute | solution.py:19
  517.8 8.0 %collective-permute-start.3 = (bf16[2,63,2048]{2,1,0:T(8,128)(2,1)S(1)}, bf16[2,63,2048]{2,1,0:T(8,128)(2,1)S(1)}, u32[]{:S(2)}, u32[]{:S(2)}) collective-permute-start(bf16[2,63,2048]{2,1,0:T(8,128)(2,1)S(1)} %slice.170), channel_id=1, source_target_pairs={{0,1},{1,2},{2,3},{3,4},{4,5},{5,6},{6,7},{8,9},{9,10},{10,11},{11... | collective-permute-start | bytes 1548296 | tf_op jit(solution)/shard_map/ppermute | solution.py:19
  (69 other events, 256.5 us)
Sparse Core Ops, SparseCore 0:
  306.4 105.4 reduce-scatter.2
  426.3 65.0 reduce-scatter.4

commit v13 on v9

--- a/solution.py
+++ b/solution.py
@@ -9,7 +9,7 @@
 ENC = 896
 SPAN = 64
 NB_LEN = 128
-CHUNKS = 4
+CHUNKS = 8
 LEAD = 2
 
 

time: 549 us -> 647 us (1.18)
  matrix products: 144 us -> 233 us
  waiting for transfers between devices: 138 us -> 76.2 us
  starting transfers between devices: 50.2 us -> 89.7 us
  other arithmetic: 27 us -> 64.4 us
  local copies, waits for them, and re-layouts: 155 us -> 144 us
    all_to_all x4 -> x8, waiting for transfers between devices: 114 us -> 70.4 us  [local(): link = lax.all_to_all(sent, 'dp', split_axis=0, concat_axis=0, tiled=True)]
    convert_element_type x8 -> x0, local copies, waits for them, and re-layouts: 30.2 us -> none  [the longest x4 18 us: attend_chunk(): value_grads = jnp.einsum('chqk,cqhd->ckhd', weight_half, grad_blocks, pre...]
    all_to_all x4 -> x8, starting transfers between devices: 18.7 us -> 39.8 us  [local(): link = lax.all_to_all(rows, 'dp', split_axis=0, concat_axis=0, tiled=True)]
    gather x4 -> x8, local copies, waits for them, and re-layouts: 18 us -> 37.3 us  [local(): rows = jnp.take(database, arrived[:, g, :].reshape(chunk_slots), axis=0)]
    unnamed x173 -> x160, local copies, waits for them, and re-layouts: 43.9 us -> 25.1 us
    all_to_all x4 -> x8, starting transfers between devices: 17.8 us -> 36.6 us  [local(): link = lax.all_to_all(sent, 'dp', split_axis=0, concat_axis=0, tiled=True)]
    all_to_all x4 -> x8, waiting for transfers between devices: 23.6 us -> 5.76 us  [local(): link = lax.all_to_all(rows, 'dp', split_axis=0, concat_axis=0, tiled=True)]
    dot_general x4 -> x8, matrix products: 9.01 us -> 25.8 us  [attend_chunk(): jnp.einsum('chqk,cqhd->ckhd', weight_half, grad_blocks, preferred_element...]
  transfers between devices with their start and end apart: 15 -> 23, of which waited for: 8 -> 9; matrix products, arithmetic and copies ran while one was open for 45% -> 61% of each run, Pallas kernels for 0% -> 0%
where the time goes in v13:
time: 647 us; the launch traced here: 636 us
  matrix products  233 us (36%)
  local copies, waits for them, and re-layouts  144 us (22%)
  starting transfers between devices  89.7 us (14%)
  waiting for transfers between devices  76.2 us (12%)
  other arithmetic  64.4 us (10%)
  between operations  16.3 us (3%)
  Pallas kernels  11.1 us (2%)
    all_to_all x8, waiting for transfers between devices, local(): link = lax.all_to_all(sent, 'dp', split_axis=0, concat_axis=0, tiled=True)  70.4 us
    dot_general x8, matrix products, attend_chunk(): jnp.einsum('pz,xz->px', proj_grads, both_weights, preferred_element_type=...  41.9 us
    all_to_all x8, starting transfers between devices, local(): link = lax.all_to_all(rows, 'dp', split_axis=0, concat_axis=0, tiled=True)  39.8 us
    gather x8, local copies, waits for them, and re-layouts, local(): rows = jnp.take(database, arrived[:, g, :].reshape(chunk_slots), axis=0)  37.3 us
    all_to_all x8, starting transfers between devices, local(): link = lax.all_to_all(sent, 'dp', split_axis=0, concat_axis=0, tiled=True)  36.6 us
    dot_general x8, matrix products, attend_chunk(): jnp.dot(neighbours, key_weight, preferred_element_type=jnp.float32)  34.5 us
    dot_general x2, matrix products, weight_term(): jnp.einsum('px,pz->xz', jnp.concatenate(seq_major[first:last], axis=0), j...  32.8 us
    dot_general x8, matrix products, attend_chunk(): jnp.einsum('chqk,cqhd->ckhd', weight_half, grad_blocks, preferred_element...  25.8 us
  transfers between devices with their start and end apart: 23, of which 9 were waited for; matrix products, arithmetic and copies ran while one was open for 61% of the time, Pallas kernels for 0%

profile of v13, /device:TPU:0, one launch (start us, length us, event | category | flops | bytes accessed | tf_op | source)
XLA Modules:
  0.0 635.6 jit_solution(5808016795937509034)
XLA Ops:
  13.1 6.3 all-to-all-start
  153.6 5.5 all-to-all-start.4
  222.4 5.3 all-to-all-start.6
  253.1 5.1 all-to-all-start.7
  281.8 5.1 all-to-all-start.8
  311.0 19.7 %fusion.219 = f32[896,4096]{1,0:T(8,128)} fusion(bf16[1792,896]{0,1:T(8,128)(2,1)S(1)} %constant_dynamic-update-slice_fusion.10, bf16[1792,4096]{0,1:T(8,128)(2,1)} %fusion.28), kind=kOutput, calls=%fused_computation.522 | convolution fusion | flops 13153337344 | bytes 32571392 | tf_op jit(solution)/shard_map/px,pz->xz/dot_general | solution.py:203
  353.0 13.1 %convolution_add_fusion = f32[896,4096]{1,0:T(8,128)} fusion(f32[896,4096]{1,0:T(8,128)} %fusion.219, bf16[256,896]{0,1:T(8,128)(2,1)S(1)} %copy-done.27, bf16[256,2048]{0,1:T(8,128)(2,1)S(1)} %bitcast.570, bf16[256,2048]{0,1:T(8,128)(2,1)S(1)} %bitcast.529), kind=kOutput, calls=%fused_computation.24 | convolution fusion | flops 1886912512 | bytes 31916032 | tf_op jit(solution)/shard_map/px,pz->xz/dot_general | solution.py:203
  378.2 5.5 all-to-all-start.9
  387.5 6.2 fusion.40
  398.0 5.3 all-to-all-done.9.refs_0_
  410.7 5.5 fusion.41
  420.5 8.2 %all-to-all-done.10.refs_1_ = bf16[4,128,896]{2,1,0:T(8,128)(2,1)} async-done(((bf16[4,128,896]{2,1,0:T(8,128)(2,1)}), bf16[4,128,896]{2,1,0:T(8,128)(2,1)}, u32[]{:S(2)}, u32[]{:S(2)}) %all-to-all-start.10) | async-done | bytes 917536 | tf_op jit(solution)/shard_map/all_to_all | solution.py:225
  436.0 5.6 fusion.42
  446.0 9.5 %all-to-all-done.11.refs_2_ = bf16[4,128,896]{2,1,0:T(8,128)(2,1)} async-done(((bf16[4,128,896]{2,1,0:T(8,128)(2,1)}), bf16[4,128,896]{2,1,0:T(8,128)(2,1)}, u32[]{:S(2)}, u32[]{:S(2)}) %all-to-all-start.11) | async-done | bytes 917536 | tf_op jit(solution)/shard_map/all_to_all | solution.py:225
  463.0 5.5 fusion.43
  472.7 9.7 %all-to-all-done.12.refs_3_ = bf16[4,128,896]{2,1,0:T(8,128)(2,1)} async-done(((bf16[4,128,896]{2,1,0:T(8,128)(2,1)}), bf16[4,128,896]{2,1,0:T(8,128)(2,1)}, u32[]{:S(2)}, u32[]{:S(2)}) %all-to-all-start.12) | async-done | bytes 917536 | tf_op jit(solution)/shard_map/all_to_all | solution.py:225
  489.5 5.5 fusion.45
  499.2 9.8 %all-to-all-done.13.refs_4_ = bf16[4,128,896]{2,1,0:T(8,128)(2,1)} async-done(((bf16[4,128,896]{2,1,0:T(8,128)(2,1)}), bf16[4,128,896]{2,1,0:T(8,128)(2,1)}, u32[]{:S(2)}, u32[]{:S(2)}) %all-to-all-start.13) | async-done | bytes 917536 | tf_op jit(solution)/shard_map/all_to_all | solution.py:225
  519.5 5.5 fusion.44
  529.3 21.5 %all-to-all-done.14.refs_5_ = bf16[4,128,896]{2,1,0:T(8,128)(2,1)} async-done(((bf16[4,128,896]{2,1,0:T(8,128)(2,1)}), bf16[4,128,896]{2,1,0:T(8,128)(2,1)}, u32[]{:S(2)}, u32[]{:S(2)}) %all-to-all-start.14) | async-done | bytes 917536 | tf_op jit(solution)/shard_map/all_to_all | solution.py:225
  550.8 6.2 all-to-all-start.15
  573.0 5.8 fusion.46
  582.7 6.4 %all-to-all-done.15.refs_6_ = bf16[4,128,896]{2,1,0:T(8,128)(2,1)} async-done(((bf16[4,128,896]{2,1,0:T(8,128)(2,1)}), bf16[4,128,896]{2,1,0:T(8,128)(2,1)}, u32[]{:S(2)}, u32[]{:S(2)}) %all-to-all-start.15) | async-done | bytes 917536 | tf_op jit(solution)/shard_map/all_to_all | solution.py:225
  617.2 11.1 %shard_map.110 = f32[32,128,896]{2,1,0:T(8,128)} custom-call(s32[32]{0:T(128)} %reshape.835.rows_ref, bf16[4,128,896]{2,1,0:T(8,128)(2,1)} %all-to-all-done.9.refs_0_, bf16[4,128,896]{2,1,0:T(8,128)(2,1)} %all-to-all-done.10.refs_1_, bf16[4,128,896]{2,1,0:T(8,128)(2,1)} %all-to-all-done.11.refs_2_, bf16[4,128,896]{2,1,0:T(8,128)(2,1)} %all-to-all-done.12.refs_3_, ...), custom_call_target="tpu_custom_call" | custom-call | tf_op jit(solution)/shard_map/pallas_call | solution.py:51
  (495 shorter events, 426.5 us)
Async XLA Ops:
  13.1 13.8 %all-to-all-start = ((s32[4,8,1]{1,2,0:T(1,128)}), s32[4,8,1]{1,2,0:T(1,128)S(1)}, u32[]{:S(2)}, u32[]{:S(2)}) async-start(s32[4,8,1]{1,2,0:T(1,128)} %copy.246), calls=%async_computation | async-start | bytes 4096 | tf_op jit(solution)/shard_map/all_to_all | solution.py:148
  21.4 64.6 %collective-permute-start.2 = (bf16[2,63,2048]{2,1,0:T(8,128)(2,1)}, bf16[2,63,2048]{2,1,0:T(8,128)(2,1)}, u32[]{:S(2)}, u32[]{:S(2)}) collective-permute-start(bf16[2,63,2048]{2,1,0:T(8,128)(2,1)} %slice.211), channel_id=1, source_target_pairs={{1,0},{2,1},{3,2},{4,3},{5,4},{6,5},{7,6},{9,8},{10,9},{11,10},{12... | collective-permute-start | bytes 1548296 | tf_op jit(solution)/shard_map/ppermute | solution.py:19
  24.6 59.4 %collective-permute-start = (bf16[2,63,2048]{2,1,0:T(8,128)(2,1)}, bf16[2,63,2048]{2,1,0:T(8,128)(2,1)}, u32[]{:S(2)}, u32[]{:S(2)}) collective-permute-start(bf16[2,63,2048]{2,1,0:T(8,128)(2,1)} %slice.193), channel_id=1, source_target_pairs={{1,0},{2,1},{3,2},{4,3},{5,4},{6,5},{7,6},{9,8},{10,9},{11,10},{12... | collective-permute-start | bytes 1548296 | tf_op jit(solution)/shard_map/ppermute | solution.py:19
  62.9 29.1 %all-to-all-start.1 = ((bf16[4,128,896]{2,1,0:T(8,128)(2,1)}), bf16[4,128,896]{2,1,0:T(8,128)(2,1)}, u32[]{:S(2)}, u32[]{:S(2)}) async-start(bf16[4,128,896]{2,1,0:T(8,128)(2,1)} %broadcast_select_fusion.15), calls=%async_computation.1 | async-start | bytes 1835008 | tf_op jit(solution)/shard_map/all_to_all | solution.py:165
  92.0 28.3 %all-to-all-start.2 = ((bf16[4,128,896]{2,1,0:T(8,128)(2,1)}), bf16[4,128,896]{2,1,0:T(8,128)(2,1)}, u32[]{:S(2)}, u32[]{:S(2)}) async-start(bf16[4,128,896]{2,1,0:T(8,128)(2,1)} %broadcast_select_fusion.14), calls=%async_computation.2 | async-start | bytes 1835008 | tf_op jit(solution)/shard_map/all_to_all | solution.py:165
  120.3 33.3 %all-to-all-start.3 = ((bf16[4,128,896]{2,1,0:T(8,128)(2,1)}), bf16[4,128,896]{2,1,0:T(8,128)(2,1)}, u32[]{:S(2)}, u32[]{:S(2)}) async-start(bf16[4,128,896]{2,1,0:T(8,128)(2,1)} %broadcast_select_fusion.13), calls=%async_computation.3 | async-start | bytes 1835008 | tf_op jit(solution)/shard_map/all_to_all | solution.py:165
  153.6 36.3 %all-to-all-start.4 = ((bf16[4,128,896]{2,1,0:T(8,128)(2,1)}), bf16[4,128,896]{2,1,0:T(8,128)(2,1)}, u32[]{:S(2)}, u32[]{:S(2)}) async-start(bf16[4,128,896]{2,1,0:T(8,128)(2,1)} %broadcast_select_fusion.12), calls=%async_computation.4 | async-start | bytes 1835008 | tf_op jit(solution)/shard_map/all_to_all | solution.py:165
  189.9 32.5 %all-to-all-start.5 = ((bf16[4,128,896]{2,1,0:T(8,128)(2,1)}), bf16[4,128,896]{2,1,0:T(8,128)(2,1)}, u32[]{:S(2)}, u32[]{:S(2)}) async-start(bf16[4,128,896]{2,1,0:T(8,128)(2,1)} %broadcast_select_fusion.11), calls=%async_computation.5 | async-start | bytes 1835008 | tf_op jit(solution)/shard_map/all_to_all | solution.py:165
  222.4 30.7 %all-to-all-start.6 = ((bf16[4,128,896]{2,1,0:T(8,128)(2,1)}), bf16[4,128,896]{2,1,0:T(8,128)(2,1)}, u32[]{:S(2)}, u32[]{:S(2)}) async-start(bf16[4,128,896]{2,1,0:T(8,128)(2,1)} %broadcast_select_fusion.10), calls=%async_computation.6 | async-start | bytes 1835008 | tf_op jit(solution)/shard_map/all_to_all | solution.py:165
  253.1 28.7 %all-to-all-start.7 = ((bf16[4,128,896]{2,1,0:T(8,128)(2,1)}), bf16[4,128,896]{2,1,0:T(8,128)(2,1)}, u32[]{:S(2)}, u32[]{:S(2)}) async-start(bf16[4,128,896]{2,1,0:T(8,128)(2,1)} %broadcast_select_fusion.9), calls=%async_computation.7 | async-start | bytes 1835008 | tf_op jit(solution)/shard_map/all_to_all | solution.py:165
  281.8 48.9 %all-to-all-start.8 = ((bf16[4,128,896]{2,1,0:T(8,128)(2,1)}), bf16[4,128,896]{2,1,0:T(8,128)(2,1)}, u32[]{:S(2)}, u32[]{:S(2)}) async-start(bf16[4,128,896]{2,1,0:T(8,128)(2,1)} %broadcast_select_fusion.8), calls=%async_computation.8 | async-start | bytes 1835008 | tf_op jit(solution)/shard_map/all_to_all | solution.py:165
  286.9 195.5 %reduce-scatter.3.cloned.1.call-start = ((), (), s32[]{:S(2)}) async-start(), calls=%async_computation.19 | async-start | bytes 16515072 | tf_op jit(solution)/shard_map/reduce_scatter | solution.py:214
  378.2 25.2 %all-to-all-start.9 = ((bf16[4,128,896]{2,1,0:T(8,128)(2,1)}), bf16[4,128,896]{2,1,0:T(8,128)(2,1)}, u32[]{:S(2)}, u32[]{:S(2)}) async-start(bf16[4,128,896]{2,1,0:T(8,128)(2,1)} %broadcast_select_fusion.7), calls=%async_computation.9 | async-start | bytes 1835008 | tf_op jit(solution)/shard_map/all_to_all | solution.py:225
  403.3 25.4 %all-to-all-start.10 = ((bf16[4,128,896]{2,1,0:T(8,128)(2,1)}), bf16[4,128,896]{2,1,0:T(8,128)(2,1)}, u32[]{:S(2)}, u32[]{:S(2)}) async-start(bf16[4,128,896]{2,1,0:T(8,128)(2,1)} %broadcast_select_fusion.6), calls=%async_computation.10 | async-start | bytes 1835008 | tf_op jit(solution)/shard_map/all_to_all | solution.py:225
  428.7 26.7 %all-to-all-start.11 = ((bf16[4,128,896]{2,1,0:T(8,128)(2,1)}), bf16[4,128,896]{2,1,0:T(8,128)(2,1)}, u32[]{:S(2)}, u32[]{:S(2)}) async-start(bf16[4,128,896]{2,1,0:T(8,128)(2,1)} %broadcast_select_fusion.5), calls=%async_computation.11 | async-start | bytes 1835008 | tf_op jit(solution)/shard_map/all_to_all | solution.py:225
  455.4 26.9 %all-to-all-start.12 = ((bf16[4,128,896]{2,1,0:T(8,128)(2,1)}), bf16[4,128,896]{2,1,0:T(8,128)(2,1)}, u32[]{:S(2)}, u32[]{:S(2)}) async-start(bf16[4,128,896]{2,1,0:T(8,128)(2,1)} %broadcast_select_fusion.4), calls=%async_computation.12 | async-start | bytes 1835008 | tf_op jit(solution)/shard_map/all_to_all | solution.py:225
  482.3 26.7 %all-to-all-start.13 = ((bf16[4,128,896]{2,1,0:T(8,128)(2,1)}), bf16[4,128,896]{2,1,0:T(8,128)(2,1)}, u32[]{:S(2)}, u32[]{:S(2)}) async-start(bf16[4,128,896]{2,1,0:T(8,128)(2,1)} %broadcast_select_fusion.3), calls=%async_computation.14 | async-start | bytes 1835008 | tf_op jit(solution)/shard_map/all_to_all | solution.py:225
  509.1 41.7 %all-to-all-start.14 = ((bf16[4,128,896]{2,1,0:T(8,128)(2,1)}), bf16[4,128,896]{2,1,0:T(8,128)(2,1)}, u32[]{:S(2)}, u32[]{:S(2)}) async-start(bf16[4,128,896]{2,1,0:T(8,128)(2,1)} %broadcast_select_fusion.2), calls=%async_computation.15 | async-start | bytes 1835008 | tf_op jit(solution)/shard_map/all_to_all | solution.py:225
  513.3 101.1 %reduce-scatter.5.cloned.1.call-start = ((), (), s32[]{:S(2)}) async-start(), calls=%async_computation.20 | async-start | bytes 2621440 | tf_op jit(solution)/shard_map/reduce_scatter | solution.py:239
  550.8 38.3 %all-to-all-start.15 = ((bf16[4,128,896]{2,1,0:T(8,128)(2,1)}), bf16[4,128,896]{2,1,0:T(8,128)(2,1)}, u32[]{:S(2)}, u32[]{:S(2)}) async-start(bf16[4,128,896]{2,1,0:T(8,128)(2,1)} %broadcast_select_fusion.1), calls=%async_computation.16 | async-start | bytes 1835008 | tf_op jit(solution)/shard_map/all_to_all | solution.py:225
  569.8 37.5 %copy-start = (bf16[2,256,2048]{2,1,0:T(8,128)(2,1)}, bf16[2,256,2048]{2,1,0:T(8,128)(2,1)S(1)}, u32[]{:S(2)}) copy-start(bf16[2,256,2048]{2,1,0:T(8,128)(2,1)S(1)} %reshape.824) | copy-start | bytes 6291460
  570.9 36.5 %collective-permute-start.1 = (bf16[2,63,2048]{2,1,0:T(8,128)(2,1)}, bf16[2,63,2048]{2,1,0:T(8,128)(2,1)}, u32[]{:S(2)}, u32[]{:S(2)}) collective-permute-start(bf16[2,63,2048]{2,1,0:T(8,128)(2,1)} %slice.288), channel_id=1, source_target_pairs={{0,1},{1,2},{2,3},{3,4},{4,5},{5,6},{6,7},{8,9},{9,10},{10,11},{11... | collective-permute-start | bytes 1548296 | tf_op jit(solution)/shard_map/ppermute | solution.py:19
  589.1 27.2 %all-to-all-start.16 = ((bf16[4,128,896]{2,1,0:T(8,128)(2,1)}), bf16[4,128,896]{2,1,0:T(8,128)(2,1)S(1)}, u32[]{:S(2)}, u32[]{:S(2)}) async-start(bf16[4,128,896]{2,1,0:T(8,128)(2,1)} %broadcast_select_fusion), calls=%async_computation.17 | async-start | bytes 1835008 | tf_op jit(solution)/shard_map/all_to_all | solution.py:225
  604.5 7.1 %collective-permute-start.3 = (bf16[2,63,2048]{2,1,0:T(8,128)(2,1)S(1)}, bf16[2,63,2048]{2,1,0:T(8,128)(2,1)}, u32[]{:S(2)}, u32[]{:S(2)}) collective-permute-start(bf16[2,63,2048]{2,1,0:T(8,128)(2,1)S(1)} %slice.298), channel_id=1, source_target_pairs={{0,1},{1,2},{2,3},{3,4},{4,5},{5,6},{6,7},{8,9},{9,10},{10,11},{11... | collective-permute-start | bytes 1548296 | tf_op jit(solution)/shard_map/ppermute | solution.py:19
  (73 other events, 407.5 us)
Sparse Core Ops, SparseCore 0:
  366.3 106.2 reduce-scatter.2
  519.6 57.6 reduce-scatter.4

commit v14 on v13

--- a/solution.py
+++ b/solution.py
@@ -9,7 +9,7 @@
 ENC = 896
 SPAN = 64
 NB_LEN = 128
-CHUNKS = 8
+CHUNKS = 2
 LEAD = 2
 
 

time: 647 us -> 573 us (0.89)
  waiting for transfers between devices: 76.2 us -> 188 us
  matrix products: 233 us -> 125 us
  starting transfers between devices: 89.7 us -> 27.7 us
  other arithmetic: 64.4 us -> 36 us
  blocking collectives: 0 us -> 11.7 us
  local copies, waits for them, and re-layouts: 144 us -> 153 us
    all_to_all x8 -> x2, waiting for transfers between devices: 5.76 us -> 57.3 us  [local(): link = lax.all_to_all(rows, 'dp', split_axis=0, concat_axis=0, tiled=True)]
    reduce_scatter x1, waiting for transfers between devices: 0.01 us -> 38.4 us  [local(): lax.psum_scatter(plane_sums.reshape(shard_count, enc_share, 2 * feat_widt...]
    convert_element_type x0 -> x4, local copies, waits for them, and re-layouts: none -> 31.9 us  [the longest x2 16.1 us: attend_chunk(): key_grads = jnp.einsum('chqk,cqhd->ckhd', score_grads, query_blocks, pref...]
    all_to_all x8 -> x2, starting transfers between devices: 39.8 us -> 9.55 us  [local(): link = lax.all_to_all(rows, 'dp', split_axis=0, concat_axis=0, tiled=True)]
    all_to_all x8 -> x2, starting transfers between devices: 36.6 us -> 9.64 us  [local(): link = lax.all_to_all(sent, 'dp', split_axis=0, concat_axis=0, tiled=True)]
    gather x8 -> x2, local copies, waits for them, and re-layouts: 37.3 us -> 11.8 us  [local(): rows = jnp.take(database, arrived[:, g, :].reshape(chunk_slots), axis=0)]
    all_to_all x8 -> x2, waiting for transfers between devices: 70.4 us -> 91.9 us  [local(): link = lax.all_to_all(sent, 'dp', split_axis=0, concat_axis=0, tiled=True)]
    dot_general x8 -> x2, matrix products: 25.8 us -> 6.36 us  [attend_chunk(): jnp.einsum('chqk,cqhd->ckhd', weight_half, grad_blocks, preferred_element...]
  transfers between devices with their start and end apart: 23 -> 10, of which waited for: 9 -> 4; matrix products, arithmetic and copies ran while one was open for 61% -> 35% of each run, Pallas kernels for 0% -> 0%
where the time goes in v14:
time: 573 us; the launch traced here: 567 us
  waiting for transfers between devices  188 us (33%)
  local copies, waits for them, and re-layouts  153 us (27%)
  matrix products  125 us (22%)
  other arithmetic  36 us (6%)
  starting transfers between devices  27.7 us (5%)
  between operations  15 us (3%)
  blocking collectives  11.7 us (2%)
  Pallas kernels  11.1 us (2%)
    all_to_all x2, waiting for transfers between devices, local(): link = lax.all_to_all(sent, 'dp', split_axis=0, concat_axis=0, tiled=True)  91.9 us
    all_to_all x2, waiting for transfers between devices, local(): link = lax.all_to_all(rows, 'dp', split_axis=0, concat_axis=0, tiled=True)  57.3 us
    reduce_scatter x1, waiting for transfers between devices, local(): lax.psum_scatter(plane_sums.reshape(shard_count, enc_share, 2 * feat_widt...  38.4 us
    unnamed x77, local copies, waits for them, and re-layouts  37.5 us
    dot_general x2, matrix products, attend_chunk(): jnp.einsum('pz,xz->px', proj_grads, both_weights, preferred_element_type=...  29.1 us
    dot_general x2, matrix products, weight_term(): jnp.einsum('px,pz->xz', jnp.concatenate(seq_major[first:last], axis=0), j...  28.1 us
    convert_element_type x2, local copies, waits for them, and re-layouts, attend_chunk(): key_grads = jnp.einsum('chqk,cqhd->ckhd', score_grads, query_blocks, pref...  16.1 us
    convert_element_type x2, local copies, waits for them, and re-layouts, attend_chunk(): value_grads = jnp.einsum('chqk,cqhd->ckhd', weight_half, grad_blocks, pre...  15.8 us
  transfers between devices with their start and end apart: 10, of which 4 were waited for; matrix products, arithmetic and copies ran while one was open for 35% of the time, Pallas kernels for 0%

profile of v14, /device:TPU:0, one launch (start us, length us, event | category | flops | bytes accessed | tf_op | source)
XLA Modules:
  0.0 566.6 jit_solution(3372009034187517494)
XLA Ops:
  10.9 11.7 %all_to_all.25 = s32[4,2,4]{2,1,0:T(2,128)S(1)} all-to-all(s32[4,2,4]{2,1,0:T(2,128)S(1)} %copy.90), channel_id=1, replica_groups=mesh['dp'=4,'seq'=8] {'dp'}, dimensions={0} | all-to-all | bytes 256 | tf_op jit(solution)/shard_map/all_to_all | solution.py:148
  23.3 5.9 %gather_fusion = bf16[16,128,896]{2,1,0:T(8,128)(2,1)} fusion(bf16[32,128,896]{2,1,0:T(8,128)(2,1)} %param.15, s32[1024]{0:T(1024)S(1)} %pad_clamp_fusion.5), kind=kCustom, calls=%fused_computation.clone | custom fusion | bytes 7340096 | tf_op jit(solution)/shard_map/jit(_take)/gather | solution.py:162
  46.7 5.9 %gather_fusion.1 = bf16[16,128,896]{2,1,0:T(8,128)(2,1)} fusion(bf16[32,128,896]{2,1,0:T(8,128)(2,1)} %param.15, s32[1024]{0:T(1024)S(1)} %get-tuple-element.51), kind=kCustom, calls=%fused_computation.3.clone | custom fusion | bytes 7340096 | tf_op jit(solution)/shard_map/jit(_take)/gather | solution.py:162
  61.8 57.3 %all-to-all-done.1 = bf16[16,128,896]{2,1,0:T(8,128)(2,1)} async-done(((bf16[16,128,896]{2,1,0:T(8,128)(2,1)}), bf16[16,128,896]{2,1,0:T(8,128)(2,1)}, u32[]{:S(2)}, u32[]{:S(2)}) %all-to-all-start.1) | async-done | bytes 3670048 | tf_op jit(solution)/shard_map/all_to_all | solution.py:165
  119.1 4.8 all-to-all-start.2
  130.2 7.5 %convert_bitcast_fusion.6 = bf16[128,8,16,128]{3,1,2,0:T(8,128)(2,1)S(1)} fusion(bf16[1024,896]{1,0:T(8,128)(2,1)S(1)} %bitcast.124, bf16[896,2048]{1,0:T(8,128)(2,1)} %param.16), kind=kOutput, calls=%fused_computation.23 | convolution fusion | flops 3760193536 | bytes 9699328 | tf_op jit(solution)/shard_map/dot_general | solution.py:66
  139.8 6.0 %convert_bitcast_fusion.7 = bf16[128,8,16,128]{3,1,2,0:T(8,128)(2,1)} fusion(bf16[1024,896]{1,0:T(8,128)(2,1)S(1)} %bitcast.125, bf16[896,2048]{1,0:T(8,128)(2,1)S(1)} %copy-done.18), kind=kOutput, calls=%fused_computation.24 | convolution fusion | flops 3760193536 | bytes 9699328 | tf_op jit(solution)/shard_map/dot_general | solution.py:69
  167.6 5.6 copy.120
  173.2 7.9 %copy.109 = bf16[4,256,16,128]{3,2,1,0:T(8,128)(2,1)} copy(bf16[4,256,16,128]{1,3,2,0:T(8,128)(2,1)} %convert_bitcast_fusion.2) | data formatting | bytes 8388608 | tf_op jit(solution)/shard_map/convert_element_type | solution.py:98
  181.1 6.1 %multiply_reduce_fusion.1 = (f32[4,16,64]{2,1,0:T(8,128)S(1)}, f32[4,16,64,256]{3,2,1,0:T(8,128)S(1)}) fusion(f32[4,16,64]{2,1,0:T(8,128)S(1)} %get-tuple-element.42, f32[4,16,64,256]{3,2,1,0:T(8,128)} %copy-done.6, bf16[4,256,16,128]{3,2,1,0:T(8,128)(2,1)} %bitcast.128, bf16[4,64,16,128]{3,2,1,0:T(8,128)(2,1)S(1)} %bitcast.137), kind=kOutput, calls=%fused_computation.18 | convolution fusion | flops 272625664 | bytes 13664256 | tf_op jit(solution)/shard_map/cqhd,ckhd->chqk/dot_general | solution.py:85
  193.6 7.9 %copy.107 = bf16[4,256,16,128]{3,2,1,0:T(8,128)(2,1)} copy(bf16[4,256,16,128]{1,3,2,0:T(8,128)(2,1)} %convert_bitcast_fusion.3) | data formatting | bytes 8388608 | tf_op jit(solution)/shard_map/convert_element_type | solution.py:95
  211.4 11.0 %fusion.71 = f32[896,4096]{1,0:T(8,128)} fusion(bf16[1024,896]{0,1:T(8,128)(2,1)S(1)} %copy-done.25, bf16[1024,4096]{1,0:T(8,128)(2,1)S(1)} %bitcast_dynamic-update-slice_fusion.2), kind=kOutput, calls=%fused_computation.130 | convolution fusion | flops 7516192768 | bytes 24903680 | tf_op jit(solution)/shard_map/px,pz->xz/dot_general | solution.py:203
  231.0 8.2 %convert_bitcast_fusion.4 = bf16[128,8,16,128]{3,1,2,0:T(8,128)(2,1)} fusion(bf16[1024,896]{1,0:T(8,128)(2,1)S(1)} %bitcast.126, bf16[896,2048]{1,0:T(8,128)(2,1)} %param.16), kind=kOutput, calls=%fused_computation.20 | convolution fusion | flops 3760193536 | bytes 9699328 | tf_op jit(solution)/shard_map/dot_general | solution.py:66
  239.2 6.3 %convert_bitcast_fusion.5 = bf16[128,8,16,128]{3,1,2,0:T(8,128)(2,1)} fusion(bf16[1024,896]{1,0:T(8,128)(2,1)S(1)} %bitcast.127, bf16[896,2048]{1,0:T(8,128)(2,1)S(1)} %copy-done.19), kind=kOutput, calls=%fused_computation.21 | convolution fusion | flops 3760193536 | bytes 9699328 | tf_op jit(solution)/shard_map/dot_general | solution.py:69
  267.3 7.9 %copy.113 = bf16[4,256,16,128]{3,2,1,0:T(8,128)(2,1)} copy(bf16[4,256,16,128]{1,3,2,0:T(8,128)(2,1)} %convert_bitcast_fusion) | data formatting | bytes 8388608 | tf_op jit(solution)/shard_map/convert_element_type | solution.py:98
  283.9 8.2 %copy.111 = bf16[4,256,16,128]{3,2,1,0:T(8,128)(2,1)} copy(bf16[4,256,16,128]{1,3,2,0:T(8,128)(2,1)} %convert_bitcast_fusion.1) | data formatting | bytes 8388608 | tf_op jit(solution)/shard_map/convert_element_type | solution.py:95
  298.8 17.1 %convolution_add_fusion = f32[896,4096]{1,0:T(8,128)} fusion(f32[896,4096]{1,0:T(8,128)} %fusion.71, bf16[1024,896]{0,1:T(8,128)(2,1)S(1)} %reshape.155, bf16[1024,4096]{1,0:T(8,128)(2,1)S(1)} %bitcast_dynamic-update-slice_fusion), kind=kOutput, calls=%fused_computation.6 | convolution fusion | flops 7519862784 | bytes 39583744 | tf_op jit(solution)/shard_map/px,pz->xz/dot_general | solution.py:203
  319.7 14.4 %convolution_convert_fusion.1 = bf16[1024,896]{1,0:T(8,128)(2,1)S(1)} fusion(bf16[1024,4096]{1,0:T(8,128)(2,1)} %copy-done.22, bf16[896,4096]{1,0:T(8,128)(2,1)S(1)} %constant_dynamic-update-slice_fusion), kind=kOutput, calls=%fused_computation.60 | convolution fusion | flops 7517110272 | bytes 17563648 | tf_op jit(solution)/shard_map/pz,xz->px/dot_general | solution.py:108
  342.0 4.9 all-to-all-start.3
  346.9 14.7 %convolution_convert_fusion = bf16[1024,896]{1,0:T(8,128)(2,1)S(1)} fusion(bf16[1024,4096]{1,0:T(8,128)(2,1)} %copy-done.23, bf16[896,4096]{1,0:T(8,128)(2,1)} %copy-done.24), kind=kOutput, calls=%fused_computation.59 | convolution fusion | flops 7517110272 | bytes 17563648 | tf_op jit(solution)/shard_map/pz,xz->px/dot_general | solution.py:108
  369.1 59.4 %all-to-all-done.3.refs_0_ = bf16[16,128,896]{2,1,0:T(8,128)(2,1)} async-done(((bf16[16,128,896]{2,1,0:T(8,128)(2,1)}), bf16[16,128,896]{2,1,0:T(8,128)(2,1)}, u32[]{:S(2)}, u32[]{:S(2)}) %all-to-all-start.3) | async-done | bytes 3670048 | tf_op jit(solution)/shard_map/all_to_all | solution.py:225
  475.8 38.4 %reduce-scatter.5.cloned.1.call-done = f32[1,28,4096]{2,1,0:T(8,128)} async-done(((f32[4,28,4096]{2,1,0:T(8,128)}), f32[1,28,4096]{2,1,0:T(8,128)}) %reduce-scatter.5.cloned.1.call-update) | async-done | bytes 458768 | tf_op jit(solution)/shard_map/reduce_scatter | solution.py:239
  516.0 32.4 %all-to-all-done.4.refs_1_ = bf16[16,128,896]{2,1,0:T(8,128)(2,1)} async-done(((bf16[16,128,896]{2,1,0:T(8,128)(2,1)}), bf16[16,128,896]{2,1,0:T(8,128)(2,1)}, u32[]{:S(2)}, u32[]{:S(2)}) %all-to-all-start.4) | async-done | bytes 3670048 | tf_op jit(solution)/shard_map/all_to_all | solution.py:225
  548.4 11.1 %shard_map.110 = f32[32,128,896]{2,1,0:T(8,128)} custom-call(s32[32]{0:T(128)} %reshape.147.rows_ref, bf16[16,128,896]{2,1,0:T(8,128)(2,1)} %all-to-all-done.3.refs_0_, bf16[16,128,896]{2,1,0:T(8,128)(2,1)} %all-to-all-done.4.refs_1_), custom_call_target="tpu_custom_call" | custom-call | tf_op jit(solution)/shard_map/pallas_call | solution.py:51
  (193 shorter events, 191.0 us)
Async XLA Ops:
  33.5 85.6 %all-to-all-start.1 = ((bf16[16,128,896]{2,1,0:T(8,128)(2,1)}), bf16[16,128,896]{2,1,0:T(8,128)(2,1)}, u32[]{:S(2)}, u32[]{:S(2)}) async-start(bf16[16,128,896]{2,1,0:T(8,128)(2,1)} %broadcast_select_fusion.3), calls=%async_computation.1 | async-start | bytes 7340032 | tf_op jit(solution)/shard_map/all_to_all | solution.py:165
  38.2 6.8 %copy-start.21 = (bf16[2,256,2048]{2,1,0:T(8,128)(2,1)S(1)}, bf16[2,256,2048]{2,1,0:T(8,128)(2,1)}, u32[]{:S(2)}) copy-start(bf16[2,256,2048]{2,1,0:T(8,128)(2,1)} %param.14) | copy-start | bytes 6291460
  39.5 19.4 %collective-permute-start.2 = (bf16[2,63,2048]{2,1,0:T(8,128)(2,1)S(1)}, bf16[2,63,2048]{2,1,0:T(8,128)(2,1)}, u32[]{:S(2)}, u32[]{:S(2)}) collective-permute-start(bf16[2,63,2048]{2,1,0:T(8,128)(2,1)S(1)} %slice.93), channel_id=1, source_target_pairs={{1,0},{2,1},{3,2},{4,3},{5,4},{6,5},{7,6},{9,8},{10,9},{11,10},{12... | collective-permute-start | bytes 1548296 | tf_op jit(solution)/shard_map/ppermute | solution.py:19
  41.9 15.0 %collective-permute-start = (bf16[2,63,2048]{2,1,0:T(8,128)(2,1)S(1)}, bf16[2,63,2048]{2,1,0:T(8,128)(2,1)}, u32[]{:S(2)}, u32[]{:S(2)}) collective-permute-start(bf16[2,63,2048]{2,1,0:T(8,128)(2,1)S(1)} %slice.85), channel_id=1, source_target_pairs={{1,0},{2,1},{3,2},{4,3},{5,4},{6,5},{7,6},{9,8},{10,9},{11,10},{12... | collective-permute-start | bytes 1548296 | tf_op jit(solution)/shard_map/ppermute | solution.py:19
  119.1 103.4 %all-to-all-start.2 = ((bf16[16,128,896]{2,1,0:T(8,128)(2,1)}), bf16[16,128,896]{2,1,0:T(8,128)(2,1)}, u32[]{:S(2)}, u32[]{:S(2)}) async-start(bf16[16,128,896]{2,1,0:T(8,128)(2,1)} %broadcast_select_fusion.2), calls=%async_computation.2 | async-start | bytes 7340032 | tf_op jit(solution)/shard_map/all_to_all | solution.py:165
  123.9 304.7 %reduce-scatter.3.cloned.1.call-start = ((), (), s32[]{:S(2)}) async-start(), calls=%async_computation.7 | async-start | bytes 16515072 | tf_op jit(solution)/shard_map/reduce_scatter | solution.py:214
  130.2 8.9 %copy-start.13 = (bf16[8,128,896]{2,1,0:T(8,128)(2,1)}, bf16[8,128,896]{2,1,0:T(8,128)(2,1)S(1)}, u32[]{:S(2)}) copy-start(bf16[8,128,896]{2,1,0:T(8,128)(2,1)S(1)} %broadcast_select_fusion.5) | copy-start | bytes 5505028
  139.8 6.0 %copy-start = (bf16[128,8,16,128]{3,2,1,0:T(8,128)(2,1)}, bf16[128,8,16,128]{3,2,1,0:T(8,128)(2,1)S(1)}, u32[]{:S(2)}) copy-start(bf16[128,8,16,128]{3,2,1,0:T(8,128)(2,1)S(1)} %copy.119) | copy-start | bytes 12582916
  147.6 39.6 %copy-start.27 = (f32[4,16,64]{2,1,0:T(8,128)}, f32[4,16,64]{2,1,0:T(8,128)S(1)}, u32[]{:S(2)}) copy-start(f32[4,16,64]{2,1,0:T(8,128)S(1)} %get-tuple-element.42) | copy-start | bytes 49156
  181.1 6.2 %copy-start.7 = (f32[4,16,64,256]{3,2,1,0:T(8,128)S(1)}, f32[4,16,64,256]{3,2,1,0:T(8,128)}, u32[]{:S(2)}) copy-start(f32[4,16,64,256]{3,2,1,0:T(8,128)} %copy-done.6) | copy-start | bytes 12582916
  206.0 5.4 copy-start.25
  231.0 8.2 %copy-start.19 = (bf16[896,2048]{1,0:T(8,128)(2,1)S(1)}, bf16[896,2048]{1,0:T(8,128)(2,1)}, u32[]{:S(2)}) copy-start(bf16[896,2048]{1,0:T(8,128)(2,1)} %param.17) | copy-start | bytes 11010052
  257.6 6.0 %copy-start.15 = (bf16[128,8,16,128]{3,2,1,0:T(8,128)(2,1)}, bf16[128,8,16,128]{3,2,1,0:T(8,128)(2,1)S(1)}, u32[]{:S(2)}) copy-start(bf16[128,8,16,128]{3,2,1,0:T(8,128)(2,1)S(1)} %copy.123) | copy-start | bytes 12582916
  298.8 17.1 %copy-start.23 = (bf16[1024,4096]{1,0:T(8,128)(2,1)}, bf16[1024,4096]{1,0:T(8,128)(2,1)S(1)}, u32[]{:S(2)}) copy-start(bf16[1024,4096]{1,0:T(8,128)(2,1)S(1)} %bitcast_dynamic-update-slice_fusion) | copy-start | bytes 25165828
  319.7 14.4 %copy-start.24 = (bf16[896,4096]{1,0:T(8,128)(2,1)}, bf16[896,4096]{1,0:T(8,128)(2,1)S(1)}, u32[]{:S(2)}) copy-start(bf16[896,4096]{1,0:T(8,128)(2,1)S(1)} %constant_dynamic-update-slice_fusion) | copy-start | bytes 22020100
  342.0 86.6 %all-to-all-start.3 = ((bf16[16,128,896]{2,1,0:T(8,128)(2,1)}), bf16[16,128,896]{2,1,0:T(8,128)(2,1)}, u32[]{:S(2)}, u32[]{:S(2)}) async-start(bf16[16,128,896]{2,1,0:T(8,128)(2,1)} %broadcast_select_fusion.1), calls=%async_computation.3 | async-start | bytes 7340032 | tf_op jit(solution)/shard_map/all_to_all | solution.py:225
  428.5 119.9 %all-to-all-start.4 = ((bf16[16,128,896]{2,1,0:T(8,128)(2,1)}), bf16[16,128,896]{2,1,0:T(8,128)(2,1)}, u32[]{:S(2)}, u32[]{:S(2)}) async-start(bf16[16,128,896]{2,1,0:T(8,128)(2,1)} %broadcast_select_fusion), calls=%async_computation.5 | async-start | bytes 7340032 | tf_op jit(solution)/shard_map/all_to_all | solution.py:225
  433.3 80.9 %reduce-scatter.5.cloned.1.call-start = ((), (), s32[]{:S(2)}) async-start(), calls=%async_computation.8 | async-start | bytes 2621440 | tf_op jit(solution)/shard_map/reduce_scatter | solution.py:239
  440.3 5.1 copy-start.16
  447.5 11.0 %copy-start.5 = (bf16[4,16,64,256]{3,2,1,0:T(8,128)(2,1)S(1)}, bf16[4,16,64,256]{3,2,1,0:T(8,128)(2,1)}, u32[]{:S(2)}) copy-start(bf16[4,16,64,256]{3,2,1,0:T(8,128)(2,1)} %copy-done.4) | copy-start | bytes 6291460
  456.4 14.7 %collective-permute-start.1 = (bf16[2,63,2048]{2,1,0:T(8,128)(2,1)}, bf16[2,63,2048]{2,1,0:T(8,128)(2,1)}, u32[]{:S(2)}, u32[]{:S(2)}) collective-permute-start(bf16[2,63,2048]{2,1,0:T(8,128)(2,1)} %slice.118), channel_id=1, source_target_pairs={{0,1},{1,2},{2,3},{3,4},{4,5},{5,6},{6,7},{8,9},{9,10},{10,11},{11... | collective-permute-start | bytes 1548296 | tf_op jit(solution)/shard_map/ppermute | solution.py:19
  462.2 8.2 %copy-start.30 = (s32[4,2,4]{2,1,0:T(2,128)S(1)}, s32[4,2,4]{2,1,0:T(2,128)}, u32[]{:S(2)}) copy-start(s32[4,2,4]{2,1,0:T(2,128)} %copy-done.29) | copy-start | bytes 388
  465.9 5.1 slice-start
  467.2 6.8 %collective-permute-start.3 = (bf16[2,63,2048]{2,1,0:T(8,128)(2,1)S(1)}, bf16[2,63,2048]{2,1,0:T(8,128)(2,1)S(1)}, u32[]{:S(2)}, u32[]{:S(2)}) collective-permute-start(bf16[2,63,2048]{2,1,0:T(8,128)(2,1)S(1)} %slice.122), channel_id=1, source_target_pairs={{0,1},{1,2},{2,3},{3,4},{4,5},{5,6},{6,7},{8,9},{9,10},{10,11},{11... | collective-permute-start | bytes 1548296 | tf_op jit(solution)/shard_map/ppermute | solution.py:19
  (21 other events, 55.0 us)
Sparse Core Ops, SparseCore 0:
  316.1 104.9 reduce-scatter.2
  437.0 77.1 reduce-scatter.4

commit v15 on v9

--- a/solution.py
+++ b/solution.py
@@ -46,7 +46,7 @@
 
 def row_sums(rows, parts, row_count):
     width = parts[0].shape[1:]
-    block_rows = 8 if row_count % 8 == 0 else row_count
+    block_rows = 4 if row_count % 4 == 0 else row_count
     whole = lambda r, rows_ref: (0, 0, 0)
     return pl.pallas_call(
         _row_sum_kernel,

time: 549 us -> 551 us (level)
  transfers between devices with their start and end apart: 15 -> 15, of which waited for: 8 -> 8; matrix products, arithmetic and copies ran while one was open for 45% -> 44% of each run, Pallas kernels for 0% -> 0%
where the time goes in v15:
time: 551 us; the launch traced here: 543 us
  local copies, waits for them, and re-layouts  155 us (28%)
  matrix products  144 us (26%)
  waiting for transfers between devices  138 us (25%)
  starting transfers between devices  50.2 us (9%)
  other arithmetic  27 us (5%)
  between operations  15.7 us (3%)
  Pallas kernels  12.9 us (2%)
    all_to_all x4, waiting for transfers between devices, local(): link = lax.all_to_all(sent, 'dp', split_axis=0, concat_axis=0, tiled=True)  114 us
    unnamed x173, local copies, waits for them, and re-layouts  43.9 us
    dot_general x4, matrix products, attend_chunk(): jnp.einsum('pz,xz->px', proj_grads, both_weights, preferred_element_type=...  37.1 us
    dot_general x2, matrix products, weight_term(): jnp.einsum('px,pz->xz', jnp.concatenate(seq_major[first:last], axis=0), j...  28.1 us
    all_to_all x4, waiting for transfers between devices, local(): link = lax.all_to_all(rows, 'dp', split_axis=0, concat_axis=0, tiled=True)  23.6 us
    dot_general x4, matrix products, attend_chunk(): jnp.dot(neighbours, key_weight, preferred_element_type=jnp.float32)  22.3 us
    all_to_all x4, starting transfers between devices, local(): link = lax.all_to_all(rows, 'dp', split_axis=0, concat_axis=0, tiled=True)  18.7 us
    gather x4, local copies, waits for them, and re-layouts, local(): rows = jnp.take(database, arrived[:, g, :].reshape(chunk_slots), axis=0)  18 us
  transfers between devices with their start and end apart: 15, of which 8 were waited for; matrix products, arithmetic and copies ran while one was open for 44% of the time, Pallas kernels for 0%

profile of v15, /device:TPU:0, one launch (start us, length us, event | category | flops | bytes accessed | tf_op | source)
XLA Modules:
  0.0 542.5 jit_solution(8769413871720556575)
XLA Ops:
  13.4 6.3 %all-to-all-start = ((s32[4,4,2]{1,2,0:T(2,128)}), s32[4,4,2]{1,2,0:T(2,128)S(1)}, u32[]{:S(2)}, u32[]{:S(2)}) async-start(s32[4,4,2]{1,2,0:T(2,128)} %copy.146), calls=%async_computation | async-start | bytes 8192 | tf_op jit(solution)/shard_map/all_to_all | solution.py:148
  34.6 5.1 all-to-all-start.1
  43.6 5.1 gather_fusion.3
  48.7 5.1 gather_fusion.5
  66.4 16.9 %all-to-all-done.1 = bf16[8,128,896]{2,1,0:T(8,128)(2,1)} async-done(((bf16[8,128,896]{2,1,0:T(8,128)(2,1)}), bf16[8,128,896]{2,1,0:T(8,128)(2,1)}, u32[]{:S(2)}, u32[]{:S(2)}) %all-to-all-start.1) | async-done | bytes 1835040 | tf_op jit(solution)/shard_map/all_to_all | solution.py:165
  83.3 4.6 all-to-all-start.2
  93.9 4.7 fusion.55
  131.2 4.6 all-to-all-start.3
  139.4 5.8 %fusion.57 = bf16[64,8,16,128]{3,1,2,0:T(8,128)(2,1)} fusion(bf16[512,896]{1,0:T(8,128)(2,1)S(1)} %bitcast.200, bf16[896,2048]{1,0:T(8,128)(2,1)} %param.16), kind=kOutput, calls=%fused_computation.117 | convolution fusion | flops 1880096768 | bytes 6684672 | tf_op jit(solution)/shard_map/dot_general | solution.py:66
  186.7 5.8 %fusion.59 = bf16[64,8,16,128]{3,1,2,0:T(8,128)(2,1)} fusion(bf16[512,896]{1,0:T(8,128)(2,1)S(1)} %bitcast.202, bf16[896,2048]{1,0:T(8,128)(2,1)} %param.16), kind=kOutput, calls=%fused_computation.119 | convolution fusion | flops 1880096768 | bytes 6684672 | tf_op jit(solution)/shard_map/dot_general | solution.py:66
  228.6 5.8 %fusion.61 = bf16[64,8,16,128]{3,1,2,0:T(8,128)(2,1)} fusion(bf16[512,896]{1,0:T(8,128)(2,1)S(1)} %bitcast.204, bf16[896,2048]{1,0:T(8,128)(2,1)} %param.16), kind=kOutput, calls=%fused_computation.121 | convolution fusion | flops 1880096768 | bytes 6684672 | tf_op jit(solution)/shard_map/dot_general | solution.py:66
  249.0 4.5 copy.189
  265.0 7.6 %fusion.152 = f32[896,4096]{1,0:T(8,128)} fusion(bf16[512,896]{0,1:T(8,128)(2,1)S(1)} %reshape.252, bf16[512,4096]{1,0:T(8,128)(2,1)S(1)} %bitcast_dynamic-update-slice_fusion), kind=kOutput, calls=%fused_computation.248 | convolution fusion | flops 3758096384 | bytes 19791872 | tf_op jit(solution)/shard_map/px,pz->xz/dot_general | solution.py:203
  272.6 20.5 %fusion.6 = f32[896,4096]{1,0:T(8,128)} fusion(f32[896,4096]{1,0:T(8,128)} %fusion.152, bf16[512,4096]{1,0:T(8,128)(2,1)} %bitcast_dynamic-update-slice_fusion.2, bf16[512,4096]{1,0:T(8,128)(2,1)} %bitcast_dynamic-update-slice_fusion.4, bf16[512,4096]{1,0:T(8,128)(2,1)} %bitcast_dynamic-update-slice_fusion.6, bf16[512,896]{0,1:T(8,128)(2,1)S(1)} %copy-done.59, ...), kind=kOutput, calls=%fused_computation.18 | convolution fusion | flops 11323965440 | bytes 44695552 | tf_op jit(solution)/shard_map/px,pz->xz/dot_general | solution.py:203
  297.5 9.7 %convolution_convert_fusion.11 = bf16[512,896]{1,0:T(8,128)(2,1)S(1)} fusion(bf16[512,4096]{1,0:T(8,128)(2,1)} %bitcast_dynamic-update-slice_fusion.6, bf16[896,4096]{1,0:T(8,128)(2,1)S(1)} %constant_dynamic-update-slice_fusion), kind=kOutput, calls=%fused_computation.125 | convolution fusion | flops 3758555136 | bytes 12451840 | tf_op jit(solution)/shard_map/pz,xz->px/dot_general | solution.py:108
  314.1 9.6 %convolution_convert_fusion.10 = bf16[512,896]{1,0:T(8,128)(2,1)S(1)} fusion(bf16[512,4096]{1,0:T(8,128)(2,1)} %bitcast_dynamic-update-slice_fusion.4, bf16[896,4096]{1,0:T(8,128)(2,1)} %copy-done.54), kind=kOutput, calls=%fused_computation.124 | convolution fusion | flops 3758555136 | bytes 12451840 | tf_op jit(solution)/shard_map/pz,xz->px/dot_general | solution.py:108
  326.1 30.0 %all-to-all-done.5.refs_0_ = bf16[8,128,896]{2,1,0:T(8,128)(2,1)} async-done(((bf16[8,128,896]{2,1,0:T(8,128)(2,1)}), bf16[8,128,896]{2,1,0:T(8,128)(2,1)}, u32[]{:S(2)}, u32[]{:S(2)}) %all-to-all-start.5) | async-done | bytes 1835040 | tf_op jit(solution)/shard_map/all_to_all | solution.py:225
  356.1 4.6 all-to-all-start.6
  364.0 8.9 %convolution_convert_fusion.9 = bf16[512,896]{1,0:T(8,128)(2,1)S(1)} fusion(bf16[512,4096]{1,0:T(8,128)(2,1)} %bitcast_dynamic-update-slice_fusion.2, bf16[896,4096]{1,0:T(8,128)(2,1)} %copy-done.54), kind=kOutput, calls=%fused_computation.123 | convolution fusion | flops 3758555136 | bytes 12451840 | tf_op jit(solution)/shard_map/pz,xz->px/dot_general | solution.py:108
  375.4 27.3 %all-to-all-done.6.refs_1_ = bf16[8,128,896]{2,1,0:T(8,128)(2,1)} async-done(((bf16[8,128,896]{2,1,0:T(8,128)(2,1)}), bf16[8,128,896]{2,1,0:T(8,128)(2,1)}, u32[]{:S(2)}, u32[]{:S(2)}) %all-to-all-start.6) | async-done | bytes 1835040 | tf_op jit(solution)/shard_map/all_to_all | solution.py:225
  416.7 8.9 %convolution_convert_fusion.8 = bf16[512,896]{1,0:T(8,128)(2,1)S(1)} fusion(bf16[512,4096]{1,0:T(8,128)(2,1)} %copy-done.56, bf16[896,4096]{1,0:T(8,128)(2,1)} %copy-done.54), kind=kOutput, calls=%fused_computation.122 | convolution fusion | flops 3758555136 | bytes 12451840 | tf_op jit(solution)/shard_map/pz,xz->px/dot_general | solution.py:108
  428.0 50.2 %all-to-all-done.7.refs_2_ = bf16[8,128,896]{2,1,0:T(8,128)(2,1)} async-done(((bf16[8,128,896]{2,1,0:T(8,128)(2,1)}), bf16[8,128,896]{2,1,0:T(8,128)(2,1)}, u32[]{:S(2)}, u32[]{:S(2)}) %all-to-all-start.7) | async-done | bytes 1835040 | tf_op jit(solution)/shard_map/all_to_all | solution.py:225
  516.0 6.6 %all-to-all-done.8.refs_3_ = bf16[8,128,896]{2,1,0:T(8,128)(2,1)} async-done(((bf16[8,128,896]{2,1,0:T(8,128)(2,1)}), bf16[8,128,896]{2,1,0:T(8,128)(2,1)}, u32[]{:S(2)}, u32[]{:S(2)}) %all-to-all-start.8) | async-done | bytes 1835040 | tf_op jit(solution)/shard_map/all_to_all | solution.py:225
  522.6 12.9 %shard_map.110 = f32[32,128,896]{2,1,0:T(8,128)} custom-call(s32[32]{0:T(128)} %reshape.239.rows_ref, bf16[8,128,896]{2,1,0:T(8,128)(2,1)} %all-to-all-done.5.refs_0_, bf16[8,128,896]{2,1,0:T(8,128)(2,1)} %all-to-all-done.6.refs_1_, bf16[8,128,896]{2,1,0:T(8,128)(2,1)} %all-to-all-done.7.refs_2_, bf16[8,128,896]{2,1,0:T(8,128)(2,1)} %all-to-all-done.8.refs_3_), custom_call_target="tpu_custom_call" | custom-call | tf_op jit(solution)/shard_map/pallas_call | solution.py:51
  (381 shorter events, 255.8 us)
Async XLA Ops:
  7.2 19.1 %copy-start.43 = (bf16[2,256,2048]{2,1,0:T(8,128)(2,1)S(1)}, bf16[2,256,2048]{2,1,0:T(8,128)(2,1)}, u32[]{:S(2)}) copy-start(bf16[2,256,2048]{2,1,0:T(8,128)(2,1)} %param.13) | copy-start | bytes 6291460
  13.4 14.9 %all-to-all-start = ((s32[4,4,2]{1,2,0:T(2,128)}), s32[4,4,2]{1,2,0:T(2,128)S(1)}, u32[]{:S(2)}, u32[]{:S(2)}) async-start(s32[4,4,2]{1,2,0:T(2,128)} %copy.146), calls=%async_computation | async-start | bytes 8192 | tf_op jit(solution)/shard_map/all_to_all | solution.py:148
  21.7 39.9 %collective-permute-start.2 = (bf16[2,63,2048]{2,1,0:T(8,128)(2,1)}, bf16[2,63,2048]{2,1,0:T(8,128)(2,1)}, u32[]{:S(2)}, u32[]{:S(2)}) collective-permute-start(bf16[2,63,2048]{2,1,0:T(8,128)(2,1)} %slice.123), channel_id=1, source_target_pairs={{1,0},{2,1},{3,2},{4,3},{5,4},{6,5},{7,6},{9,8},{10,9},{11,10},{12... | collective-permute-start | bytes 1548296 | tf_op jit(solution)/shard_map/ppermute | solution.py:19
  25.0 34.6 %collective-permute-start = (bf16[2,63,2048]{2,1,0:T(8,128)(2,1)}, bf16[2,63,2048]{2,1,0:T(8,128)(2,1)}, u32[]{:S(2)}, u32[]{:S(2)}) collective-permute-start(bf16[2,63,2048]{2,1,0:T(8,128)(2,1)} %slice.113), channel_id=1, source_target_pairs={{1,0},{2,1},{3,2},{4,3},{5,4},{6,5},{7,6},{9,8},{10,9},{11,10},{12... | collective-permute-start | bytes 1548296 | tf_op jit(solution)/shard_map/ppermute | solution.py:19
  34.6 48.8 %all-to-all-start.1 = ((bf16[8,128,896]{2,1,0:T(8,128)(2,1)}), bf16[8,128,896]{2,1,0:T(8,128)(2,1)}, u32[]{:S(2)}, u32[]{:S(2)}) async-start(bf16[8,128,896]{2,1,0:T(8,128)(2,1)} %broadcast_select_fusion.7), calls=%async_computation.1 | async-start | bytes 3670016 | tf_op jit(solution)/shard_map/all_to_all | solution.py:165
  83.3 47.9 %all-to-all-start.2 = ((bf16[8,128,896]{2,1,0:T(8,128)(2,1)}), bf16[8,128,896]{2,1,0:T(8,128)(2,1)}, u32[]{:S(2)}, u32[]{:S(2)}) async-start(bf16[8,128,896]{2,1,0:T(8,128)(2,1)} %broadcast_select_fusion.6), calls=%async_computation.2 | async-start | bytes 3670016 | tf_op jit(solution)/shard_map/all_to_all | solution.py:165
  131.2 47.1 %all-to-all-start.3 = ((bf16[8,128,896]{2,1,0:T(8,128)(2,1)}), bf16[8,128,896]{2,1,0:T(8,128)(2,1)}, u32[]{:S(2)}, u32[]{:S(2)}) async-start(bf16[8,128,896]{2,1,0:T(8,128)(2,1)} %broadcast_select_fusion.5), calls=%async_computation.3 | async-start | bytes 3670016 | tf_op jit(solution)/shard_map/all_to_all | solution.py:165
  178.4 46.5 %all-to-all-start.4 = ((bf16[8,128,896]{2,1,0:T(8,128)(2,1)}), bf16[8,128,896]{2,1,0:T(8,128)(2,1)}, u32[]{:S(2)}, u32[]{:S(2)}) async-start(bf16[8,128,896]{2,1,0:T(8,128)(2,1)} %broadcast_select_fusion.4), calls=%async_computation.4 | async-start | bytes 3670016 | tf_op jit(solution)/shard_map/all_to_all | solution.py:165
  182.8 220.0 %reduce-scatter.3.cloned.1.call-start = ((), (), s32[]{:S(2)}) async-start(), calls=%async_computation.11 | async-start | bytes 16515072 | tf_op jit(solution)/shard_map/reduce_scatter | solution.py:214
  309.6 46.5 %all-to-all-start.5 = ((bf16[8,128,896]{2,1,0:T(8,128)(2,1)}), bf16[8,128,896]{2,1,0:T(8,128)(2,1)}, u32[]{:S(2)}, u32[]{:S(2)}) async-start(bf16[8,128,896]{2,1,0:T(8,128)(2,1)} %broadcast_select_fusion.3), calls=%async_computation.5 | async-start | bytes 3670016 | tf_op jit(solution)/shard_map/all_to_all | solution.py:225
  326.1 34.5 %copy-start.75 = (s32[8]{0:T(128)S(1)}, s32[8]{0:T(128)}, u32[]{:S(2)}) copy-start(s32[8]{0:T(128)} %get-tuple-element.40) | copy-start | bytes 100
  326.1 34.5 %copy-start.76 = (s32[8]{0:T(128)S(1)}, s32[8]{0:T(128)}, u32[]{:S(2)}) copy-start(s32[8]{0:T(128)} %get-tuple-element.36) | copy-start | bytes 100
  326.1 34.6 %copy-start.18 = (f32[2,16,64,256]{3,2,1,0:T(8,128)S(1)}, f32[2,16,64,256]{3,2,1,0:T(8,128)}, u32[]{:S(2)}) copy-start(f32[2,16,64,256]{3,2,1,0:T(8,128)} %copy-done.17) | copy-start | bytes 6291460
  326.1 34.6 %copy-start.70 = (f32[2,16,64]{2,1,0:T(8,128)S(1)}, f32[2,16,64]{2,1,0:T(8,128)}, u32[]{:S(2)}) copy-start(f32[2,16,64]{2,1,0:T(8,128)} %copy-done.69) | copy-start | bytes 24580
  356.1 46.7 %all-to-all-start.6 = ((bf16[8,128,896]{2,1,0:T(8,128)(2,1)}), bf16[8,128,896]{2,1,0:T(8,128)(2,1)}, u32[]{:S(2)}, u32[]{:S(2)}) async-start(bf16[8,128,896]{2,1,0:T(8,128)(2,1)} %broadcast_select_fusion.2), calls=%async_computation.6 | async-start | bytes 3670016 | tf_op jit(solution)/shard_map/all_to_all | solution.py:225
  375.4 31.8 %copy-start.1 = (bf16[64,8,16,128]{3,2,1,0:T(8,128)(2,1)S(1)}, bf16[64,8,16,128]{3,2,1,0:T(8,128)(2,1)}, u32[]{:S(2)}) copy-start(bf16[64,8,16,128]{3,2,1,0:T(8,128)(2,1)} %copy-done) | copy-start | bytes 6291460
  375.4 31.8 %copy-start.9 = (bf16[2,16,64,256]{3,2,1,0:T(8,128)(2,1)S(1)}, bf16[2,16,64,256]{3,2,1,0:T(8,128)(2,1)}, u32[]{:S(2)}) copy-start(bf16[2,16,64,256]{3,2,1,0:T(8,128)(2,1)} %copy-done.8) | copy-start | bytes 3145732
  402.8 75.4 %all-to-all-start.7 = ((bf16[8,128,896]{2,1,0:T(8,128)(2,1)}), bf16[8,128,896]{2,1,0:T(8,128)(2,1)}, u32[]{:S(2)}, u32[]{:S(2)}) async-start(bf16[8,128,896]{2,1,0:T(8,128)(2,1)} %broadcast_select_fusion.1), calls=%async_computation.8 | async-start | bytes 3670016 | tf_op jit(solution)/shard_map/all_to_all | solution.py:225
  407.2 107.0 %reduce-scatter.5.cloned.1.call-start = ((), (), s32[]{:S(2)}) async-start(), calls=%async_computation.12 | async-start | bytes 2621440 | tf_op jit(solution)/shard_map/reduce_scatter | solution.py:239
  428.0 54.6 %copy-start.5 = (bf16[64,8,16,128]{3,2,1,0:T(8,128)(2,1)S(1)}, bf16[64,8,16,128]{3,2,1,0:T(8,128)(2,1)}, u32[]{:S(2)}) copy-start(bf16[64,8,16,128]{3,2,1,0:T(8,128)(2,1)} %copy-done.4) | copy-start | bytes 6291460
  428.0 54.6 %copy-start.13 = (bf16[2,16,64,256]{3,2,1,0:T(8,128)(2,1)S(1)}, bf16[2,16,64,256]{3,2,1,0:T(8,128)(2,1)}, u32[]{:S(2)}) copy-start(bf16[2,16,64,256]{3,2,1,0:T(8,128)(2,1)} %copy-done.12) | copy-start | bytes 3145732
  478.2 44.4 %all-to-all-start.8 = ((bf16[8,128,896]{2,1,0:T(8,128)(2,1)}), bf16[8,128,896]{2,1,0:T(8,128)(2,1)}, u32[]{:S(2)}, u32[]{:S(2)}) async-start(bf16[8,128,896]{2,1,0:T(8,128)(2,1)} %broadcast_select_fusion), calls=%async_computation.9 | async-start | bytes 3670016 | tf_op jit(solution)/shard_map/all_to_all | solution.py:225
  496.3 11.9 %collective-permute-start.1 = (bf16[2,63,2048]{2,1,0:T(8,128)(2,1)}, bf16[2,63,2048]{2,1,0:T(8,128)(2,1)}, u32[]{:S(2)}, u32[]{:S(2)}) collective-permute-start(bf16[2,63,2048]{2,1,0:T(8,128)(2,1)} %slice.164), channel_id=1, source_target_pairs={{0,1},{1,2},{2,3},{3,4},{4,5},{5,6},{6,7},{8,9},{9,10},{10,11},{11... | collective-permute-start | bytes 1548296 | tf_op jit(solution)/shard_map/ppermute | solution.py:19
  505.4 7.0 %collective-permute-start.3 = (bf16[2,63,2048]{2,1,0:T(8,128)(2,1)S(1)}, bf16[2,63,2048]{2,1,0:T(8,128)(2,1)S(1)}, u32[]{:S(2)}, u32[]{:S(2)}) collective-permute-start(bf16[2,63,2048]{2,1,0:T(8,128)(2,1)S(1)} %slice.170), channel_id=1, source_target_pairs={{0,1},{1,2},{2,3},{3,4},{4,5},{5,6},{6,7},{8,9},{9,10},{10,11},{11... | collective-permute-start | bytes 1548296 | tf_op jit(solution)/shard_map/ppermute | solution.py:19
  (72 other events, 269.0 us)
Sparse Core Ops, SparseCore 0:
  293.3 105.2 reduce-scatter.2
  416.8 64.2 reduce-scatter.4
